TPU v7x, 128 devices: a whole 4x4x4 slice. The times are simulated.
128 devices in a mesh: user: 16 (over z, x), cand: 8 (over y, core).
Axes of the slice: x: 4, y: 4, z: 4, core: 2. Of those that a mesh axis runs over, the one named last changes fastest.
Arguments:
- cand_emb: bfloat16 [65536, 512], P(('user', 'cand')), may hold values from -40 to 40
- cand_route: int32 [65536], P(('user', 'cand')), may hold values from 0 to 127, as said below
- hist_kv: bfloat16 [2, 16, 1024, 1024], P(None, 'user'), may hold values from -6 to 6
- hist_len: int32 [16], P('user'), may hold values from 256 to 1024, as said below
- w_in: bfloat16 [2, 512, 1024], replicated, may hold values from -0.25 to 0.25
- w_out: bfloat16 [2, 512, 512], replicated, may hold values from -0.25 to 0.25
Outputs:
- scored: float32 [65536, 512], P(('user', 'cand'))
Inputs may be any that keep to these rules, and one draw needn't show every extreme that they name: `cand_route`: among the rows of one device no value is named by more than 8 rows, and one and the same value is named by exactly 8 rows on every device. `hist_len`: some user has a full history.
All inputs are finite; a program needn't handle non-finite values.
Results may differ from a plain program's by a relative error of at most 0.003.
Values may be sent and summed in bfloat16 or wider, within the bound.
No kernel may reach another device: no remote copies, remote signals or barrier semaphores. Data moves between devices by JAX's collectives and lax.ppermute only.
A program may use at most 64 MiB of HBM per device.

v0:
```python
import jax
import jax.numpy as jnp
from jax import lax
from jax.sharding import PartitionSpec as P

HEADS = 4


epsilon = 1e-05


def layer_normed(values):
    center = values - jnp.mean(values, axis=-1, keepdims=True)
    spread = jnp.mean(center * center, axis=-1, keepdims=True)
    return center * lax.rsqrt(spread + epsilon)


def attend(queries, hist_keys, hist_values, in_history, factor):
    row_count, features = queries.shape
    history_span = hist_keys.shape[0]
    head_dim = features // HEADS
    key_heads = hist_keys.reshape(history_span, HEADS, head_dim)
    value_heads = hist_values.reshape(history_span, HEADS, head_dim)

    def one_block(row_block):
        block_rows = row_block.shape[0]
        scores = jnp.einsum(
            "bhd,jhd->hbj",
            row_block.reshape(block_rows, HEADS, head_dim),
            key_heads,
            preferred_element_type=jnp.float32,
        )
        weight = jnp.where(in_history[None, None, :], jax.nn.silu(scores * factor), 0.0).astype(
            jnp.bfloat16
        )
        attended = jnp.einsum(
            "hbj,jhd->bhd", weight, value_heads, preferred_element_type=jnp.float32
        )
        return attended.reshape(block_rows, features)

    blocks = queries.reshape(row_count // 512, 512, features)
    return lax.map(one_block, blocks).reshape(row_count, features)


def run_layers(cand_rows, hist_kv, hist_len, w_in, w_out):
    features = cand_rows.shape[1]
    history_span = hist_kv.shape[2]
    factor = (features // HEADS) ** (-0.5)
    in_history = jnp.arange(history_span, dtype=jnp.int32) < hist_len[0]
    residual = cand_rows.astype(jnp.float32)
    for layer_index in range(w_in.shape[0]):
        normed = layer_normed(residual).astype(jnp.bfloat16)
        projected = jax.nn.silu(
            jnp.dot(normed, w_in[layer_index], preferred_element_type=jnp.float32)
        ).astype(jnp.bfloat16)
        attended = attend(
            projected[:, features:],
            hist_kv[layer_index, 0, :, :features],
            hist_kv[layer_index, 0, :, features:],
            in_history,
            factor,
        )
        branch = (layer_normed(attended) * projected[:, :features].astype(jnp.float32)).astype(
            jnp.bfloat16
        )
        residual = residual + jnp.dot(
            branch, w_out[layer_index], preferred_element_type=jnp.float32
        )
    return residual


def local(cand_emb, cand_route, hist_kv, hist_len, w_in, w_out):
    cand_rows, features = cand_emb.shape
    user_count = lax.axis_size("user")
    group_size = lax.axis_size("cand")
    scorers = user_count * group_size
    capacity = 2 * cand_rows // scorers
    onehot = (cand_route[:, None] == jnp.arange(scorers, dtype=jnp.int32)[None, :]).astype(
        jnp.int32
    )
    ranking = jnp.sum(jnp.cumsum(onehot, axis=0) * onehot, axis=1) - 1
    position = cand_route * capacity + ranking
    packed = jnp.zeros((scorers * capacity, features), cand_emb.dtype).at[position].set(cand_emb)
    outgoing = packed.reshape(scorers, capacity, features)
    items = lax.all_to_all(outgoing, ("user", "cand"), split_axis=0, concat_axis=0, tiled=True)
    flat_rows = items.reshape(-1, features)
    finished = run_layers(flat_rows, hist_kv, hist_len, w_in, w_out).reshape(items.shape)
    returned = lax.all_to_all(finished, ("user", "cand"), split_axis=0, concat_axis=0, tiled=True)
    return returned.reshape(-1, features)[position]


def solution(mesh):
    placed = (
        P(("user", "cand"), None),
        P(("user", "cand")),
        P(None, "user", None, None),
        P("user"),
        P(),
        P(),
    )
    return jax.shard_map(
        local, mesh=mesh, in_specs=placed, out_specs=P(("user", "cand"), None), check_vma=False
    )
```

profile of v0, /device:TPU:0, one launch (start us, length us, event | category | flops | bytes accessed | tf_op | source)
XLA Modules:
  0.0 133.6 jit_solution(14134571466975086065)
XLA Ops:
  2.7 4.0 %scatter_custom_fusion = bf16[1024,512]{1,0:T(8,128)(2,1)} fusion(s32[512]{0:T(512)S(1)} %compare_select_fusion, bf16[512,512]{1,0:T(8,128)(2,1)} %param.10, bf16[]{:T(256)} %constant.55.clone.1), kind=kCustom, calls=%fused_computation.58 | custom fusion | bytes 1049088 | tf_op jit(solution)/shard_map/scatter | solution.py:83
  6.7 11.3 %all-to-all-start = ((bf16[128,8,512]{2,1,0:T(8,128)(2,1)}), bf16[128,8,512]{2,1,0:T(8,128)(2,1)S(1)}, u32[]{:S(2)}, u32[]{:S(2)}) async-start(bf16[128,8,512]{2,1,0:T(8,128)(2,1)} %bitcast.4), calls=%async_computation | async-start | bytes 2097152 | tf_op jit(solution)/shard_map/all_to_all | solution.py:85
  18.0 3.9 %fusion.49 = (bf16[1,1,1024,512]{3,2,1,0:T(8,128)(2,1)S(1)}, bf16[1,1,1024,512]{3,2,1,0:T(8,128)(2,1)}, bf16[1,1,1024,512]{3,2,1,0:T(8,128)(2,1)}, bf16[1,1,1024,512]{3,2,1,0:T(8,128)(2,1)}) fusion(bf16[2,1,1024,1024]{3,2,1,0:T(8,128)(2,1)} %param.12), kind=kLoop, calls=%fused_computation.81 | loop fusion | bytes 8388608 | tf_op jit(solution)/shard_map/slice | solution.py:59
  21.9 1.5 %copy.29 = bf16[1,1,1024,512]{2,3,1,0:T(8,128)(2,1)S(1)} copy(bf16[1,1,1024,512]{3,2,1,0:T(8,128)(2,1)} %get-tuple-element.138) | data formatting | bytes 2097152
  24.7 2.3 %copy.16 = bf16[1,1,1024,512]{2,3,1,0:T(8,128)(2,1)} copy(bf16[1,1,1024,512]{3,2,1,0:T(8,128)(2,1)} %get-tuple-element.140) | data formatting | bytes 2097152 | tf_op jit(solution)/shard_map/slice | solution.py:59
  27.0 1.5 %copy.30 = bf16[1,1,1024,512]{2,3,1,0:T(8,128)(2,1)S(1)} copy(bf16[1,1,1024,512]{3,2,1,0:T(8,128)(2,1)} %get-tuple-element.139) | data formatting | bytes 2097152
  31.2 5.7 %all-to-all-done = bf16[128,8,512]{2,1,0:T(8,128)(2,1)S(1)} async-done(((bf16[128,8,512]{2,1,0:T(8,128)(2,1)}), bf16[128,8,512]{2,1,0:T(8,128)(2,1)S(1)}, u32[]{:S(2)}, u32[]{:S(2)}) %all-to-all-start) | async-done | bytes 1048608 | tf_op jit(solution)/shard_map/all_to_all | solution.py:85
  37.7 2.0 %multiply_convert_fusion.1 = bf16[1024,1024]{1,0:T(8,128)(2,1)S(1)} fusion(bf16[128,8,512]{2,1,0:T(8,128)(2,1)S(1)} %all-to-all-done, bf16[2,512,1024]{2,1,0:T(8,128)(2,1)S(1)} %copy-done.12, f32[128,8]{1,0:T(8,128)S(1)} %add_rsqrt_fusion, f32[128,8]{1,0:T(8,128)S(1)} %broadcast_multiply_fusion), kind=kOutput, calls=%fused_computation.23 | convolution fusion | flops 1081081856 | bytes 4325376 | tf_op jit(solution)/shard_map/dot_general | solution.py:54
  41.5 16.9 %while.22 = (s32[]{:T(128)}, f32[2,512,512]{1,2,0:T(8,128)S(1)}, bf16[2,512,512]{2,1,0:T(8,128)(2,1)}, bf16[1024,4,128]{2,0,1:T(8,128)(2,1)}, bf16[1024,4,128]{0,2,1:T(8,128)(2,1)}, /*index=5*/s32[]{:T(128)}, s32[]{:T(128)}) while((s32[]{:T(128)}, f32[2,512,512]{1,2,0:T(8,128)S(1)}, bf16[2,512,512]{2,1,0:T(8,128)(2,1)}, ...), condition=%wide.region_7.8_spmd.clone, body=%wide.region_6.7_spmd.clone.sunk | while | flops 1088422912 | bytes 7866457 | solution.py:42
  44.2 5.6 %fusion.70 = f32[4,512,128]{1,2,0:T(8,128)S(1)} fusion(bf16[1024,4,128]{0,2,1:T(8,128)(2,1)} %get-tuple-element.239, pred[1024]{0:T(1024)(128)(4,1)S(1)} %iota_compare_fusion.7, bf16[512,4,128]{0,2,1:T(8,128)(2,1)} %bitcast.115, bf16[1024,4,128]{2,0,1:T(8,128)(2,1)} %get-tuple-element.238), kind=kOutput, calls=%fused_computation.5.clone.1 | convolution fusion | flops 1088421888 | bytes 3671040 | tf_op jit(solution)/shard_map/while/body/eval_jaxpr/hbj,jhd->bhd/dot_general | solution.py:36
  52.7 5.6 %fusion.70 = f32[4,512,128]{1,2,0:T(8,128)S(1)} fusion(bf16[1024,4,128]{0,2,1:T(8,128)(2,1)} %get-tuple-element.239, pred[1024]{0:T(1024)(128)(4,1)S(1)} %iota_compare_fusion.7, bf16[512,4,128]{0,2,1:T(8,128)(2,1)} %bitcast.115, bf16[1024,4,128]{2,0,1:T(8,128)(2,1)} %get-tuple-element.238), kind=kOutput, calls=%fused_computation.5.clone.1 | convolution fusion | flops 1088421888 | bytes 3671040 | tf_op jit(solution)/shard_map/while/body/eval_jaxpr/hbj,jhd->bhd/dot_general | solution.py:36
  58.4 1.8 %copy.19 = f32[2,512,512]{2,1,0:T(8,128)} copy(f32[2,512,512]{1,2,0:T(8,128)S(1)} %get-tuple-element.69) | data formatting | bytes 4194304 | tf_op jit(solution)/shard_map/while | solution.py:42
  62.0 2.0 %fusion.26 = bf16[1024,512]{1,0:T(8,128)(2,1)S(1)} fusion(f32[2,512,512]{2,1,0:T(8,128)S(1)} %copy-done.5, bf16[1024,1024]{1,0:T(8,128)(2,1)} %copy-done.7, f32[1024]{0:T(1024)S(1)} %bitcast.127, f32[1024]{0:T(1024)S(1)} %bitcast.129), kind=kLoop, calls=%fused_computation.39 | loop fusion | flops 2621440 | bytes 4202496 | tf_op jit(solution)/shard_map/convert_element_type | solution.py:63
  65.3 1.9 %copy-done.13 = bf16[2,512,1024]{2,1,0:T(8,128)(2,1)S(1)} copy-done((bf16[2,512,1024]{2,1,0:T(8,128)(2,1)S(1)}, bf16[2,512,1024]{2,1,0:T(8,128)(2,1)}, u32[]{:S(2)}) %copy-start.13) | copy-done | bytes 2097176
  67.2 2.3 %multiply_convert_fusion = bf16[1024,1024]{1,0:T(8,128)(2,1)S(1)} fusion(f32[1024,512]{1,0:T(8,128)S(1)} %get-tuple-element.146, bf16[2,512,1024]{2,1,0:T(8,128)(2,1)S(1)} %copy-done.13, f32[1024]{0:T(1024)S(1)} %add_rsqrt_fusion.1, f32[1024]{0:T(1024)S(1)} %broadcast_multiply_fusion.1), kind=kOutput, calls=%fused_computation.22 | convolution fusion | flops 1080557568 | bytes 5251072 | tf_op jit(solution)/shard_map/dot_general | solution.py:54
  71.1 17.0 %while.23 = (s32[]{:T(128)}, f32[2,512,512]{1,2,0:T(8,128)S(1)}, bf16[2,512,512]{2,1,0:T(8,128)(2,1)}, bf16[1024,4,128]{2,0,1:T(8,128)(2,1)}, bf16[1024,4,128]{0,2,1:T(8,128)(2,1)}, /*index=5*/s32[]{:T(128)}, s32[]{:T(128)}) while((s32[]{:T(128)}, f32[2,512,512]{1,2,0:T(8,128)S(1)}, bf16[2,512,512]{2,1,0:T(8,128)(2,1)}, ...), condition=%wide.region_13.14_spmd.clone, body=%wide.region_12.13_spmd.clone.sunk | while | flops 1088422912 | bytes 7866457 | solution.py:42
  73.9 5.6 %fusion.74 = f32[4,512,128]{1,2,0:T(8,128)S(1)} fusion(bf16[1024,4,128]{0,2,1:T(8,128)(2,1)} %get-tuple-element.260, pred[1024]{0:T(1024)(128)(4,1)S(1)} %iota_compare_fusion.8, bf16[512,4,128]{0,2,1:T(8,128)(2,1)} %bitcast.116, bf16[1024,4,128]{2,0,1:T(8,128)(2,1)} %get-tuple-element.259), kind=kOutput, calls=%fused_computation.14.clone.1 | convolution fusion | flops 1088421888 | bytes 3671040 | tf_op jit(solution)/shard_map/while/body/eval_jaxpr/hbj,jhd->bhd/dot_general | solution.py:36
  82.4 5.6 %fusion.74 = f32[4,512,128]{1,2,0:T(8,128)S(1)} fusion(bf16[1024,4,128]{0,2,1:T(8,128)(2,1)} %get-tuple-element.260, pred[1024]{0:T(1024)(128)(4,1)S(1)} %iota_compare_fusion.8, bf16[512,4,128]{0,2,1:T(8,128)(2,1)} %bitcast.116, bf16[1024,4,128]{2,0,1:T(8,128)(2,1)} %get-tuple-element.259), kind=kOutput, calls=%fused_computation.14.clone.1 | convolution fusion | flops 1088421888 | bytes 3671040 | tf_op jit(solution)/shard_map/while/body/eval_jaxpr/hbj,jhd->bhd/dot_general | solution.py:36
  88.1 1.9 %copy.24 = f32[2,512,512]{2,1,0:T(8,128)} copy(f32[2,512,512]{1,2,0:T(8,128)S(1)} %get-tuple-element.70) | data formatting | bytes 4194304 | tf_op jit(solution)/shard_map/while | solution.py:42
  91.7 2.1 %fusion.23 = bf16[1024,512]{1,0:T(8,128)(2,1)S(1)} fusion(f32[2,512,512]{2,1,0:T(8,128)S(1)} %copy-done.4, bf16[1024,1024]{1,0:T(8,128)(2,1)} %copy-done.6, f32[1024]{0:T(1024)S(1)} %bitcast.128, f32[1024]{0:T(1024)S(1)} %bitcast.130), kind=kLoop, calls=%fused_computation.35 | loop fusion | flops 2621440 | bytes 4202496 | tf_op jit(solution)/shard_map/convert_element_type | solution.py:63
  93.9 2.1 %add_bitcast_fusion = f32[128,8,512]{2,1,0:T(8,128)} fusion(f32[1024,512]{1,0:T(8,128)S(1)} %copy-done.1, bf16[1024,512]{1,0:T(8,128)(2,1)S(1)} %fusion.23, bf16[2,512,512]{2,1,0:T(8,128)(2,1)S(1)} %copy-done.9), kind=kOutput, calls=%fused_computation.40 | convolution fusion | flops 537395200 | bytes 5767168 | tf_op jit(solution)/shard_map/dot_general | solution.py:66
  95.9 5.0 %all-to-all-start.1 = ((f32[128,8,512]{2,1,0:T(8,128)}), f32[128,8,512]{2,1,0:T(8,128)S(1)}, u32[]{:S(2)}, u32[]{:S(2)}) async-start(f32[128,8,512]{2,1,0:T(8,128)} %add_bitcast_fusion), calls=%async_computation.1 | async-start | bytes 4194304 | tf_op jit(solution)/shard_map/all_to_all | solution.py:88
  101.0 30.3 %all-to-all-done.1 = f32[128,8,512]{2,1,0:T(8,128)S(1)} async-done(((f32[128,8,512]{2,1,0:T(8,128)}), f32[128,8,512]{2,1,0:T(8,128)S(1)}, u32[]{:S(2)}, u32[]{:S(2)}) %all-to-all-start.1) | async-done | bytes 2097184 | tf_op jit(solution)/shard_map/all_to_all | solution.py:88
  131.3 2.3 %gather_fusion = f32[512,512]{1,0:T(8,128)} fusion(f32[1024,512]{1,0:T(8,128)S(1)} %bitcast.112, s32[1024]{0:T(1024)S(1)} %pad_clamp_fusion), kind=kCustom, calls=%fused_computation | custom fusion | bytes 2099200 | tf_op jit(solution)/shard_map/gather | solution.py:89
  (81 shorter events, 26.7 us)
Async XLA Ops:
  2.7 4.0 %copy-start.10 = (s32[512]{0:T(512)}, s32[512]{0:T(512)S(1)}, u32[]{:S(2)}) copy-start(s32[512]{0:T(512)S(1)} %compare_select_fusion) | copy-start | bytes 6148
  6.7 30.2 %all-to-all-start = ((bf16[128,8,512]{2,1,0:T(8,128)(2,1)}), bf16[128,8,512]{2,1,0:T(8,128)(2,1)S(1)}, u32[]{:S(2)}, u32[]{:S(2)}) async-start(bf16[128,8,512]{2,1,0:T(8,128)(2,1)} %bitcast.4), calls=%async_computation | async-start | bytes 2097152 | tf_op jit(solution)/shard_map/all_to_all | solution.py:85
  31.2 6.5 %copy-start.12 = (bf16[2,512,1024]{2,1,0:T(8,128)(2,1)S(1)}, bf16[2,512,1024]{2,1,0:T(8,128)(2,1)}, u32[]{:S(2)}) copy-start(bf16[2,512,1024]{2,1,0:T(8,128)(2,1)} %param.14) | copy-start | bytes 6291460
  36.9 2.9 %copy-start.2 = (bf16[128,8,512]{2,1,0:T(8,128)(2,1)}, bf16[128,8,512]{2,1,0:T(8,128)(2,1)S(1)}, u32[]{:S(2)}) copy-start(bf16[128,8,512]{2,1,0:T(8,128)(2,1)S(1)} %all-to-all-done) | copy-start | bytes 3145732
  39.8 1.7 %copy-start.7 = (bf16[1024,1024]{1,0:T(8,128)(2,1)}, bf16[1024,1024]{1,0:T(8,128)(2,1)S(1)}, u32[]{:S(2)}) copy-start(bf16[1024,1024]{1,0:T(8,128)(2,1)S(1)} %multiply_convert_fusion.1) | copy-start | bytes 6291460
  60.4 1.6 %copy-start.5 = (f32[2,512,512]{2,1,0:T(8,128)S(1)}, f32[2,512,512]{2,1,0:T(8,128)}, u32[]{:S(2)}) copy-start(f32[2,512,512]{2,1,0:T(8,128)} %copy.19) | copy-start | bytes 6291460
  62.0 2.0 %copy-start.3 = (bf16[128,8,512]{2,1,0:T(8,128)(2,1)S(1)}, bf16[128,8,512]{2,1,0:T(8,128)(2,1)}, u32[]{:S(2)}) copy-start(bf16[128,8,512]{2,1,0:T(8,128)(2,1)} %copy-done.2) | copy-start | bytes 3145732
  62.0 2.0 %copy-start.8 = (bf16[2,512,512]{2,1,0:T(8,128)(2,1)S(1)}, bf16[2,512,512]{2,1,0:T(8,128)(2,1)}, u32[]{:S(2)}) copy-start(bf16[2,512,512]{2,1,0:T(8,128)(2,1)} %param.15) | copy-start | bytes 3145732
  64.8 4.6 %copy-start = (f32[1024,512]{1,0:T(8,128)}, f32[1024,512]{1,0:T(8,128)S(1)}, u32[]{:S(2)}) copy-start(f32[1024,512]{1,0:T(8,128)S(1)} %get-tuple-element.146) | copy-start | bytes 6291460
  64.8 2.4 %copy-start.13 = (bf16[2,512,1024]{2,1,0:T(8,128)(2,1)S(1)}, bf16[2,512,1024]{2,1,0:T(8,128)(2,1)}, u32[]{:S(2)}) copy-start(bf16[2,512,1024]{2,1,0:T(8,128)(2,1)} %param.14) | copy-start | bytes 6291460
  69.4 1.6 %copy-start.6 = (bf16[1024,1024]{1,0:T(8,128)(2,1)}, bf16[1024,1024]{1,0:T(8,128)(2,1)S(1)}, u32[]{:S(2)}) copy-start(bf16[1024,1024]{1,0:T(8,128)(2,1)S(1)} %multiply_convert_fusion) | copy-start | bytes 6291460
  90.1 1.6 %copy-start.4 = (f32[2,512,512]{2,1,0:T(8,128)S(1)}, f32[2,512,512]{2,1,0:T(8,128)}, u32[]{:S(2)}) copy-start(f32[2,512,512]{2,1,0:T(8,128)} %copy.24) | copy-start | bytes 6291460
  91.7 2.1 %copy-start.1 = (f32[1024,512]{1,0:T(8,128)S(1)}, f32[1024,512]{1,0:T(8,128)}, u32[]{:S(2)}) copy-start(f32[1024,512]{1,0:T(8,128)} %copy-done) | copy-start | bytes 6291460
  91.7 2.2 %copy-start.9 = (bf16[2,512,512]{2,1,0:T(8,128)(2,1)S(1)}, bf16[2,512,512]{2,1,0:T(8,128)(2,1)}, u32[]{:S(2)}) copy-start(bf16[2,512,512]{2,1,0:T(8,128)(2,1)} %param.15) | copy-start | bytes 3145732
  95.9 5.0 %copy-start.11 = (s32[512]{0:T(512)S(1)}, s32[512]{0:T(512)}, u32[]{:S(2)}) copy-start(s32[512]{0:T(512)} %copy-done.10) | copy-start | bytes 6148
  95.9 35.4 %all-to-all-start.1 = ((f32[128,8,512]{2,1,0:T(8,128)}), f32[128,8,512]{2,1,0:T(8,128)S(1)}, u32[]{:S(2)}, u32[]{:S(2)}) async-start(f32[128,8,512]{2,1,0:T(8,128)} %add_bitcast_fusion), calls=%async_computation.1 | async-start | bytes 4194304 | tf_op jit(solution)/shard_map/all_to_all | solution.py:88
where the time goes:
time: 135 us; the launch traced here: 134 us
  local copies, waits for them, and re-layouts  40.5 us (30%)
  waiting for transfers between devices  36.1 us (27%)
  matrix products  29.7 us (22%)
  starting transfers between devices  16.3 us (12%)
  other arithmetic  10.6 us (8%)
    all_to_all x1, waiting for transfers between devices, local(): lax.all_to_all(finished, ('user', 'cand'), split_axis=0, concat_axis=0, t...  30.3 us
    dot_general x4, matrix products, one_block(): jnp.einsum('hbj,jhd->bhd', weight, value_heads, preferred_element_type=jn...  22.5 us
    all_to_all x1, starting transfers between devices, local(): lax.all_to_all(outgoing, ('user', 'cand'), split_axis=0, concat_axis=0, t...  11.3 us
    unnamed x37, local copies, waits for them, and re-layouts  10.7 us
    dynamic_slice x8, local copies, waits for them, and re-layouts, attend(): return lax.map(one_block, blocks).reshape(row_count, features)  8.35 us
    slice x3, local copies, waits for them, and re-layouts, run_layers(): hist_kv[layer_index, 0, :, features:]  7.54 us
    all_to_all x1, waiting for transfers between devices, local(): lax.all_to_all(outgoing, ('user', 'cand'), split_axis=0, concat_axis=0, t...  5.72 us
    all_to_all x1, starting transfers between devices, local(): lax.all_to_all(finished, ('user', 'cand'), split_axis=0, concat_axis=0, t...  5 us
  transfers between devices with their start and end apart: 2, of which 2 were waited for; matrix products, arithmetic and copies ran while one was open for 10% of the time, Pallas kernels for 0%

commit v1 on v0

v1 whole, which is shorter than its diff:
```python
import functools

import jax
import jax.numpy as jnp
from jax import lax
from jax.experimental import pallas as pl
from jax.experimental.pallas import tpu as pltpu
from jax.sharding import PartitionSpec as P

HEADS = 4
ROW_BLOCK = 256

epsilon = 1e-05


def half_silu(t):
    return t + t * jnp.tanh(t)


def layer_normed(values):
    center = values - jnp.mean(values, axis=-1, keepdims=True)
    spread = jnp.mean(center * center, axis=-1, keepdims=True)
    return center * lax.rsqrt(spread + epsilon)


def layers_kernel(length_ref, rows_ref, hist_ref, w_in_ref, w_out_ref, out_ref):
    block_rows, features = rows_ref.shape
    layer_count = w_in_ref.shape[0]
    history_span = hist_ref.shape[1]
    head_dim = features // HEADS
    factor = head_dim ** (-0.5)
    length = length_ref[0]
    in_history = lax.broadcasted_iota(jnp.int32, (1, history_span), 1) < length

    start = rows_ref[...].astype(jnp.float32)
    residual = start
    for layer_index in range(layer_count):
        normed = layer_normed(residual).astype(jnp.bfloat16)
        mixed = jnp.dot(normed, w_in_ref[layer_index], preferred_element_type=jnp.float32)
        projected = half_silu(mixed * 0.5).astype(jnp.bfloat16)
        gate = projected[:, :features].astype(jnp.float32)
        heads = []
        for head in range(HEADS):
            low = head * head_dim
            query = projected[:, features + low:features + low + head_dim]
            keys = hist_ref[layer_index, :, low:low + head_dim]
            values = hist_ref[layer_index, :, features + low:features + low + head_dim]
            scores = lax.dot_general(
                query, keys, (((1,), (1,)), ((), ())), preferred_element_type=jnp.float32
            )
            weight = half_silu(scores * (0.5 * factor))
            weight = jnp.where(in_history, weight, 0.0).astype(jnp.bfloat16)
            heads.append(jnp.dot(weight, values, preferred_element_type=jnp.float32))
        attended = jnp.concatenate(heads, axis=1)
        branch = (layer_normed(attended) * gate).astype(jnp.bfloat16)
        residual = residual + jnp.dot(
            branch, w_out_ref[layer_index], preferred_element_type=jnp.float32
        )
    out_ref[...] = (residual - start).astype(out_ref.dtype)


def run_layers(rows, history, length, w_in, w_out):
    row_count, features = rows.shape
    layer_count, history_span, width = history.shape
    grid_spec = pltpu.PrefetchScalarGridSpec(
        num_scalar_prefetch=1,
        grid=(row_count // ROW_BLOCK,),
        in_specs=[
            pl.BlockSpec((ROW_BLOCK, features), lambda i, n: (i, 0)),
            pl.BlockSpec((layer_count, history_span, width), lambda i, n: (0, 0, 0)),
            pl.BlockSpec(w_in.shape, lambda i, n: (0, 0, 0)),
            pl.BlockSpec(w_out.shape, lambda i, n: (0, 0, 0)),
        ],
        out_specs=pl.BlockSpec((ROW_BLOCK, features), lambda i, n: (i, 0)),
    )
    flops = 2 * row_count * layer_count * (
        features * 2 * features + 2 * history_span * features + features * features
    )
    return pl.pallas_call(
        layers_kernel,
        grid_spec=grid_spec,
        out_shape=jax.ShapeDtypeStruct((row_count, features), jnp.bfloat16),
        compiler_params=pltpu.CompilerParams(
            dimension_semantics=("arbitrary",), vmem_limit_bytes=48 * 1024 * 1024
        ),
        cost_estimate=pl.CostEstimate(
            flops=flops,
            transcendentals=row_count * layer_count * (HEADS * history_span + 2 * features),
            bytes_accessed=2 * (history.size + w_in.size + w_out.size + 2 * rows.size),
        ),
    )(length, rows, history, w_in, w_out)


def local(cand_emb, cand_route, hist_kv, hist_len, w_in, w_out):
    cand_rows, features = cand_emb.shape
    user_count = lax.axis_size("user")
    group_size = lax.axis_size("cand")
    scorers = user_count * group_size
    capacity = 2 * cand_rows // scorers
    slots = scorers * capacity
    onehot = (cand_route[:, None] == jnp.arange(scorers, dtype=jnp.int32)[None, :]).astype(
        jnp.int32
    )
    ranking = jnp.sum(jnp.cumsum(onehot, axis=0) * onehot, axis=1) - 1
    position = cand_route * capacity + ranking
    placing = (
        lax.broadcasted_iota(jnp.int32, (slots, cand_rows), 0) == position[None, :]
    ).astype(jnp.bfloat16)
    packed = jnp.dot(placing, cand_emb, preferred_element_type=jnp.float32).astype(jnp.bfloat16)
    outgoing = packed.reshape(scorers, capacity, features)
    items = lax.all_to_all(outgoing, ("user", "cand"), split_axis=0, concat_axis=0, tiled=True)
    history = hist_kv.reshape(hist_kv.shape[0], hist_kv.shape[2], hist_kv.shape[3])
    delta = run_layers(items.reshape(-1, features), history, hist_len, w_in, w_out)
    returned = lax.all_to_all(
        delta.reshape(items.shape), ("user", "cand"), split_axis=0, concat_axis=0, tiled=True
    )
    gathered = lax.dot_general(
        placing,
        returned.reshape(-1, features),
        (((0,), (0,)), ((), ())),
        preferred_element_type=jnp.float32,
    )
    return cand_emb.astype(jnp.float32) + gathered


def solution(mesh):
    placed = (
        P(("user", "cand"), None),
        P(("user", "cand")),
        P(None, "user", None, None),
        P("user"),
        P(),
        P(),
    )
    return jax.shard_map(
        local, mesh=mesh, in_specs=placed, out_specs=P(("user", "cand"), None), check_vma=False
    )
```

time: 135 us -> 85.9 us (0.64)
  local copies, waits for them, and re-layouts: 40.5 us -> 2.05 us
  matrix products: 29.7 us -> 4.61 us
  Pallas kernels: 0 us -> 23.3 us
  blocking collectives: 0 us -> 23.2 us
  waiting for transfers between devices: 36.1 us -> 18.4 us
  other arithmetic: 10.6 us -> 1.86 us
  starting transfers between devices: 16.3 us -> 11.1 us
    all_to_all x1 -> x0, waiting for transfers between devices: 30.3 us -> none  [local(): lax.all_to_all(finished, ('user', 'cand'), split_axis=0, concat_axis=0, t...]
    dot_general x8 -> x2, matrix products: 29.7 us -> 4.61 us  [the longest x1 2.88 us: local(): jnp.dot(placing, cand_emb, preferred_element_type=jnp.float32)]
    pallas_call x0 -> x1, Pallas kernels: none -> 23.3 us  [run_layers(): pl.pallas_call(layers_kernel, grid_spec=grid_spec, out_shape=jax.ShapeDty...]
    all_to_all x0 -> x1, blocking collectives: none -> 23.2 us  [local(): lax.all_to_all(delta.reshape(items.shape), ('user', 'cand'), split_axis=0...]
    all_to_all x1, waiting for transfers between devices: 5.72 us -> 18.4 us  [local(): lax.all_to_all(outgoing, ('user', 'cand'), split_axis=0, concat_axis=0, t...]
    slice x5 -> x0, local copies, waits for them, and re-layouts: 9.89 us -> none  [the longest x3 7.54 us: run_layers(): hist_kv[layer_index, 0, :, features:]]
    unnamed x37 -> x7, local copies, waits for them, and re-layouts: 10.7 us -> 1.24 us
    dynamic_slice x8 -> x0, local copies, waits for them, and re-layouts: 8.35 us -> none  [attend(): return lax.map(one_block, blocks).reshape(row_count, features)]
  transfers between devices with their start and end apart: 2 -> 1, of which waited for: 2 -> 1; matrix products, arithmetic and copies ran while one was open for 10% -> 0% of each run, Pallas kernels for 0% -> 0%
where the time goes in v1:
time: 85.9 us; the launch traced here: 85.4 us
  Pallas kernels  23.3 us (27%)
  blocking collectives  23.2 us (27%)
  waiting for transfers between devices  18.4 us (21%)
  starting transfers between devices  11.1 us (13%)
  matrix products  4.61 us (5%)
  local copies, waits for them, and re-layouts  2.05 us (2%)
  other arithmetic  1.86 us (2%)
    pallas_call x1, Pallas kernels, run_layers(): pl.pallas_call(layers_kernel, grid_spec=grid_spec, out_shape=jax.ShapeDty...  23.3 us
    all_to_all x1, blocking collectives, local(): lax.all_to_all(delta.reshape(items.shape), ('user', 'cand'), split_axis=0...  23.2 us
    all_to_all x1, waiting for transfers between devices, local(): lax.all_to_all(outgoing, ('user', 'cand'), split_axis=0, concat_axis=0, t...  18.4 us
    all_to_all x1, starting transfers between devices, local(): lax.all_to_all(outgoing, ('user', 'cand'), split_axis=0, concat_axis=0, t...  11.1 us
    dot_general x1, matrix products, local(): jnp.dot(placing, cand_emb, preferred_element_type=jnp.float32)  2.88 us
    dot_general x1, matrix products, local(): lax.dot_general(placing, returned.reshape(-1, features), (((0,), (0,)), (...  1.73 us
  transfers between devices with their start and end apart: 1, of which 1 were waited for; matrix products, arithmetic and copies ran while one was open for 0% of the time, Pallas kernels for 0%

profile of v1, /device:TPU:0, one launch (start us, length us, event | category | flops | bytes accessed | tf_op | source)
XLA Modules:
  0.0 85.4 jit_solution(15700834045176856361)
XLA Ops:
  0.0 0.8 copy.7
  0.8 0.2 fusion.9
  1.1 0.9 %fusion.8 = s32[512]{0:T(512)S(1)} fusion(s32[128,4,128]{0,2,1:T(8,128)S(1)} %copy.8, s32[512]{0:T(512)} %param.7), kind=kLoop, calls=%fused_computation.10 | loop fusion | flops 196096 | bytes 266240 | tf_op jit(solution)/shard_map/reduce_sum | solution.py:104
  2.0 0.7 add_add_fusion
  2.7 0.0 copy-start
  2.7 2.9 %fusion.3 = bf16[128,8,512]{2,1,0:T(8,128)(2,1)} fusion(bf16[512,512]{1,0:T(8,128)(2,1)} %param.6, s32[512]{0:T(512)S(1)} %add_add_fusion), kind=kOutput, calls=%fused_computation.4 | convolution fusion | flops 537919488 | bytes 1574912 | tf_op jit(solution)/shard_map/dot_general | solution.py:109
  5.6 11.1 %all-to-all-start = ((bf16[128,8,512]{2,1,0:T(8,128)(2,1)}), bf16[128,8,512]{2,1,0:T(8,128)(2,1)S(1)}, u32[]{:S(2)}, u32[]{:S(2)}) async-start(bf16[128,8,512]{2,1,0:T(8,128)(2,1)} %fusion.3), calls=%async_computation | async-start | bytes 2097152 | tf_op jit(solution)/shard_map/all_to_all | solution.py:111
  17.4 18.4 %all-to-all-done = bf16[128,8,512]{2,1,0:T(8,128)(2,1)S(1)} async-done(((bf16[128,8,512]{2,1,0:T(8,128)(2,1)}), bf16[128,8,512]{2,1,0:T(8,128)(2,1)S(1)}, u32[]{:S(2)}, u32[]{:S(2)}) %all-to-all-start) | async-done | bytes 1048608 | tf_op jit(solution)/shard_map/all_to_all | solution.py:111
  35.8 0.0 copy-done
  35.8 0.0 copy-start.1
  35.8 1.2 %copy-done.1 = bf16[2,512,512]{2,1,0:T(8,128)(2,1)S(1)} copy-done((bf16[2,512,512]{2,1,0:T(8,128)(2,1)S(1)}, bf16[2,512,512]{2,1,0:T(8,128)(2,1)}, u32[]{:S(2)}) %copy-start.1) | copy-done | bytes 1048600
  37.1 23.3 %shard_map.64 = bf16[1024,512]{1,0:T(8,128)(2,1)S(1)} custom-call(s32[1]{0:T(128)S(6)} %copy.9.length_ref, bf16[1024,512]{1,0:T(8,128)(2,1)S(1)} %bitcast.21, bf16[2,1024,1024]{2,1,0:T(8,128)(2,1)} %bitcast.27, bf16[2,512,1024]{2,1,0:T(8,128)(2,1)S(1)} %copy-done, bf16[2,512,512]{2,1,0:T(8,128)(2,1)S(1)} %copy-done.1), custom_call_target="tpu_custom_call" | custom-call | flops 7516192768 | bytes 9437184 | tf_op jit(solution)/shard_map/pallas_call | solution.py:79
  60.4 0.0 copy-start.2
  60.4 23.2 %all_to_all.10 = bf16[128,8,512]{2,1,0:T(8,128)(2,1)S(1)} all-to-all(bf16[128,8,512]{2,1,0:T(8,128)(2,1)S(1)} %bitcast.22), channel_id=1, replica_groups=mesh['user'=16,'cand'=8] {'user','cand'}, dimensions={0} | all-to-all | bytes 2097152 | tf_op jit(solution)/shard_map/all_to_all | solution.py:114
  83.6 0.0 copy-done.2
  83.6 1.7 %fusion.4 = f32[512,512]{1,0:T(8,128)} fusion(bf16[128,8,512]{2,1,0:T(8,128)(2,1)S(1)} %all_to_all.10, s32[512]{0:T(512)S(1)} %add_add_fusion, bf16[512,512]{1,0:T(8,128)(2,1)S(1)} %copy-done.2), kind=kOutput, calls=%fused_computation.5 | convolution fusion | flops 537919488 | bytes 2623488 | tf_op jit(solution)/shard_map/dot_general | solution.py:117
  (6 shorter events, 0.1 us)
Async XLA Ops:
  2.7 33.1 %copy-start = (bf16[2,512,1024]{2,1,0:T(8,128)(2,1)S(1)}, bf16[2,512,1024]{2,1,0:T(8,128)(2,1)}, u32[]{:S(2)}) copy-start(bf16[2,512,1024]{2,1,0:T(8,128)(2,1)} %w_in_ref.1) | copy-start | bytes 6291460
  5.6 30.2 %all-to-all-start = ((bf16[128,8,512]{2,1,0:T(8,128)(2,1)}), bf16[128,8,512]{2,1,0:T(8,128)(2,1)S(1)}, u32[]{:S(2)}, u32[]{:S(2)}) async-start(bf16[128,8,512]{2,1,0:T(8,128)(2,1)} %fusion.3), calls=%async_computation | async-start | bytes 2097152 | tf_op jit(solution)/shard_map/all_to_all | solution.py:111
  35.8 1.2 %copy-start.1 = (bf16[2,512,512]{2,1,0:T(8,128)(2,1)S(1)}, bf16[2,512,512]{2,1,0:T(8,128)(2,1)}, u32[]{:S(2)}) copy-start(bf16[2,512,512]{2,1,0:T(8,128)(2,1)} %w_out_ref.1) | copy-start | bytes 3145732
  60.4 23.2 %copy-start.2 = (bf16[512,512]{1,0:T(8,128)(2,1)S(1)}, bf16[512,512]{1,0:T(8,128)(2,1)}, u32[]{:S(2)}) copy-start(bf16[512,512]{1,0:T(8,128)(2,1)} %param.6) | copy-start | bytes 1572868

commit v2 on v1

v2 whole, which is shorter than its diff:
```python
import jax
import jax.numpy as jnp
from jax import lax
from jax.experimental import pallas as pl
from jax.experimental.pallas import tpu as pltpu
from jax.sharding import PartitionSpec as P

HEADS = 4
SLOT_BLOCK = 16

epsilon = 1e-05


def half_silu(t):
    return t + t * jnp.tanh(t)


def layer_normed(values):
    center = values - jnp.mean(values, axis=-1, keepdims=True)
    spread = jnp.mean(center * center, axis=-1, keepdims=True)
    return center * lax.rsqrt(spread + epsilon)


def layers_kernel(length_ref, busy_ref, rows_ref, hist_ref, w_in_ref, w_out_ref, out_ref):
    sources, slots, features = rows_ref.shape
    block_rows = sources * slots
    layer_count = w_in_ref.shape[0]
    history_span = hist_ref.shape[1]
    head_dim = features // HEADS
    factor = head_dim ** (-0.5)
    step = pl.program_id(0)

    @pl.when(busy_ref[step] == 0)
    def _():
        out_ref[...] = jnp.zeros(out_ref.shape, out_ref.dtype)

    @pl.when(busy_ref[step] != 0)
    def _():
        length = length_ref[0]
        in_history = lax.broadcasted_iota(jnp.int32, (history_span, 1), 0) < length
        start = rows_ref[...].astype(jnp.float32).reshape(block_rows, features)
        residual = start
        for layer_index in range(layer_count):
            normed = layer_normed(residual).astype(jnp.bfloat16)
            mixed = jnp.dot(normed, w_in_ref[layer_index], preferred_element_type=jnp.float32)
            projected = half_silu(mixed * 0.5).astype(jnp.bfloat16)
            gate = projected[:, :features].astype(jnp.float32)
            values_all = jnp.where(
                in_history, hist_ref[layer_index, :, features:], jnp.zeros((), jnp.bfloat16)
            )
            heads = []
            for head in range(HEADS):
                low = head * head_dim
                query = projected[:, features + low:features + low + head_dim]
                keys = hist_ref[layer_index, :, low:low + head_dim]
                scores = lax.dot_general(
                    query, keys, (((1,), (1,)), ((), ())), preferred_element_type=jnp.float32
                )
                weight = half_silu(scores * (0.5 * factor)).astype(jnp.bfloat16)
                heads.append(
                    jnp.dot(
                        weight,
                        values_all[:, low:low + head_dim],
                        preferred_element_type=jnp.float32,
                    )
                )
            attended = jnp.concatenate(heads, axis=1)
            branch = (layer_normed(attended) * gate).astype(jnp.bfloat16)
            residual = residual + jnp.dot(
                branch, w_out_ref[layer_index], preferred_element_type=jnp.float32
            )
        out_ref[...] = (residual - start).reshape(sources, slots, features).astype(out_ref.dtype)


def run_layers(buckets, history, length, w_in, w_out):
    sources, capacity, features = buckets.shape
    layer_count, history_span, width = history.shape
    steps = capacity // SLOT_BLOCK
    busy = jnp.any(
        buckets.reshape(sources, steps, SLOT_BLOCK * features) != 0, axis=(0, 2)
    ).astype(jnp.int32)
    grid_spec = pltpu.PrefetchScalarGridSpec(
        num_scalar_prefetch=2,
        grid=(steps,),
        in_specs=[
            pl.BlockSpec((sources, SLOT_BLOCK, features), lambda i, n, b: (0, i, 0)),
            pl.BlockSpec((layer_count, history_span, width), lambda i, n, b: (0, 0, 0)),
            pl.BlockSpec(w_in.shape, lambda i, n, b: (0, 0, 0)),
            pl.BlockSpec(w_out.shape, lambda i, n, b: (0, 0, 0)),
        ],
        out_specs=pl.BlockSpec((sources, SLOT_BLOCK, features), lambda i, n, b: (0, i, 0)),
    )
    row_count = sources * capacity
    flops = 2 * row_count * layer_count * (
        features * 2 * features + 2 * history_span * features + features * features
    )
    return pl.pallas_call(
        layers_kernel,
        grid_spec=grid_spec,
        out_shape=jax.ShapeDtypeStruct(buckets.shape, jnp.bfloat16),
        compiler_params=pltpu.CompilerParams(
            dimension_semantics=("arbitrary",), vmem_limit_bytes=48 * 1024 * 1024
        ),
        cost_estimate=pl.CostEstimate(
            flops=flops,
            transcendentals=row_count * layer_count * (HEADS * history_span + 2 * features),
            bytes_accessed=2 * (history.size + w_in.size + w_out.size + 2 * buckets.size),
        ),
    )(length, busy, buckets, history, w_in, w_out)


def local(cand_emb, cand_route, hist_kv, hist_len, w_in, w_out):
    cand_rows, features = cand_emb.shape
    user_count = lax.axis_size("user")
    group_size = lax.axis_size("cand")
    capacity = 2 * cand_rows // user_count
    slots = user_count * capacity
    owner = cand_route // group_size
    onehot = (owner[:, None] == jnp.arange(user_count, dtype=jnp.int32)[None, :]).astype(
        jnp.int32
    )
    ranking = jnp.sum(jnp.cumsum(onehot, axis=0) * onehot, axis=1) - 1
    position = owner * capacity + ranking
    placing = (
        lax.broadcasted_iota(jnp.int32, (slots, cand_rows), 0) == position[None, :]
    ).astype(jnp.bfloat16)
    packed = jnp.dot(placing, cand_emb, preferred_element_type=jnp.float32).astype(jnp.bfloat16)
    outgoing = packed.reshape(user_count, capacity, features)
    items = lax.all_to_all(outgoing, "user", split_axis=0, concat_axis=0, tiled=True)
    history = hist_kv.reshape(hist_kv.shape[0], hist_kv.shape[2], hist_kv.shape[3])
    delta = run_layers(items, history, hist_len, w_in, w_out)
    returned = lax.all_to_all(delta, "user", split_axis=0, concat_axis=0, tiled=True)
    gathered = lax.dot_general(
        placing,
        returned.reshape(-1, features),
        (((0,), (0,)), ((), ())),
        preferred_element_type=jnp.float32,
    )
    return cand_emb.astype(jnp.float32) + gathered


def solution(mesh):
    placed = (
        P(("user", "cand"), None),
        P(("user", "cand")),
        P(None, "user", None, None),
        P("user"),
        P(),
        P(),
    )
    return jax.shard_map(
        local, mesh=mesh, in_specs=placed, out_specs=P(("user", "cand"), None), check_vma=False
    )
```

time: 85.9 us -> 75 us (0.87)
  Pallas kernels: 23.3 us -> 19.3 us
  blocking collectives: 23.2 us -> 19.6 us
  starting transfers between devices: 11.1 us -> 8.09 us
  other arithmetic: 1.86 us -> 3.86 us
  waiting for transfers between devices: 18.4 us -> 17 us
    pallas_call x1, Pallas kernels: 23.3 us -> 19.3 us  [run_layers(): pl.pallas_call(layers_kernel, grid_spec=grid_spec, out_shape=jax.ShapeDty...]
    all_to_all x1, blocking collectives: 23.2 us -> 19.6 us  [local(): lax.all_to_all(delta, 'user', split_axis=0, concat_axis=0, tiled=True)]
    all_to_all x1, starting transfers between devices: 11.1 us -> 8.09 us  [local(): lax.all_to_all(outgoing, 'user', split_axis=0, concat_axis=0, tiled=True)]
    all_to_all x1, waiting for transfers between devices: 18.4 us -> 17 us  [local(): lax.all_to_all(outgoing, 'user', split_axis=0, concat_axis=0, tiled=True)]
    another operation x3 -> x2, other arithmetic: 0.26 us -> 1.19 us
where the time goes in v2:
time: 75 us; the launch traced here: 74.5 us
  blocking collectives  19.6 us (26%)
  Pallas kernels  19.3 us (26%)
  waiting for transfers between devices  17 us (23%)
  starting transfers between devices  8.09 us (11%)
  matrix products  4.46 us (6%)
  other arithmetic  3.86 us (5%)
  local copies, waits for them, and re-layouts  1.54 us (2%)
    all_to_all x1, blocking collectives, local(): lax.all_to_all(delta, 'user', split_axis=0, concat_axis=0, tiled=True)  19.6 us
    pallas_call x1, Pallas kernels, run_layers(): pl.pallas_call(layers_kernel, grid_spec=grid_spec, out_shape=jax.ShapeDty...  19.3 us
    all_to_all x1, waiting for transfers between devices, local(): lax.all_to_all(outgoing, 'user', split_axis=0, concat_axis=0, tiled=True)  17 us
    all_to_all x1, starting transfers between devices, local(): lax.all_to_all(outgoing, 'user', split_axis=0, concat_axis=0, tiled=True)  8.09 us
    dot_general x1, matrix products, local(): jnp.dot(placing, cand_emb, preferred_element_type=jnp.float32)  2.73 us
    dot_general x1, matrix products, local(): lax.dot_general(placing, returned.reshape(-1, features), (((0,), (0,)), (...  1.73 us
  transfers between devices with their start and end apart: 1, of which 1 were waited for; matrix products, arithmetic and copies ran while one was open for 0% of the time, Pallas kernels for 0%

profile of v2, /device:TPU:0, one launch (start us, length us, event | category | flops | bytes accessed | tf_op | source)
XLA Modules:
  0.0 74.5 jit_solution(9027826562244716154)
XLA Ops:
  0.0 0.7 fusion.13
  0.7 0.7 add_select_fusion
  1.4 1.2 %reduce-window.6 = s32[16,4,128]{2,0,1:T(8,128)S(1)} reduce-window(s32[16,4,128]{2,0,1:T(8,128)S(1)} %fusion.8, s32[]{:T(128)} %constant.22.clone.1), window={size=1x1x128 pad=0_0x0_0x127_0}, to_apply=%region_0.1 | reduce-window | flops 1040384 | bytes 65540 | tf_op jit(solution)/shard_map/reduce-window
  2.5 0.2 slice_reduce_fusion
  2.8 0.1 fusion.7
  2.9 0.7 add_add_fusion
  3.6 2.7 %fusion.2 = bf16[1024,512]{1,0:T(8,128)(2,1)} fusion(bf16[512,512]{1,0:T(8,128)(2,1)} %param.6, s32[512]{0:T(512)S(1)} %add_add_fusion), kind=kOutput, calls=%fused_computation.4 | convolution fusion | flops 537919488 | bytes 1574912 | tf_op jit(solution)/shard_map/dot_general | solution.py:127
  6.3 0.0 copy-start
  6.3 8.1 %all-to-all-start = ((bf16[16,64,512]{2,1,0:T(8,128)(2,1)}), bf16[16,64,512]{2,1,0:T(8,128)(2,1)S(1)}, u32[]{:S(2)}, u32[]{:S(2)}) async-start(bf16[16,64,512]{2,1,0:T(8,128)(2,1)} %bitcast.22), calls=%async_computation | async-start | bytes 2097152 | tf_op jit(solution)/shard_map/all_to_all | solution.py:129
  15.1 17.0 %all-to-all-done.rows_ref = bf16[16,64,512]{2,1,0:T(8,128)(2,1)S(1)} async-done(((bf16[16,64,512]{2,1,0:T(8,128)(2,1)}), bf16[16,64,512]{2,1,0:T(8,128)(2,1)S(1)}, u32[]{:S(2)}, u32[]{:S(2)}) %all-to-all-start) | async-done | bytes 1048608 | tf_op jit(solution)/shard_map/all_to_all | solution.py:129
  32.1 0.4 compare_reduce_fusion
  32.4 0.1 reduce_or.14
  32.5 0.1 reduce_or.18
  32.7 0.0 copy-done
  32.7 0.0 copy-start.1
  32.7 1.2 %copy-done.1 = bf16[2,512,512]{2,1,0:T(8,128)(2,1)S(1)} copy-done((bf16[2,512,512]{2,1,0:T(8,128)(2,1)S(1)}, bf16[2,512,512]{2,1,0:T(8,128)(2,1)}, u32[]{:S(2)}) %copy-start.1) | copy-done | bytes 1048600
  33.9 19.3 %shard_map.64 = bf16[16,64,512]{2,1,0:T(8,128)(2,1)S(1)} custom-call(s32[1]{0:T(128)S(6)} %copy.10.length_ref, s32[4]{0:T(128)S(1)} %convert_element_type.18.busy_ref, bf16[16,64,512]{2,1,0:T(8,128)(2,1)S(1)} %all-to-all-done.rows_ref, bf16[2,1024,1024]{2,1,0:T(8,128)(2,1)} %bitcast.24, bf16[2,512,1024]{2,1,0:T(8,128)(2,1)S(1)} %copy-done, ...), custom_call_target="tpu_custom_call" | custom-call | flops 7516192768 | bytes 9437184 | tf_op jit(solution)/shard_map/pallas_call | solution.py:97
  53.2 0.0 copy-start.2
  53.2 19.6 %all_to_all.10 = bf16[16,64,512]{2,1,0:T(8,128)(2,1)S(1)} all-to-all(bf16[16,64,512]{2,1,0:T(8,128)(2,1)S(1)} %shard_map.64), channel_id=1, replica_groups=mesh['user'=16,'cand'=8] {'user'}, dimensions={0} | all-to-all | bytes 2097152 | tf_op jit(solution)/shard_map/all_to_all | solution.py:132
  72.8 0.0 copy-done.2
  72.8 1.7 %fusion.3 = f32[512,512]{1,0:T(8,128)} fusion(bf16[1024,512]{1,0:T(8,128)(2,1)S(1)} %bitcast.23, s32[512]{0:T(512)S(1)} %add_add_fusion, bf16[512,512]{1,0:T(8,128)(2,1)S(1)} %copy-done.2), kind=kOutput, calls=%fused_computation.5 | convolution fusion | flops 537919488 | bytes 2623488 | tf_op jit(solution)/shard_map/dot_general | solution.py:133
  (4 shorter events, 0.1 us)
Async XLA Ops:
  6.3 26.3 %copy-start = (bf16[2,512,1024]{2,1,0:T(8,128)(2,1)S(1)}, bf16[2,512,1024]{2,1,0:T(8,128)(2,1)}, u32[]{:S(2)}) copy-start(bf16[2,512,1024]{2,1,0:T(8,128)(2,1)} %w_in_ref.1) | copy-start | bytes 6291460
  6.3 25.7 %all-to-all-start = ((bf16[16,64,512]{2,1,0:T(8,128)(2,1)}), bf16[16,64,512]{2,1,0:T(8,128)(2,1)S(1)}, u32[]{:S(2)}, u32[]{:S(2)}) async-start(bf16[16,64,512]{2,1,0:T(8,128)(2,1)} %bitcast.22), calls=%async_computation | async-start | bytes 2097152 | tf_op jit(solution)/shard_map/all_to_all | solution.py:129
  32.7 1.2 %copy-start.1 = (bf16[2,512,512]{2,1,0:T(8,128)(2,1)S(1)}, bf16[2,512,512]{2,1,0:T(8,128)(2,1)}, u32[]{:S(2)}) copy-start(bf16[2,512,512]{2,1,0:T(8,128)(2,1)} %w_out_ref.1) | copy-start | bytes 3145732
  53.2 19.6 %copy-start.2 = (bf16[512,512]{1,0:T(8,128)(2,1)S(1)}, bf16[512,512]{1,0:T(8,128)(2,1)}, u32[]{:S(2)}) copy-start(bf16[512,512]{1,0:T(8,128)(2,1)} %param.6) | copy-start | bytes 1572868

commit v3 on v2

--- a/solution.py
+++ b/solution.py
@@ -1,3 +1,5 @@
+import functools
+
 import jax
 import jax.numpy as jnp
 from jax import lax
@@ -11,8 +13,8 @@
 epsilon = 1e-05
 
 
-def half_silu(t):
-    return t + t * jnp.tanh(t)
+def silu(v):
+    return v * jax.nn.sigmoid(v)
 
 
 def layer_normed(values):
@@ -43,7 +45,7 @@
         for layer_index in range(layer_count):
             normed = layer_normed(residual).astype(jnp.bfloat16)
             mixed = jnp.dot(normed, w_in_ref[layer_index], preferred_element_type=jnp.float32)
-            projected = half_silu(mixed * 0.5).astype(jnp.bfloat16)
+            projected = silu(mixed).astype(jnp.bfloat16)
             gate = projected[:, :features].astype(jnp.float32)
             values_all = jnp.where(
                 in_history, hist_ref[layer_index, :, features:], jnp.zeros((), jnp.bfloat16)
@@ -52,11 +54,12 @@
             for head in range(HEADS):
                 low = head * head_dim
                 query = projected[:, features + low:features + low + head_dim]
+                query = (query.astype(jnp.float32) * factor).astype(jnp.bfloat16)
                 keys = hist_ref[layer_index, :, low:low + head_dim]
                 scores = lax.dot_general(
                     query, keys, (((1,), (1,)), ((), ())), preferred_element_type=jnp.float32
                 )
-                weight = half_silu(scores * (0.5 * factor)).astype(jnp.bfloat16)
+                weight = silu(scores).astype(jnp.bfloat16)
                 heads.append(
                     jnp.dot(
                         weight,
@@ -109,22 +112,58 @@
     )(length, busy, buckets, history, w_in, w_out)
 
 
+def pack_kernel(route_ref, emb_ref, packed_ref, position_ref, *, group_size, user_count):
+    cand_rows = emb_ref.shape[0]
+    capacity = packed_ref.shape[0] // user_count
+    owner = route_ref[...] // group_size
+    member = (lax.broadcasted_iota(jnp.int32, (user_count, cand_rows), 0) == owner).astype(
+        jnp.float32
+    )
+    earlier = (
+        lax.broadcasted_iota(jnp.int32, (cand_rows, cand_rows), 0)
+        < lax.broadcasted_iota(jnp.int32, (cand_rows, cand_rows), 1)
+    ).astype(jnp.bfloat16)
+    before = jnp.dot(member.astype(jnp.bfloat16), earlier, preferred_element_type=jnp.float32)
+    ranking = jnp.sum(member * before, axis=0, keepdims=True).astype(jnp.int32)
+    position = owner * capacity + ranking
+    position_ref[...] = position
+    placing = (
+        lax.broadcasted_iota(jnp.int32, (packed_ref.shape[0], cand_rows), 0) == position
+    ).astype(jnp.bfloat16)
+    packed_ref[...] = jnp.dot(
+        placing, emb_ref[...], preferred_element_type=jnp.float32
+    ).astype(packed_ref.dtype)
+
+
+def pack_rows(cand_emb, cand_route, user_count, group_size):
+    cand_rows, features = cand_emb.shape
+    slots = 2 * cand_rows
+    return pl.pallas_call(
+        functools.partial(pack_kernel, group_size=group_size, user_count=user_count),
+        out_shape=(
+            jax.ShapeDtypeStruct((slots, features), jnp.bfloat16),
+            jax.ShapeDtypeStruct((1, cand_rows), jnp.int32),
+        ),
+        in_specs=[pl.BlockSpec(memory_space=pltpu.VMEM)] * 2,
+        out_specs=(pl.BlockSpec(memory_space=pltpu.VMEM),) * 2,
+        cost_estimate=pl.CostEstimate(
+            flops=2 * slots * cand_rows * features + 2 * user_count * cand_rows * cand_rows,
+            transcendentals=0,
+            bytes_accessed=2 * (cand_emb.size + slots * features),
+        ),
+    )(cand_route.reshape(1, cand_rows), cand_emb)
+
+
 def local(cand_emb, cand_route, hist_kv, hist_len, w_in, w_out):
     cand_rows, features = cand_emb.shape
     user_count = lax.axis_size("user")
     group_size = lax.axis_size("cand")
-    capacity = 2 * cand_rows // user_count
-    slots = user_count * capacity
-    owner = cand_route // group_size
-    onehot = (owner[:, None] == jnp.arange(user_count, dtype=jnp.int32)[None, :]).astype(
-        jnp.int32
+    packed, position = pack_rows(cand_emb, cand_route, user_count, group_size)
+    slots = packed.shape[0]
+    capacity = slots // user_count
+    placing = (lax.broadcasted_iota(jnp.int32, (slots, cand_rows), 0) == position).astype(
+        jnp.bfloat16
     )
-    ranking = jnp.sum(jnp.cumsum(onehot, axis=0) * onehot, axis=1) - 1
-    position = owner * capacity + ranking
-    placing = (
-        lax.broadcasted_iota(jnp.int32, (slots, cand_rows), 0) == position[None, :]
-    ).astype(jnp.bfloat16)
-    packed = jnp.dot(placing, cand_emb, preferred_element_type=jnp.float32).astype(jnp.bfloat16)
     outgoing = packed.reshape(user_count, capacity, features)
     items = lax.all_to_all(outgoing, "user", split_axis=0, concat_axis=0, tiled=True)
     history = hist_kv.reshape(hist_kv.shape[0], hist_kv.shape[2], hist_kv.shape[3])

time: 75 us -> 69.4 us (0.925)
  other arithmetic: 3.86 us -> 0.5 us
  matrix products: 4.46 us -> 1.73 us
    pallas_call x0 -> x1, Pallas kernels: none -> 3.07 us  [pack_rows(): pl.pallas_call(functools.partial(pack_kernel, group_size=group_size, user...]
    dot_general x1 -> x0, matrix products: 2.73 us -> none  [local(): jnp.dot(placing, cand_emb, preferred_element_type=jnp.float32)]
    pallas_call x1, Pallas kernels: 19.3 us -> 16.9 us  [run_layers(): pl.pallas_call(layers_kernel, grid_spec=grid_spec, out_shape=jax.ShapeDty...]
    another operation x2 -> x0, other arithmetic: 1.19 us -> none
where the time goes in v3:
time: 69.4 us; the launch traced here: 68.7 us
  Pallas kernels  19.9 us (29%)
  blocking collectives  19.6 us (28%)
  waiting for transfers between devices  17 us (24%)
  starting transfers between devices  7.96 us (11%)
  matrix products  1.73 us (2%)
  local copies, waits for them, and re-layouts  1.32 us (2%)
  between operations  0.7 us (1%)
    all_to_all x1, blocking collectives, local(): lax.all_to_all(delta, 'user', split_axis=0, concat_axis=0, tiled=True)  19.6 us
    all_to_all x1, waiting for transfers between devices, local(): lax.all_to_all(outgoing, 'user', split_axis=0, concat_axis=0, tiled=True)  17 us
    pallas_call x1, Pallas kernels, run_layers(): pl.pallas_call(layers_kernel, grid_spec=grid_spec, out_shape=jax.ShapeDty...  16.9 us
    all_to_all x1, starting transfers between devices, local(): lax.all_to_all(outgoing, 'user', split_axis=0, concat_axis=0, tiled=True)  7.96 us
    pallas_call x1, Pallas kernels, pack_rows(): pl.pallas_call(functools.partial(pack_kernel, group_size=group_size, user...  3.07 us
    dot_general x1, matrix products, local(): lax.dot_general(placing, returned.reshape(-1, features), (((0,), (0,)), (...  1.73 us
  transfers between devices with their start and end apart: 1, of which 1 were waited for; matrix products, arithmetic and copies ran while one was open for 0% of the time, Pallas kernels for 0%

profile of v3, /device:TPU:0, one launch (start us, length us, event | category | flops | bytes accessed | tf_op | source)
XLA Modules:
  0.0 68.7 jit_solution(3454095504410698109)
XLA Ops:
  0.0 0.0 copy-start
  0.0 3.1 %shard_map.64 = (bf16[1024,512]{1,0:T(8,128)(2,1)}, s32[1,512]{1,0:T(1,128)}) custom-call(s32[1,512]{1,0:T(1,128)} %bitcast.9, bf16[512,512]{1,0:T(8,128)(2,1)} %emb_ref.1), custom_call_target="tpu_custom_call" | custom-call | flops 545259520 | bytes 1572864 | tf_op jit(solution)/shard_map/pallas_call | solution.py:141
  3.1 8.0 %all-to-all-start = ((bf16[16,64,512]{2,1,0:T(8,128)(2,1)}), bf16[16,64,512]{2,1,0:T(8,128)(2,1)S(1)}, u32[]{:S(2)}, u32[]{:S(2)}) async-start(bf16[16,64,512]{2,1,0:T(8,128)(2,1)} %bitcast.6), calls=%async_computation | async-start | bytes 2097152 | tf_op jit(solution)/shard_map/all_to_all | solution.py:168
  11.7 17.0 %all-to-all-done.rows_ref = bf16[16,64,512]{2,1,0:T(8,128)(2,1)S(1)} async-done(((bf16[16,64,512]{2,1,0:T(8,128)(2,1)}), bf16[16,64,512]{2,1,0:T(8,128)(2,1)S(1)}, u32[]{:S(2)}, u32[]{:S(2)}) %all-to-all-start) | async-done | bytes 1048608 | tf_op jit(solution)/shard_map/all_to_all | solution.py:168
  28.7 0.4 compare_reduce_fusion
  29.1 0.1 reduce_or.14
  29.1 0.1 reduce_or.18
  29.3 0.0 copy-done
  29.3 0.0 copy-start.1
  29.3 1.2 %copy-done.1 = bf16[2,512,512]{2,1,0:T(8,128)(2,1)S(1)} copy-done((bf16[2,512,512]{2,1,0:T(8,128)(2,1)S(1)}, bf16[2,512,512]{2,1,0:T(8,128)(2,1)}, u32[]{:S(2)}) %copy-start.1) | copy-done | bytes 1048600
  30.5 16.9 %shard_map.65 = bf16[16,64,512]{2,1,0:T(8,128)(2,1)S(1)} custom-call(s32[1]{0:T(128)S(6)} %copy.7.length_ref, s32[4]{0:T(128)S(1)} %convert_element_type.8.busy_ref, bf16[16,64,512]{2,1,0:T(8,128)(2,1)S(1)} %all-to-all-done.rows_ref, bf16[2,1024,1024]{2,1,0:T(8,128)(2,1)} %bitcast.8, bf16[2,512,1024]{2,1,0:T(8,128)(2,1)S(1)} %copy-done, ...), custom_call_target="tpu_custom_call" | custom-call | flops 7516192768 | bytes 9437184 | tf_op jit(solution)/shard_map/pallas_call | solution.py:100
  47.4 0.0 copy-start.2
  47.4 0.0 copy-start.3
  47.4 19.6 %all_to_all.10 = bf16[16,64,512]{2,1,0:T(8,128)(2,1)S(1)} all-to-all(bf16[16,64,512]{2,1,0:T(8,128)(2,1)S(1)} %shard_map.65), channel_id=1, replica_groups=mesh['user'=16,'cand'=8] {'user'}, dimensions={0} | all-to-all | bytes 2097152 | tf_op jit(solution)/shard_map/all_to_all | solution.py:171
  67.0 0.0 copy-done.2
  67.0 0.0 copy-done.3
  67.0 1.7 %fusion.1 = f32[512,512]{1,0:T(8,128)} fusion(bf16[1024,512]{1,0:T(8,128)(2,1)S(1)} %bitcast.7, s32[512]{0:T(512)S(1)} %bitcast.10, bf16[512,512]{1,0:T(8,128)(2,1)S(1)} %copy-done.2), kind=kOutput, calls=%fused_computation.3 | convolution fusion | flops 537919488 | bytes 2623488 | tf_op jit(solution)/shard_map/dot_general | solution.py:172
  (1 shorter events, 0.0 us)
Async XLA Ops:
  0.0 29.3 %copy-start = (bf16[2,512,1024]{2,1,0:T(8,128)(2,1)S(1)}, bf16[2,512,1024]{2,1,0:T(8,128)(2,1)}, u32[]{:S(2)}) copy-start(bf16[2,512,1024]{2,1,0:T(8,128)(2,1)} %w_in_ref.1) | copy-start | bytes 6291460
  3.1 25.6 %all-to-all-start = ((bf16[16,64,512]{2,1,0:T(8,128)(2,1)}), bf16[16,64,512]{2,1,0:T(8,128)(2,1)S(1)}, u32[]{:S(2)}, u32[]{:S(2)}) async-start(bf16[16,64,512]{2,1,0:T(8,128)(2,1)} %bitcast.6), calls=%async_computation | async-start | bytes 2097152 | tf_op jit(solution)/shard_map/all_to_all | solution.py:168
  29.3 1.2 %copy-start.1 = (bf16[2,512,512]{2,1,0:T(8,128)(2,1)S(1)}, bf16[2,512,512]{2,1,0:T(8,128)(2,1)}, u32[]{:S(2)}) copy-start(bf16[2,512,512]{2,1,0:T(8,128)(2,1)} %w_out_ref.1) | copy-start | bytes 3145732
  47.4 19.6 %copy-start.2 = (bf16[512,512]{1,0:T(8,128)(2,1)S(1)}, bf16[512,512]{1,0:T(8,128)(2,1)}, u32[]{:S(2)}) copy-start(bf16[512,512]{1,0:T(8,128)(2,1)} %emb_ref.1) | copy-start | bytes 1572868
  47.4 19.6 %copy-start.3 = (s32[1,512]{1,0:T(1,128)S(1)}, s32[1,512]{1,0:T(1,128)}, u32[]{:S(2)}) copy-start(s32[1,512]{1,0:T(1,128)} %get-tuple-element.7) | copy-start | bytes 6148

commit v4 on v3

--- a/solution.py
+++ b/solution.py
@@ -54,12 +54,11 @@
             for head in range(HEADS):
                 low = head * head_dim
                 query = projected[:, features + low:features + low + head_dim]
-                query = (query.astype(jnp.float32) * factor).astype(jnp.bfloat16)
                 keys = hist_ref[layer_index, :, low:low + head_dim]
                 scores = lax.dot_general(
                     query, keys, (((1,), (1,)), ((), ())), preferred_element_type=jnp.float32
                 )
-                weight = silu(scores).astype(jnp.bfloat16)
+                weight = silu(scores * factor).astype(jnp.bfloat16)
                 heads.append(
                     jnp.dot(
                         weight,

time: 69.4 us -> 70.2 us (1.012)
  Pallas kernels: 19.9 us -> 21 us
    pallas_call x1, Pallas kernels: 16.9 us -> 17.9 us  [run_layers(): pl.pallas_call(layers_kernel, grid_spec=grid_spec, out_shape=jax.ShapeDty...]
where the time goes in v4:
time: 70.2 us; the launch traced here: 69.8 us
  Pallas kernels  21 us (30%)
  blocking collectives  19.6 us (28%)
  waiting for transfers between devices  17 us (24%)
  starting transfers between devices  7.96 us (11%)
  matrix products  1.73 us (2%)
  local copies, waits for them, and re-layouts  1.32 us (2%)
    all_to_all x1, blocking collectives, local(): lax.all_to_all(delta, 'user', split_axis=0, concat_axis=0, tiled=True)  19.6 us
    pallas_call x1, Pallas kernels, run_layers(): pl.pallas_call(layers_kernel, grid_spec=grid_spec, out_shape=jax.ShapeDty...  17.9 us
    all_to_all x1, waiting for transfers between devices, local(): lax.all_to_all(outgoing, 'user', split_axis=0, concat_axis=0, tiled=True)  17 us
    all_to_all x1, starting transfers between devices, local(): lax.all_to_all(outgoing, 'user', split_axis=0, concat_axis=0, tiled=True)  7.96 us
    pallas_call x1, Pallas kernels, pack_rows(): pl.pallas_call(functools.partial(pack_kernel, group_size=group_size, user...  3.07 us
    dot_general x1, matrix products, local(): lax.dot_general(placing, returned.reshape(-1, features), (((0,), (0,)), (...  1.73 us
  transfers between devices with their start and end apart: 1, of which 1 were waited for; matrix products, arithmetic and copies ran while one was open for 0% of the time, Pallas kernels for 0%

profile of v4, /device:TPU:0, one launch (start us, length us, event | category | flops | bytes accessed | tf_op | source)
XLA Modules:
  0.0 69.8 jit_solution(12750188002259124210)
XLA Ops:
  0.0 0.0 copy-start
  0.0 3.1 %shard_map.64 = (bf16[1024,512]{1,0:T(8,128)(2,1)}, s32[1,512]{1,0:T(1,128)}) custom-call(s32[1,512]{1,0:T(1,128)} %bitcast.9, bf16[512,512]{1,0:T(8,128)(2,1)} %emb_ref.1), custom_call_target="tpu_custom_call" | custom-call | flops 545259520 | bytes 1572864 | tf_op jit(solution)/shard_map/pallas_call | solution.py:140
  3.1 8.0 %all-to-all-start = ((bf16[16,64,512]{2,1,0:T(8,128)(2,1)}), bf16[16,64,512]{2,1,0:T(8,128)(2,1)S(1)}, u32[]{:S(2)}, u32[]{:S(2)}) async-start(bf16[16,64,512]{2,1,0:T(8,128)(2,1)} %bitcast.6), calls=%async_computation | async-start | bytes 2097152 | tf_op jit(solution)/shard_map/all_to_all | solution.py:167
  11.7 17.0 %all-to-all-done.rows_ref = bf16[16,64,512]{2,1,0:T(8,128)(2,1)S(1)} async-done(((bf16[16,64,512]{2,1,0:T(8,128)(2,1)}), bf16[16,64,512]{2,1,0:T(8,128)(2,1)S(1)}, u32[]{:S(2)}, u32[]{:S(2)}) %all-to-all-start) | async-done | bytes 1048608 | tf_op jit(solution)/shard_map/all_to_all | solution.py:167
  28.7 0.4 compare_reduce_fusion
  29.1 0.1 reduce_or.14
  29.1 0.1 reduce_or.18
  29.3 0.0 copy-done
  29.3 0.0 copy-start.1
  29.3 1.2 %copy-done.1 = bf16[2,512,512]{2,1,0:T(8,128)(2,1)S(1)} copy-done((bf16[2,512,512]{2,1,0:T(8,128)(2,1)S(1)}, bf16[2,512,512]{2,1,0:T(8,128)(2,1)}, u32[]{:S(2)}) %copy-start.1) | copy-done | bytes 1048600
  30.5 17.9 %shard_map.65 = bf16[16,64,512]{2,1,0:T(8,128)(2,1)S(1)} custom-call(s32[1]{0:T(128)S(6)} %copy.7.length_ref, s32[4]{0:T(128)S(1)} %convert_element_type.8.busy_ref, bf16[16,64,512]{2,1,0:T(8,128)(2,1)S(1)} %all-to-all-done.rows_ref, bf16[2,1024,1024]{2,1,0:T(8,128)(2,1)} %bitcast.8, bf16[2,512,1024]{2,1,0:T(8,128)(2,1)S(1)} %copy-done, ...), custom_call_target="tpu_custom_call" | custom-call | flops 7516192768 | bytes 9437184 | tf_op jit(solution)/shard_map/pallas_call | solution.py:99
  48.5 0.0 copy-start.2
  48.5 0.0 copy-start.3
  48.5 19.6 %all_to_all.10 = bf16[16,64,512]{2,1,0:T(8,128)(2,1)S(1)} all-to-all(bf16[16,64,512]{2,1,0:T(8,128)(2,1)S(1)} %shard_map.65), channel_id=1, replica_groups=mesh['user'=16,'cand'=8] {'user'}, dimensions={0} | all-to-all | bytes 2097152 | tf_op jit(solution)/shard_map/all_to_all | solution.py:170
  68.1 0.0 copy-done.2
  68.1 0.0 copy-done.3
  68.1 1.7 %fusion.1 = f32[512,512]{1,0:T(8,128)} fusion(bf16[1024,512]{1,0:T(8,128)(2,1)S(1)} %bitcast.7, s32[512]{0:T(512)S(1)} %bitcast.10, bf16[512,512]{1,0:T(8,128)(2,1)S(1)} %copy-done.2), kind=kOutput, calls=%fused_computation.3 | convolution fusion | flops 537919488 | bytes 2623488 | tf_op jit(solution)/shard_map/dot_general | solution.py:171
  (1 shorter events, 0.0 us)
Async XLA Ops:
  0.0 29.3 %copy-start = (bf16[2,512,1024]{2,1,0:T(8,128)(2,1)S(1)}, bf16[2,512,1024]{2,1,0:T(8,128)(2,1)}, u32[]{:S(2)}) copy-start(bf16[2,512,1024]{2,1,0:T(8,128)(2,1)} %w_in_ref.1) | copy-start | bytes 6291460
  3.1 25.6 %all-to-all-start = ((bf16[16,64,512]{2,1,0:T(8,128)(2,1)}), bf16[16,64,512]{2,1,0:T(8,128)(2,1)S(1)}, u32[]{:S(2)}, u32[]{:S(2)}) async-start(bf16[16,64,512]{2,1,0:T(8,128)(2,1)} %bitcast.6), calls=%async_computation | async-start | bytes 2097152 | tf_op jit(solution)/shard_map/all_to_all | solution.py:167
  29.3 1.2 %copy-start.1 = (bf16[2,512,512]{2,1,0:T(8,128)(2,1)S(1)}, bf16[2,512,512]{2,1,0:T(8,128)(2,1)}, u32[]{:S(2)}) copy-start(bf16[2,512,512]{2,1,0:T(8,128)(2,1)} %w_out_ref.1) | copy-start | bytes 3145732
  48.5 19.6 %copy-start.2 = (bf16[512,512]{1,0:T(8,128)(2,1)S(1)}, bf16[512,512]{1,0:T(8,128)(2,1)}, u32[]{:S(2)}) copy-start(bf16[512,512]{1,0:T(8,128)(2,1)} %emb_ref.1) | copy-start | bytes 1572868
  48.5 19.6 %copy-start.3 = (s32[1,512]{1,0:T(1,128)S(1)}, s32[1,512]{1,0:T(1,128)}, u32[]{:S(2)}) copy-start(s32[1,512]{1,0:T(1,128)} %get-tuple-element.7) | copy-start | bytes 6148

commit v5 on v4

--- a/solution.py
+++ b/solution.py
@@ -23,7 +23,10 @@
     return center * lax.rsqrt(spread + epsilon)
 
 
-def layers_kernel(length_ref, busy_ref, rows_ref, hist_ref, w_in_ref, w_out_ref, out_ref):
+def layers_kernel(
+    length_ref, busy_ref, rows_ref, w_in_ref, hist_hbm, w_out_hbm, out_ref, hist_ref, w_out_ref,
+    copy_sems,
+):
     sources, slots, features = rows_ref.shape
     block_rows = sources * slots
     layer_count = w_in_ref.shape[0]
@@ -31,10 +34,27 @@
     head_dim = features // HEADS
     factor = head_dim ** (-0.5)
     step = pl.program_id(0)
+    copies = [
+        pltpu.make_async_copy(hist_hbm.at[layer], hist_ref.at[layer], copy_sems.at[layer])
+        for layer in range(layer_count)
+    ]
+    copies.append(pltpu.make_async_copy(w_out_hbm, w_out_ref, copy_sems.at[layer_count]))
+
+    @pl.when(step == 0)
+    def _():
+        for copy in copies:
+            copy.start()
+
+    def arrive(index):
+        @pl.when(step == 0)
+        def _():
+            copies[index].wait()
 
     @pl.when(busy_ref[step] == 0)
     def _():
         out_ref[...] = jnp.zeros(out_ref.shape, out_ref.dtype)
+        for index in range(len(copies)):
+            arrive(index)
 
     @pl.when(busy_ref[step] != 0)
     def _():
@@ -47,6 +67,7 @@
             mixed = jnp.dot(normed, w_in_ref[layer_index], preferred_element_type=jnp.float32)
             projected = silu(mixed).astype(jnp.bfloat16)
             gate = projected[:, :features].astype(jnp.float32)
+            arrive(layer_index)
             values_all = jnp.where(
                 in_history, hist_ref[layer_index, :, features:], jnp.zeros((), jnp.bfloat16)
             )
@@ -68,6 +89,8 @@
                 )
             attended = jnp.concatenate(heads, axis=1)
             branch = (layer_normed(attended) * gate).astype(jnp.bfloat16)
+            if layer_index == 0:
+                arrive(layer_count)
             residual = residual + jnp.dot(
                 branch, w_out_ref[layer_index], preferred_element_type=jnp.float32
             )
@@ -86,11 +109,16 @@
         grid=(steps,),
         in_specs=[
             pl.BlockSpec((sources, SLOT_BLOCK, features), lambda i, n, b: (0, i, 0)),
-            pl.BlockSpec((layer_count, history_span, width), lambda i, n, b: (0, 0, 0)),
             pl.BlockSpec(w_in.shape, lambda i, n, b: (0, 0, 0)),
-            pl.BlockSpec(w_out.shape, lambda i, n, b: (0, 0, 0)),
+            pl.BlockSpec(memory_space=pltpu.MemorySpace.HBM),
+            pl.BlockSpec(memory_space=pltpu.MemorySpace.HBM),
         ],
         out_specs=pl.BlockSpec((sources, SLOT_BLOCK, features), lambda i, n, b: (0, i, 0)),
+        scratch_shapes=[
+            pltpu.VMEM(history.shape, history.dtype),
+            pltpu.VMEM(w_out.shape, w_out.dtype),
+            pltpu.SemaphoreType.DMA((layer_count + 1,)),
+        ],
     )
     row_count = sources * capacity
     flops = 2 * row_count * layer_count * (
@@ -108,7 +136,7 @@
             transcendentals=row_count * layer_count * (HEADS * history_span + 2 * features),
             bytes_accessed=2 * (history.size + w_in.size + w_out.size + 2 * buckets.size),
         ),
-    )(length, busy, buckets, history, w_in, w_out)
+    )(length, busy, buckets, w_in, history, w_out)
 
 
 def pack_kernel(route_ref, emb_ref, packed_ref, position_ref, *, group_size, user_count):

time: 70.2 us -> 69.6 us (level)
  no operation moved by 1% of the time
where the time goes in v5:
time: 69.6 us; the launch traced here: 69.3 us
  Pallas kernels  20.5 us (29%)
  blocking collectives  19.6 us (28%)
  waiting for transfers between devices  17 us (24%)
  starting transfers between devices  7.96 us (11%)
  matrix products  1.73 us (2%)
  local copies, waits for them, and re-layouts  1.32 us (2%)
  between operations  0.7 us (1%)
    all_to_all x1, blocking collectives, local(): lax.all_to_all(delta, 'user', split_axis=0, concat_axis=0, tiled=True)  19.6 us
    pallas_call x1, Pallas kernels, run_layers(): pl.pallas_call(layers_kernel, grid_spec=grid_spec, out_shape=jax.ShapeDty...  17.4 us
    all_to_all x1, waiting for transfers between devices, local(): lax.all_to_all(outgoing, 'user', split_axis=0, concat_axis=0, tiled=True)  17 us
    all_to_all x1, starting transfers between devices, local(): lax.all_to_all(outgoing, 'user', split_axis=0, concat_axis=0, tiled=True)  7.96 us
    pallas_call x1, Pallas kernels, pack_rows(): pl.pallas_call(functools.partial(pack_kernel, group_size=group_size, user...  3.07 us
    dot_general x1, matrix products, local(): lax.dot_general(placing, returned.reshape(-1, features), (((0,), (0,)), (...  1.73 us
  transfers between devices with their start and end apart: 1, of which 1 were waited for; matrix products, arithmetic and copies ran while one was open for 0% of the time, Pallas kernels for 0%

profile of v5, /device:TPU:0, one launch (start us, length us, event | category | flops | bytes accessed | tf_op | source)
XLA Modules:
  0.0 69.3 jit_solution(4587048768642658816)
XLA Ops:
  0.0 0.0 copy-start
  0.0 3.1 %shard_map.64 = (bf16[1024,512]{1,0:T(8,128)(2,1)}, s32[1,512]{1,0:T(1,128)}) custom-call(s32[1,512]{1,0:T(1,128)} %bitcast.9, bf16[512,512]{1,0:T(8,128)(2,1)} %emb_ref.1), custom_call_target="tpu_custom_call" | custom-call | flops 545259520 | bytes 1572864 | tf_op jit(solution)/shard_map/pallas_call | solution.py:168
  3.1 8.0 %all-to-all-start = ((bf16[16,64,512]{2,1,0:T(8,128)(2,1)}), bf16[16,64,512]{2,1,0:T(8,128)(2,1)S(1)}, u32[]{:S(2)}, u32[]{:S(2)}) async-start(bf16[16,64,512]{2,1,0:T(8,128)(2,1)} %bitcast.6), calls=%async_computation | async-start | bytes 2097152 | tf_op jit(solution)/shard_map/all_to_all | solution.py:195
  11.7 17.0 %all-to-all-done.rows_ref = bf16[16,64,512]{2,1,0:T(8,128)(2,1)S(1)} async-done(((bf16[16,64,512]{2,1,0:T(8,128)(2,1)}), bf16[16,64,512]{2,1,0:T(8,128)(2,1)S(1)}, u32[]{:S(2)}, u32[]{:S(2)}) %all-to-all-start) | async-done | bytes 1048608 | tf_op jit(solution)/shard_map/all_to_all | solution.py:195
  28.7 0.4 compare_reduce_fusion
  29.1 0.1 reduce_or.14
  29.1 0.1 reduce_or.18
  29.3 0.0 copy-done
  29.3 0.0 copy-start.1
  29.3 1.2 %copy-done.1 = bf16[2,512,512]{2,1,0:T(8,128)(2,1)S(1)} copy-done((bf16[2,512,512]{2,1,0:T(8,128)(2,1)S(1)}, bf16[2,512,512]{2,1,0:T(8,128)(2,1)}, u32[]{:S(2)}) %copy-start.1) | copy-done | bytes 1048600
  30.5 17.4 %shard_map.65 = bf16[16,64,512]{2,1,0:T(8,128)(2,1)S(1)} custom-call(s32[1]{0:T(128)S(6)} %copy.7.length_ref, s32[4]{0:T(128)S(1)} %convert_element_type.8.busy_ref, bf16[16,64,512]{2,1,0:T(8,128)(2,1)S(1)} %all-to-all-done.rows_ref, bf16[2,512,1024]{2,1,0:T(8,128)(2,1)S(1)} %copy-done, bf16[2,1024,1024]{2,1,0:T(8,128)(2,1)} %bitcast.8, ...), custom_call_target="tpu_custom_call" | custom-call | flops 7516192768 | bytes 9437184 | tf_op jit(solution)/shard_map/pallas_call | solution.py:127
  48.0 0.0 copy-start.2
  48.0 0.0 copy-start.3
  48.0 19.6 %all_to_all.10 = bf16[16,64,512]{2,1,0:T(8,128)(2,1)S(1)} all-to-all(bf16[16,64,512]{2,1,0:T(8,128)(2,1)S(1)} %shard_map.65), channel_id=1, replica_groups=mesh['user'=16,'cand'=8] {'user'}, dimensions={0} | all-to-all | bytes 2097152 | tf_op jit(solution)/shard_map/all_to_all | solution.py:198
  67.6 0.0 copy-done.2
  67.6 0.0 copy-done.3
  67.6 1.7 %fusion.1 = f32[512,512]{1,0:T(8,128)} fusion(bf16[1024,512]{1,0:T(8,128)(2,1)S(1)} %bitcast.7, s32[512]{0:T(512)S(1)} %bitcast.10, bf16[512,512]{1,0:T(8,128)(2,1)S(1)} %copy-done.2), kind=kOutput, calls=%fused_computation.3 | convolution fusion | flops 537919488 | bytes 2623488 | tf_op jit(solution)/shard_map/dot_general | solution.py:199
  (1 shorter events, 0.0 us)
Async XLA Ops:
  0.0 29.3 %copy-start = (bf16[2,512,1024]{2,1,0:T(8,128)(2,1)S(1)}, bf16[2,512,1024]{2,1,0:T(8,128)(2,1)}, u32[]{:S(2)}) copy-start(bf16[2,512,1024]{2,1,0:T(8,128)(2,1)} %w_in_ref.1) | copy-start | bytes 6291460
  3.1 25.6 %all-to-all-start = ((bf16[16,64,512]{2,1,0:T(8,128)(2,1)}), bf16[16,64,512]{2,1,0:T(8,128)(2,1)S(1)}, u32[]{:S(2)}, u32[]{:S(2)}) async-start(bf16[16,64,512]{2,1,0:T(8,128)(2,1)} %bitcast.6), calls=%async_computation | async-start | bytes 2097152 | tf_op jit(solution)/shard_map/all_to_all | solution.py:195
  29.3 1.2 %copy-start.1 = (bf16[2,512,512]{2,1,0:T(8,128)(2,1)S(1)}, bf16[2,512,512]{2,1,0:T(8,128)(2,1)}, u32[]{:S(2)}) copy-start(bf16[2,512,512]{2,1,0:T(8,128)(2,1)} %w_out_hbm.1) | copy-start | bytes 3145732
  48.0 19.6 %copy-start.2 = (bf16[512,512]{1,0:T(8,128)(2,1)S(1)}, bf16[512,512]{1,0:T(8,128)(2,1)}, u32[]{:S(2)}) copy-start(bf16[512,512]{1,0:T(8,128)(2,1)} %emb_ref.1) | copy-start | bytes 1572868
  48.0 19.6 %copy-start.3 = (s32[1,512]{1,0:T(1,128)S(1)}, s32[1,512]{1,0:T(1,128)}, u32[]{:S(2)}) copy-start(s32[1,512]{1,0:T(1,128)} %get-tuple-element.7) | copy-start | bytes 6148

commit v6 on v5

--- a/solution.py
+++ b/solution.py
@@ -139,10 +139,9 @@
     )(length, busy, buckets, w_in, history, w_out)
 
 
-def pack_kernel(route_ref, emb_ref, packed_ref, position_ref, *, group_size, user_count):
-    cand_rows = emb_ref.shape[0]
-    capacity = packed_ref.shape[0] // user_count
-    owner = route_ref[...] // group_size
+def rank_of(route, group_size, user_count, capacity):
+    cand_rows = route.shape[1]
+    owner = route // group_size
     member = (lax.broadcasted_iota(jnp.int32, (user_count, cand_rows), 0) == owner).astype(
         jnp.float32
     )
@@ -152,8 +151,17 @@
     ).astype(jnp.bfloat16)
     before = jnp.dot(member.astype(jnp.bfloat16), earlier, preferred_element_type=jnp.float32)
     ranking = jnp.sum(member * before, axis=0, keepdims=True).astype(jnp.int32)
-    position = owner * capacity + ranking
-    position_ref[...] = position
+    return owner * capacity + ranking
+
+
+def position_kernel(route_ref, position_ref, *, group_size, user_count, capacity):
+    position_ref[...] = rank_of(route_ref[...], group_size, user_count, capacity)
+
+
+def pack_kernel(route_ref, emb_ref, packed_ref, *, group_size, user_count):
+    cand_rows = emb_ref.shape[0]
+    capacity = packed_ref.shape[0] // user_count
+    position = rank_of(route_ref[...], group_size, user_count, capacity)
     placing = (
         lax.broadcasted_iota(jnp.int32, (packed_ref.shape[0], cand_rows), 0) == position
     ).astype(jnp.bfloat16)
@@ -165,20 +173,35 @@
 def pack_rows(cand_emb, cand_route, user_count, group_size):
     cand_rows, features = cand_emb.shape
     slots = 2 * cand_rows
-    return pl.pallas_call(
+    route = cand_route.reshape(1, cand_rows)
+    packed = pl.pallas_call(
         functools.partial(pack_kernel, group_size=group_size, user_count=user_count),
-        out_shape=(
-            jax.ShapeDtypeStruct((slots, features), jnp.bfloat16),
-            jax.ShapeDtypeStruct((1, cand_rows), jnp.int32),
-        ),
+        out_shape=jax.ShapeDtypeStruct((slots, features), jnp.bfloat16),
         in_specs=[pl.BlockSpec(memory_space=pltpu.VMEM)] * 2,
-        out_specs=(pl.BlockSpec(memory_space=pltpu.VMEM),) * 2,
+        out_specs=pl.BlockSpec(memory_space=pltpu.VMEM),
         cost_estimate=pl.CostEstimate(
             flops=2 * slots * cand_rows * features + 2 * user_count * cand_rows * cand_rows,
             transcendentals=0,
             bytes_accessed=2 * (cand_emb.size + slots * features),
         ),
-    )(cand_route.reshape(1, cand_rows), cand_emb)
+    )(route, cand_emb)
+    position = pl.pallas_call(
+        functools.partial(
+            position_kernel,
+            group_size=group_size,
+            user_count=user_count,
+            capacity=slots // user_count,
+        ),
+        out_shape=jax.ShapeDtypeStruct((1, cand_rows), jnp.int32),
+        in_specs=[pl.BlockSpec(memory_space=pltpu.VMEM)],
+        out_specs=pl.BlockSpec(memory_space=pltpu.VMEM),
+        cost_estimate=pl.CostEstimate(
+            flops=2 * user_count * cand_rows * cand_rows,
+            transcendentals=0,
+            bytes_accessed=8 * cand_rows,
+        ),
+    )(route)
+    return packed, position
 
 
 def local(cand_emb, cand_route, hist_kv, hist_len, w_in, w_out):

time: 69.6 us -> 71.5 us (1.027)
  blocking collectives: 19.6 us -> 0 us
  waiting for transfers between devices: 17 us -> 31.9 us
  starting transfers between devices: 7.96 us -> 11.8 us
  Pallas kernels: 20.5 us -> 22.6 us
    all_to_all x1 -> x0, blocking collectives: 19.6 us -> none  [local(): lax.all_to_all(delta, 'user', split_axis=0, concat_axis=0, tiled=True)]
    all_to_all x0 -> x1, waiting for transfers between devices: none -> 14.9 us  [local(): lax.all_to_all(delta, 'user', split_axis=0, concat_axis=0, tiled=True)]
    all_to_all x0 -> x1, starting transfers between devices: none -> 3.8 us  [local(): lax.all_to_all(delta, 'user', split_axis=0, concat_axis=0, tiled=True)]
    pallas_call x0 -> x1, Pallas kernels: none -> 1.44 us  [pack_rows(): pl.pallas_call(functools.partial(position_kernel, group_size=group_size,...]
  transfers between devices with their start and end apart: 1 -> 2, of which waited for: 1 -> 2; matrix products, arithmetic and copies ran while one was open for 0% -> 0% of each run, Pallas kernels for 0% -> 2%
where the time goes in v6:
time: 71.5 us; the launch traced here: 71.2 us
  waiting for transfers between devices  31.9 us (45%)
  Pallas kernels  22.6 us (32%)
  starting transfers between devices  11.8 us (17%)
  matrix products  2.38 us (3%)
  local copies, waits for them, and re-layouts  1.32 us (2%)
    pallas_call x1, Pallas kernels, run_layers(): pl.pallas_call(layers_kernel, grid_spec=grid_spec, out_shape=jax.ShapeDty...  18.1 us
    all_to_all x1, waiting for transfers between devices, local(): lax.all_to_all(outgoing, 'user', split_axis=0, concat_axis=0, tiled=True)  17 us
    all_to_all x1, waiting for transfers between devices, local(): lax.all_to_all(delta, 'user', split_axis=0, concat_axis=0, tiled=True)  14.9 us
    all_to_all x1, starting transfers between devices, local(): lax.all_to_all(outgoing, 'user', split_axis=0, concat_axis=0, tiled=True)  7.96 us
    all_to_all x1, starting transfers between devices, local(): lax.all_to_all(delta, 'user', split_axis=0, concat_axis=0, tiled=True)  3.8 us
    pallas_call x1, Pallas kernels, pack_rows(): pl.pallas_call(functools.partial(pack_kernel, group_size=group_size, user...  3.07 us
    dot_general x1, matrix products, local(): lax.dot_general(placing, returned.reshape(-1, features), (((0,), (0,)), (...  2.38 us
    pallas_call x1, Pallas kernels, pack_rows(): pl.pallas_call(functools.partial(position_kernel, group_size=group_size,...  1.44 us
  transfers between devices with their start and end apart: 2, of which 2 were waited for; matrix products, arithmetic and copies ran while one was open for 0% of the time, Pallas kernels for 2%

profile of v6, /device:TPU:0, one launch (start us, length us, event | category | flops | bytes accessed | tf_op | source)
XLA Modules:
  0.0 71.2 jit_solution(3088353475835816882)
XLA Ops:
  0.0 0.0 copy-start
  0.0 3.1 %shard_map.65 = bf16[1024,512]{1,0:T(8,128)(2,1)} custom-call(s32[1,512]{1,0:T(1,128)} %bitcast.9, bf16[512,512]{1,0:T(8,128)(2,1)} %emb_ref.1), custom_call_target="tpu_custom_call" | custom-call | flops 545259520 | bytes 1572864 | tf_op jit(solution)/shard_map/pallas_call | solution.py:177
  3.1 8.0 %all-to-all-start = ((bf16[16,64,512]{2,1,0:T(8,128)(2,1)}), bf16[16,64,512]{2,1,0:T(8,128)(2,1)S(1)}, u32[]{:S(2)}, u32[]{:S(2)}) async-start(bf16[16,64,512]{2,1,0:T(8,128)(2,1)} %bitcast.7), calls=%async_computation | async-start | bytes 2097152 | tf_op jit(solution)/shard_map/all_to_all | solution.py:218
  11.7 17.0 %all-to-all-done.rows_ref = bf16[16,64,512]{2,1,0:T(8,128)(2,1)S(1)} async-done(((bf16[16,64,512]{2,1,0:T(8,128)(2,1)}), bf16[16,64,512]{2,1,0:T(8,128)(2,1)S(1)}, u32[]{:S(2)}, u32[]{:S(2)}) %all-to-all-start) | async-done | bytes 1048608 | tf_op jit(solution)/shard_map/all_to_all | solution.py:218
  28.7 0.4 compare_reduce_fusion
  29.0 0.1 reduce_or.14
  29.1 0.1 reduce_or.18
  29.3 0.0 copy-done
  29.3 0.0 copy-start.1
  29.3 1.2 %copy-done.1 = bf16[2,512,512]{2,1,0:T(8,128)(2,1)S(1)} copy-done((bf16[2,512,512]{2,1,0:T(8,128)(2,1)S(1)}, bf16[2,512,512]{2,1,0:T(8,128)(2,1)}, u32[]{:S(2)}) %copy-start.1) | copy-done | bytes 1048600
  30.5 18.1 %shard_map.66 = bf16[16,64,512]{2,1,0:T(8,128)(2,1)} custom-call(s32[1]{0:T(128)S(6)} %copy.7.length_ref, s32[4]{0:T(128)S(1)} %convert_element_type.8.busy_ref, bf16[16,64,512]{2,1,0:T(8,128)(2,1)S(1)} %all-to-all-done.rows_ref, bf16[2,512,1024]{2,1,0:T(8,128)(2,1)S(1)} %copy-done, bf16[2,1024,1024]{2,1,0:T(8,128)(2,1)} %bitcast.8, ...), custom_call_target="tpu_custom_call" | custom-call | flops 7516192768 | bytes 9437184 | tf_op jit(solution)/shard_map/pallas_call | solution.py:127
  48.6 0.0 copy-start.2
  48.6 3.8 %all-to-all-start.1 = ((bf16[16,64,512]{2,1,0:T(8,128)(2,1)}), bf16[16,64,512]{2,1,0:T(8,128)(2,1)S(1)}, u32[]{:S(2)}, u32[]{:S(2)}) async-start(bf16[16,64,512]{2,1,0:T(8,128)(2,1)} %shard_map.66), calls=%async_computation.1 | async-start | bytes 2097152 | tf_op jit(solution)/shard_map/all_to_all | solution.py:221
  52.4 1.4 %shard_map.64 = s32[1,512]{1,0:T(1,128)} custom-call(s32[1,512]{1,0:T(1,128)} %bitcast.10), custom_call_target="tpu_custom_call" | custom-call | flops 8388608 | bytes 4096 | tf_op jit(solution)/shard_map/pallas_call | solution.py:188
  53.9 14.9 %all-to-all-done.1 = bf16[16,64,512]{2,1,0:T(8,128)(2,1)S(1)} async-done(((bf16[16,64,512]{2,1,0:T(8,128)(2,1)}), bf16[16,64,512]{2,1,0:T(8,128)(2,1)S(1)}, u32[]{:S(2)}, u32[]{:S(2)}) %all-to-all-start.1) | async-done | bytes 1048608 | tf_op jit(solution)/shard_map/all_to_all | solution.py:221
  68.8 0.0 copy-done.2
  68.8 2.4 %fusion.1 = f32[512,512]{1,0:T(8,128)} fusion(bf16[1024,512]{1,0:T(8,128)(2,1)S(1)} %bitcast.6, s32[512]{0:T(512)} %bitcast.11, bf16[512,512]{1,0:T(8,128)(2,1)S(1)} %copy-done.2), kind=kOutput, calls=%fused_computation.3 | convolution fusion | flops 537919488 | bytes 2623488 | tf_op jit(solution)/shard_map/dot_general | solution.py:222
  (1 shorter events, 0.0 us)
Async XLA Ops:
  0.0 29.3 %copy-start = (bf16[2,512,1024]{2,1,0:T(8,128)(2,1)S(1)}, bf16[2,512,1024]{2,1,0:T(8,128)(2,1)}, u32[]{:S(2)}) copy-start(bf16[2,512,1024]{2,1,0:T(8,128)(2,1)} %w_in_ref.1) | copy-start | bytes 6291460
  3.1 25.6 %all-to-all-start = ((bf16[16,64,512]{2,1,0:T(8,128)(2,1)}), bf16[16,64,512]{2,1,0:T(8,128)(2,1)S(1)}, u32[]{:S(2)}, u32[]{:S(2)}) async-start(bf16[16,64,512]{2,1,0:T(8,128)(2,1)} %bitcast.7), calls=%async_computation | async-start | bytes 2097152 | tf_op jit(solution)/shard_map/all_to_all | solution.py:218
  29.3 1.2 %copy-start.1 = (bf16[2,512,512]{2,1,0:T(8,128)(2,1)S(1)}, bf16[2,512,512]{2,1,0:T(8,128)(2,1)}, u32[]{:S(2)}) copy-start(bf16[2,512,512]{2,1,0:T(8,128)(2,1)} %w_out_hbm.1) | copy-start | bytes 3145732
  48.6 20.1 %copy-start.2 = (bf16[512,512]{1,0:T(8,128)(2,1)S(1)}, bf16[512,512]{1,0:T(8,128)(2,1)}, u32[]{:S(2)}) copy-start(bf16[512,512]{1,0:T(8,128)(2,1)} %emb_ref.1) | copy-start | bytes 1572868
  48.6 20.1 %all-to-all-start.1 = ((bf16[16,64,512]{2,1,0:T(8,128)(2,1)}), bf16[16,64,512]{2,1,0:T(8,128)(2,1)S(1)}, u32[]{:S(2)}, u32[]{:S(2)}) async-start(bf16[16,64,512]{2,1,0:T(8,128)(2,1)} %shard_map.66), calls=%async_computation.1 | async-start | bytes 2097152 | tf_op jit(solution)/shard_map/all_to_all | solution.py:221

commit v7 on v5

--- a/solution.py
+++ b/solution.py
@@ -23,22 +23,18 @@
     return center * lax.rsqrt(spread + epsilon)
 
 
-def layers_kernel(
-    length_ref, busy_ref, rows_ref, w_in_ref, hist_hbm, w_out_hbm, out_ref, hist_ref, w_out_ref,
-    copy_sems,
-):
+def layers_kernel(length_ref, busy_ref, rows_ref, w_in_ref, tables_hbm, out_ref, tables_ref, copy_sems):
     sources, slots, features = rows_ref.shape
     block_rows = sources * slots
     layer_count = w_in_ref.shape[0]
-    history_span = hist_ref.shape[1]
+    history_span = tables_ref.shape[1] - features
     head_dim = features // HEADS
     factor = head_dim ** (-0.5)
     step = pl.program_id(0)
     copies = [
-        pltpu.make_async_copy(hist_hbm.at[layer], hist_ref.at[layer], copy_sems.at[layer])
+        pltpu.make_async_copy(tables_hbm.at[layer], tables_ref.at[layer], copy_sems.at[layer])
         for layer in range(layer_count)
     ]
-    copies.append(pltpu.make_async_copy(w_out_hbm, w_out_ref, copy_sems.at[layer_count]))
 
     @pl.when(step == 0)
     def _():
@@ -58,8 +54,6 @@
 
     @pl.when(busy_ref[step] != 0)
     def _():
-        length = length_ref[0]
-        in_history = lax.broadcasted_iota(jnp.int32, (history_span, 1), 0) < length
         start = rows_ref[...].astype(jnp.float32).reshape(block_rows, features)
         residual = start
         for layer_index in range(layer_count):
@@ -68,14 +62,11 @@
             projected = silu(mixed).astype(jnp.bfloat16)
             gate = projected[:, :features].astype(jnp.float32)
             arrive(layer_index)
-            values_all = jnp.where(
-                in_history, hist_ref[layer_index, :, features:], jnp.zeros((), jnp.bfloat16)
-            )
             heads = []
             for head in range(HEADS):
                 low = head * head_dim
                 query = projected[:, features + low:features + low + head_dim]
-                keys = hist_ref[layer_index, :, low:low + head_dim]
+                keys = tables_ref[layer_index, :history_span, low:low + head_dim]
                 scores = lax.dot_general(
                     query, keys, (((1,), (1,)), ((), ())), preferred_element_type=jnp.float32
                 )
@@ -83,16 +74,18 @@
                 heads.append(
                     jnp.dot(
                         weight,
-                        values_all[:, low:low + head_dim],
+                        tables_ref[
+                            layer_index, :history_span, features + low:features + low + head_dim
+                        ],
                         preferred_element_type=jnp.float32,
                     )
                 )
             attended = jnp.concatenate(heads, axis=1)
             branch = (layer_normed(attended) * gate).astype(jnp.bfloat16)
-            if layer_index == 0:
-                arrive(layer_count)
             residual = residual + jnp.dot(
-                branch, w_out_ref[layer_index], preferred_element_type=jnp.float32
+                branch,
+                tables_ref[layer_index, history_span:, :features],
+                preferred_element_type=jnp.float32,
             )
         out_ref[...] = (residual - start).reshape(sources, slots, features).astype(out_ref.dtype)
 
@@ -100,6 +93,17 @@
 def run_layers(buckets, history, length, w_in, w_out):
     sources, capacity, features = buckets.shape
     layer_count, history_span, width = history.shape
+    in_history = lax.broadcasted_iota(jnp.int32, (1, history_span, 1), 1) < length[0]
+    tables = jnp.concatenate(
+        [
+            history[:, :, :features],
+            jnp.where(in_history, history[:, :, features:], jnp.zeros((), history.dtype)),
+        ],
+        axis=2,
+    )
+    tables = jnp.concatenate(
+        [tables, jnp.pad(w_out, ((0, 0), (0, 0), (0, width - features)))], axis=1
+    )
     steps = capacity // SLOT_BLOCK
     busy = jnp.any(
         buckets.reshape(sources, steps, SLOT_BLOCK * features) != 0, axis=(0, 2)
@@ -111,13 +115,11 @@
             pl.BlockSpec((sources, SLOT_BLOCK, features), lambda i, n, b: (0, i, 0)),
             pl.BlockSpec(w_in.shape, lambda i, n, b: (0, 0, 0)),
             pl.BlockSpec(memory_space=pltpu.MemorySpace.HBM),
-            pl.BlockSpec(memory_space=pltpu.MemorySpace.HBM),
         ],
         out_specs=pl.BlockSpec((sources, SLOT_BLOCK, features), lambda i, n, b: (0, i, 0)),
         scratch_shapes=[
-            pltpu.VMEM(history.shape, history.dtype),
-            pltpu.VMEM(w_out.shape, w_out.dtype),
-            pltpu.SemaphoreType.DMA((layer_count + 1,)),
+            pltpu.VMEM(tables.shape, tables.dtype),
+            pltpu.SemaphoreType.DMA((layer_count,)),
         ],
     )
     row_count = sources * capacity
@@ -136,7 +138,7 @@
             transcendentals=row_count * layer_count * (HEADS * history_span + 2 * features),
             bytes_accessed=2 * (history.size + w_in.size + w_out.size + 2 * buckets.size),
         ),
-    )(length, busy, buckets, w_in, history, w_out)
+    )(length, busy, buckets, w_in, tables)
 
 
 def pack_kernel(route_ref, emb_ref, packed_ref, position_ref, *, group_size, user_count):

time: 69.6 us -> 69.7 us (level)
  waiting for transfers between devices: 17 us -> 2.36 us
  other arithmetic: 0.5 us -> 15 us
  blocking collectives: 19.6 us -> 21.2 us
  local copies, waits for them, and re-layouts: 1.32 us -> 0.11 us
    all_to_all x1, waiting for transfers between devices: 17 us -> 2.36 us  [local(): lax.all_to_all(outgoing, 'user', split_axis=0, concat_axis=0, tiled=True)]
    concatenate x0 -> x1, other arithmetic: none -> 11.9 us  [run_layers(): jnp.concatenate([tables, jnp.pad(w_out, ((0, 0), (0, 0), (0, width - feat...]
    slice x0 -> x1, other arithmetic: none -> 2.63 us  [run_layers(): history[:, :, :features]]
    all_to_all x1, blocking collectives: 19.6 us -> 21.2 us  [local(): lax.all_to_all(delta, 'user', split_axis=0, concat_axis=0, tiled=True)]
    unnamed x8, local copies, waits for them, and re-layouts: 1.23 us -> 0.02 us
  transfers between devices with their start and end apart: 1 -> 1, of which waited for: 1 -> 1; matrix products, arithmetic and copies ran while one was open for 0% -> 21% of each run, Pallas kernels for 0% -> 0%
where the time goes in v7:
time: 69.7 us; the launch traced here: 69.4 us
  blocking collectives  21.2 us (30%)
  Pallas kernels  20.2 us (29%)
  other arithmetic  15 us (22%)
  starting transfers between devices  7.96 us (11%)
  waiting for transfers between devices  2.36 us (3%)
  matrix products  1.73 us (2%)
  between operations  0.82 us (1%)
    all_to_all x1, blocking collectives, local(): lax.all_to_all(delta, 'user', split_axis=0, concat_axis=0, tiled=True)  21.2 us
    pallas_call x1, Pallas kernels, run_layers(): pl.pallas_call(layers_kernel, grid_spec=grid_spec, out_shape=jax.ShapeDty...  17.3 us
    concatenate x1, other arithmetic, run_layers(): jnp.concatenate([tables, jnp.pad(w_out, ((0, 0), (0, 0), (0, width - feat...  11.9 us
    all_to_all x1, starting transfers between devices, local(): lax.all_to_all(outgoing, 'user', split_axis=0, concat_axis=0, tiled=True)  7.96 us
    pallas_call x1, Pallas kernels, pack_rows(): pl.pallas_call(functools.partial(pack_kernel, group_size=group_size, user...  2.92 us
    slice x1, other arithmetic, run_layers(): history[:, :, :features]  2.63 us
    all_to_all x1, waiting for transfers between devices, local(): lax.all_to_all(outgoing, 'user', split_axis=0, concat_axis=0, tiled=True)  2.36 us
    dot_general x1, matrix products, local(): lax.dot_general(placing, returned.reshape(-1, features), (((0,), (0,)), (...  1.73 us
  transfers between devices with their start and end apart: 1, of which 1 were waited for; matrix products, arithmetic and copies ran while one was open for 21% of the time, Pallas kernels for 0%

profile of v7, /device:TPU:0, one launch (start us, length us, event | category | flops | bytes accessed | tf_op | source)
XLA Modules:
  0.0 69.4 jit_solution(13354655343566017801)
XLA Ops:
  0.0 2.9 %shard_map.64 = (bf16[1024,512]{1,0:T(8,128)(2,1)}, s32[1,512]{1,0:T(1,128)}) custom-call(s32[1,512]{1,0:T(1,128)} %bitcast.11, bf16[512,512]{1,0:T(8,128)(2,1)} %emb_ref.1), custom_call_target="tpu_custom_call" | custom-call | flops 545259520 | bytes 1572864 | tf_op jit(solution)/shard_map/pallas_call | solution.py:170
  2.9 8.0 %all-to-all-start = ((bf16[16,64,512]{2,1,0:T(8,128)(2,1)}), bf16[16,64,512]{2,1,0:T(8,128)(2,1)S(1)}, u32[]{:S(2)}, u32[]{:S(2)}) async-start(bf16[16,64,512]{2,1,0:T(8,128)(2,1)} %bitcast.9), calls=%async_computation | async-start | bytes 2097152 | tf_op jit(solution)/shard_map/all_to_all | solution.py:197
  10.9 0.0 copy-start.1
  11.7 2.6 %fusion.5 = (bf16[2,1024,512]{2,1,0:T(8,128)(2,1)S(1)}, bf16[2,1024,512]{2,1,0:T(8,128)(2,1)S(1)}) fusion(bf16[2,1024,1024]{2,1,0:T(8,128)(2,1)} %bitcast.8, pred[1024]{0:T(1024)(128)(4,1)S(1)} %iota_compare_fusion.5), kind=kLoop, calls=%fused_computation.10 | loop fusion | flops 1048576 | bytes 8389632 | tf_op jit(solution)/shard_map/slice | solution.py:99
  14.3 0.0 copy-done.1
  14.3 0.0 copy-start
  14.3 11.9 %fusion.1.tables_hbm = bf16[2,1536,1024]{2,1,0:T(8,128)(2,1)} fusion(bf16[2,512,512]{2,1,0:T(8,128)(2,1)S(1)} %copy-done.1, bf16[2,1024,512]{2,1,0:T(8,128)(2,1)S(1)} %get-tuple-element.10, bf16[2,1024,512]{2,1,0:T(8,128)(2,1)S(1)} %get-tuple-element.9), kind=kLoop, calls=%fused_computation.2 | loop fusion | flops 25165824 | bytes 11534336 | tf_op jit(solution)/shard_map/concatenate | solution.py:104
  26.2 2.4 %all-to-all-done.rows_ref = bf16[16,64,512]{2,1,0:T(8,128)(2,1)S(1)} async-done(((bf16[16,64,512]{2,1,0:T(8,128)(2,1)}), bf16[16,64,512]{2,1,0:T(8,128)(2,1)S(1)}, u32[]{:S(2)}, u32[]{:S(2)}) %all-to-all-start) | async-done | bytes 1048608 | tf_op jit(solution)/shard_map/all_to_all | solution.py:197
  28.5 0.4 compare_reduce_fusion
  28.9 0.1 reduce_or.14
  29.0 0.1 reduce_or.18
  29.1 0.0 copy-done
  29.1 0.0 copy-start.2
  29.1 0.0 copy-start.3
  29.1 17.3 %shard_map.65 = bf16[16,64,512]{2,1,0:T(8,128)(2,1)S(1)} custom-call(s32[1]{0:T(128)} %copy.7.length_ref, s32[4]{0:T(128)S(1)} %convert_element_type.10.busy_ref, bf16[16,64,512]{2,1,0:T(8,128)(2,1)S(1)} %all-to-all-done.rows_ref, bf16[2,512,1024]{2,1,0:T(8,128)(2,1)S(1)} %copy-done, bf16[2,1536,1024]{2,1,0:T(8,128)(2,1)} %fusion.1.tables_hbm), custom_call_target="tpu_custom_call" | custom-call | flops 7516192768 | bytes 9437184 | tf_op jit(solution)/shard_map/pallas_call | solution.py:129
  46.4 21.2 %all_to_all.10 = bf16[16,64,512]{2,1,0:T(8,128)(2,1)S(1)} all-to-all(bf16[16,64,512]{2,1,0:T(8,128)(2,1)S(1)} %shard_map.65), channel_id=1, replica_groups=mesh['user'=16,'cand'=8] {'user'}, dimensions={0} | all-to-all | bytes 2097152 | tf_op jit(solution)/shard_map/all_to_all | solution.py:200
  67.7 0.0 copy-done.2
  67.7 0.0 copy-done.3
  67.7 1.7 %fusion.3 = f32[512,512]{1,0:T(8,128)} fusion(bf16[1024,512]{1,0:T(8,128)(2,1)S(1)} %bitcast.10, s32[512]{0:T(512)S(1)} %bitcast.12, bf16[512,512]{1,0:T(8,128)(2,1)S(1)} %copy-done.2), kind=kOutput, calls=%fused_computation.7 | convolution fusion | flops 537919488 | bytes 2623488 | tf_op jit(solution)/shard_map/dot_general | solution.py:201
  (2 shorter events, 0.0 us)
Async XLA Ops:
  2.9 25.6 %all-to-all-start = ((bf16[16,64,512]{2,1,0:T(8,128)(2,1)}), bf16[16,64,512]{2,1,0:T(8,128)(2,1)S(1)}, u32[]{:S(2)}, u32[]{:S(2)}) async-start(bf16[16,64,512]{2,1,0:T(8,128)(2,1)} %bitcast.9), calls=%async_computation | async-start | bytes 2097152 | tf_op jit(solution)/shard_map/all_to_all | solution.py:197
  10.9 3.4 %copy-start.1 = (bf16[2,512,512]{2,1,0:T(8,128)(2,1)S(1)}, bf16[2,512,512]{2,1,0:T(8,128)(2,1)}, u32[]{:S(2)}) copy-start(bf16[2,512,512]{2,1,0:T(8,128)(2,1)} %param.11) | copy-start | bytes 3145732
  14.3 14.8 %copy-start = (bf16[2,512,1024]{2,1,0:T(8,128)(2,1)S(1)}, bf16[2,512,1024]{2,1,0:T(8,128)(2,1)}, u32[]{:S(2)}) copy-start(bf16[2,512,1024]{2,1,0:T(8,128)(2,1)} %w_in_ref.1) | copy-start | bytes 6291460
  29.1 38.6 %copy-start.2 = (bf16[512,512]{1,0:T(8,128)(2,1)S(1)}, bf16[512,512]{1,0:T(8,128)(2,1)}, u32[]{:S(2)}) copy-start(bf16[512,512]{1,0:T(8,128)(2,1)} %emb_ref.1) | copy-start | bytes 1572868
  29.1 38.6 %copy-start.3 = (s32[1,512]{1,0:T(1,128)S(1)}, s32[1,512]{1,0:T(1,128)}, u32[]{:S(2)}) copy-start(s32[1,512]{1,0:T(1,128)} %get-tuple-element.7) | copy-start | bytes 6148

commit v8 on v7

--- a/solution.py
+++ b/solution.py
@@ -23,7 +23,7 @@
     return center * lax.rsqrt(spread + epsilon)
 
 
-def layers_kernel(length_ref, busy_ref, rows_ref, w_in_ref, tables_hbm, out_ref, tables_ref, copy_sems):
+def layers_kernel(rows_ref, w_in_ref, tables_hbm, out_ref, tables_ref, copy_sems):
     sources, slots, features = rows_ref.shape
     block_rows = sources * slots
     layer_count = w_in_ref.shape[0]
@@ -46,13 +46,15 @@
         def _():
             copies[index].wait()
 
-    @pl.when(busy_ref[step] == 0)
+    busy = jnp.max(jnp.abs(rows_ref[...].astype(jnp.float32))) > 0
+
+    @pl.when(jnp.logical_not(busy))
     def _():
         out_ref[...] = jnp.zeros(out_ref.shape, out_ref.dtype)
         for index in range(len(copies)):
             arrive(index)
 
-    @pl.when(busy_ref[step] != 0)
+    @pl.when(busy)
     def _():
         start = rows_ref[...].astype(jnp.float32).reshape(block_rows, features)
         residual = start
@@ -105,18 +107,15 @@
         [tables, jnp.pad(w_out, ((0, 0), (0, 0), (0, width - features)))], axis=1
     )
     steps = capacity // SLOT_BLOCK
-    busy = jnp.any(
-        buckets.reshape(sources, steps, SLOT_BLOCK * features) != 0, axis=(0, 2)
-    ).astype(jnp.int32)
     grid_spec = pltpu.PrefetchScalarGridSpec(
-        num_scalar_prefetch=2,
+        num_scalar_prefetch=0,
         grid=(steps,),
         in_specs=[
-            pl.BlockSpec((sources, SLOT_BLOCK, features), lambda i, n, b: (0, i, 0)),
-            pl.BlockSpec(w_in.shape, lambda i, n, b: (0, 0, 0)),
+            pl.BlockSpec((sources, SLOT_BLOCK, features), lambda i: (0, i, 0)),
+            pl.BlockSpec(w_in.shape, lambda i: (0, 0, 0)),
             pl.BlockSpec(memory_space=pltpu.MemorySpace.HBM),
         ],
-        out_specs=pl.BlockSpec((sources, SLOT_BLOCK, features), lambda i, n, b: (0, i, 0)),
+        out_specs=pl.BlockSpec((sources, SLOT_BLOCK, features), lambda i: (0, i, 0)),
         scratch_shapes=[
             pltpu.VMEM(tables.shape, tables.dtype),
             pltpu.SemaphoreType.DMA((layer_count,)),
@@ -138,7 +137,7 @@
             transcendentals=row_count * layer_count * (HEADS * history_span + 2 * features),
             bytes_accessed=2 * (history.size + w_in.size + w_out.size + 2 * buckets.size),
         ),
-    )(length, busy, buckets, w_in, tables)
+    )(buckets, w_in, tables)
 
 
 def pack_kernel(route_ref, emb_ref, packed_ref, position_ref, *, group_size, user_count):

time: 69.7 us -> 69 us (0.990)
  no operation moved by 1% of the time
where the time goes in v8:
time: 69 us; the launch traced here: 68.8 us
  blocking collectives  21.3 us (31%)
  Pallas kernels  20.1 us (29%)
  other arithmetic  14.5 us (21%)
  starting transfers between devices  7.96 us (12%)
  waiting for transfers between devices  2.33 us (3%)
  matrix products  1.73 us (3%)
  between operations  0.8 us (1%)
    all_to_all x1, blocking collectives, local(): lax.all_to_all(delta, 'user', split_axis=0, concat_axis=0, tiled=True)  21.3 us
    pallas_call x1, Pallas kernels, run_layers(): pl.pallas_call(layers_kernel, grid_spec=grid_spec, out_shape=jax.ShapeDty...  17.2 us
    concatenate x1, other arithmetic, run_layers(): jnp.concatenate([tables, jnp.pad(w_out, ((0, 0), (0, 0), (0, width - feat...  11.9 us
    all_to_all x1, starting transfers between devices, local(): lax.all_to_all(outgoing, 'user', split_axis=0, concat_axis=0, tiled=True)  7.96 us
    pallas_call x1, Pallas kernels, pack_rows(): pl.pallas_call(functools.partial(pack_kernel, group_size=group_size, user...  2.92 us
    slice x1, other arithmetic, run_layers(): history[:, :, :features]  2.63 us
    all_to_all x1, waiting for transfers between devices, local(): lax.all_to_all(outgoing, 'user', split_axis=0, concat_axis=0, tiled=True)  2.33 us
    dot_general x1, matrix products, local(): lax.dot_general(placing, returned.reshape(-1, features), (((0,), (0,)), (...  1.73 us
  transfers between devices with their start and end apart: 1, of which 1 were waited for; matrix products, arithmetic and copies ran while one was open for 21% of the time, Pallas kernels for 0%

profile of v8, /device:TPU:0, one launch (start us, length us, event | category | flops | bytes accessed | tf_op | source)
XLA Modules:
  0.0 68.8 jit_solution(3234541039083113468)
XLA Ops:
  0.0 2.9 %shard_map.64 = (bf16[1024,512]{1,0:T(8,128)(2,1)}, s32[1,512]{1,0:T(1,128)}) custom-call(s32[1,512]{1,0:T(1,128)} %bitcast.11, bf16[512,512]{1,0:T(8,128)(2,1)} %emb_ref.1), custom_call_target="tpu_custom_call" | custom-call | flops 545259520 | bytes 1572864 | tf_op jit(solution)/shard_map/pallas_call | solution.py:169
  2.9 8.0 %all-to-all-start = ((bf16[16,64,512]{2,1,0:T(8,128)(2,1)}), bf16[16,64,512]{2,1,0:T(8,128)(2,1)S(1)}, u32[]{:S(2)}, u32[]{:S(2)}) async-start(bf16[16,64,512]{2,1,0:T(8,128)(2,1)} %bitcast.9), calls=%async_computation | async-start | bytes 2097152 | tf_op jit(solution)/shard_map/all_to_all | solution.py:196
  10.9 0.0 copy-start.1
  11.7 2.6 %fusion.5 = (bf16[2,1024,512]{2,1,0:T(8,128)(2,1)S(1)}, bf16[2,1024,512]{2,1,0:T(8,128)(2,1)S(1)}) fusion(bf16[2,1024,1024]{2,1,0:T(8,128)(2,1)} %bitcast.8, pred[1024]{0:T(1024)(128)(4,1)S(1)} %iota_compare_fusion.5), kind=kLoop, calls=%fused_computation.9 | loop fusion | flops 1048576 | bytes 8389632 | tf_op jit(solution)/shard_map/slice | solution.py:101
  14.3 0.0 copy-start
  14.3 0.0 copy-done.1
  14.3 11.9 %fusion.1.tables_hbm = bf16[2,1536,1024]{2,1,0:T(8,128)(2,1)} fusion(bf16[2,512,512]{2,1,0:T(8,128)(2,1)S(1)} %copy-done.1, bf16[2,1024,512]{2,1,0:T(8,128)(2,1)S(1)} %get-tuple-element.10, bf16[2,1024,512]{2,1,0:T(8,128)(2,1)S(1)} %get-tuple-element.9), kind=kLoop, calls=%fused_computation.2 | loop fusion | flops 25165824 | bytes 11534336 | tf_op jit(solution)/shard_map/concatenate | solution.py:106
  26.2 0.0 copy-start.3
  26.2 2.3 %all-to-all-done.rows_ref = bf16[16,64,512]{2,1,0:T(8,128)(2,1)S(1)} async-done(((bf16[16,64,512]{2,1,0:T(8,128)(2,1)}), bf16[16,64,512]{2,1,0:T(8,128)(2,1)S(1)}, u32[]{:S(2)}, u32[]{:S(2)}) %all-to-all-start) | async-done | bytes 1048608 | tf_op jit(solution)/shard_map/all_to_all | solution.py:196
  28.5 0.0 copy-done
  28.5 0.0 copy-start.2
  28.5 17.2 %shard_map.65 = bf16[16,64,512]{2,1,0:T(8,128)(2,1)S(1)} custom-call(bf16[16,64,512]{2,1,0:T(8,128)(2,1)S(1)} %all-to-all-done.rows_ref, bf16[2,512,1024]{2,1,0:T(8,128)(2,1)S(1)} %copy-done, bf16[2,1536,1024]{2,1,0:T(8,128)(2,1)} %fusion.1.tables_hbm), custom_call_target="tpu_custom_call" | custom-call | flops 7516192768 | bytes 9437184 | tf_op jit(solution)/shard_map/pallas_call | solution.py:128
  45.8 21.3 %all_to_all.10 = bf16[16,64,512]{2,1,0:T(8,128)(2,1)S(1)} all-to-all(bf16[16,64,512]{2,1,0:T(8,128)(2,1)S(1)} %shard_map.65), channel_id=1, replica_groups=mesh['user'=16,'cand'=8] {'user'}, dimensions={0} | all-to-all | bytes 2097152 | tf_op jit(solution)/shard_map/all_to_all | solution.py:199
  67.1 0.0 copy-done.3
  67.1 0.0 copy-done.2
  67.1 1.7 %fusion.3 = f32[512,512]{1,0:T(8,128)} fusion(bf16[1024,512]{1,0:T(8,128)(2,1)S(1)} %bitcast.10, s32[512]{0:T(512)S(1)} %bitcast.12, bf16[512,512]{1,0:T(8,128)(2,1)S(1)} %copy-done.2), kind=kOutput, calls=%fused_computation.6 | convolution fusion | flops 537919488 | bytes 2623488 | tf_op jit(solution)/shard_map/dot_general | solution.py:200
  (1 shorter events, 0.0 us)
Async XLA Ops:
  2.9 25.6 %all-to-all-start = ((bf16[16,64,512]{2,1,0:T(8,128)(2,1)}), bf16[16,64,512]{2,1,0:T(8,128)(2,1)S(1)}, u32[]{:S(2)}, u32[]{:S(2)}) async-start(bf16[16,64,512]{2,1,0:T(8,128)(2,1)} %bitcast.9), calls=%async_computation | async-start | bytes 2097152 | tf_op jit(solution)/shard_map/all_to_all | solution.py:196
  10.9 3.4 %copy-start.1 = (bf16[2,512,512]{2,1,0:T(8,128)(2,1)S(1)}, bf16[2,512,512]{2,1,0:T(8,128)(2,1)}, u32[]{:S(2)}) copy-start(bf16[2,512,512]{2,1,0:T(8,128)(2,1)} %param.11) | copy-start | bytes 3145732
  14.3 14.2 %copy-start = (bf16[2,512,1024]{2,1,0:T(8,128)(2,1)S(1)}, bf16[2,512,1024]{2,1,0:T(8,128)(2,1)}, u32[]{:S(2)}) copy-start(bf16[2,512,1024]{2,1,0:T(8,128)(2,1)} %w_in_ref.1) | copy-start | bytes 6291460
  26.2 40.9 %copy-start.3 = (s32[1,512]{1,0:T(1,128)S(1)}, s32[1,512]{1,0:T(1,128)}, u32[]{:S(2)}) copy-start(s32[1,512]{1,0:T(1,128)} %get-tuple-element.7) | copy-start | bytes 6148
  28.5 38.5 %copy-start.2 = (bf16[512,512]{1,0:T(8,128)(2,1)S(1)}, bf16[512,512]{1,0:T(8,128)(2,1)}, u32[]{:S(2)}) copy-start(bf16[512,512]{1,0:T(8,128)(2,1)} %emb_ref.1) | copy-start | bytes 1572868

commit v9 on v8

--- a/solution.py
+++ b/solution.py
@@ -27,7 +27,7 @@
     sources, slots, features = rows_ref.shape
     block_rows = sources * slots
     layer_count = w_in_ref.shape[0]
-    history_span = tables_ref.shape[1] - features
+    history_span = (tables_ref.shape[1] - features) // 2
     head_dim = features // HEADS
     factor = head_dim ** (-0.5)
     step = pl.program_id(0)
@@ -69,6 +69,9 @@
                 low = head * head_dim
                 query = projected[:, features + low:features + low + head_dim]
                 keys = tables_ref[layer_index, :history_span, low:low + head_dim]
+                values = tables_ref[
+                    layer_index, history_span:2 * history_span, low:low + head_dim
+                ]
                 scores = lax.dot_general(
                     query, keys, (((1,), (1,)), ((), ())), preferred_element_type=jnp.float32
                 )
@@ -76,9 +79,7 @@
                 heads.append(
                     jnp.dot(
                         weight,
-                        tables_ref[
-                            layer_index, :history_span, features + low:features + low + head_dim
-                        ],
+                        values,
                         preferred_element_type=jnp.float32,
                     )
                 )
@@ -86,7 +87,7 @@
             branch = (layer_normed(attended) * gate).astype(jnp.bfloat16)
             residual = residual + jnp.dot(
                 branch,
-                tables_ref[layer_index, history_span:, :features],
+                tables_ref[layer_index, 2 * history_span:, :],
                 preferred_element_type=jnp.float32,
             )
         out_ref[...] = (residual - start).reshape(sources, slots, features).astype(out_ref.dtype)
@@ -100,11 +101,9 @@
         [
             history[:, :, :features],
             jnp.where(in_history, history[:, :, features:], jnp.zeros((), history.dtype)),
+            w_out,
         ],
-        axis=2,
-    )
-    tables = jnp.concatenate(
-        [tables, jnp.pad(w_out, ((0, 0), (0, 0), (0, width - features)))], axis=1
+        axis=1,
     )
     steps = capacity // SLOT_BLOCK
     grid_spec = pltpu.PrefetchScalarGridSpec(

time: 69 us -> 66.8 us (0.968)
  waiting for transfers between devices: 2.33 us -> 4.92 us
  other arithmetic: 14.5 us -> 12 us
  blocking collectives: 21.3 us -> 19.5 us
    all_to_all x1, waiting for transfers between devices: 2.33 us -> 4.92 us  [local(): lax.all_to_all(outgoing, 'user', split_axis=0, concat_axis=0, tiled=True)]
    concatenate x1, other arithmetic: 11.9 us -> 9.3 us  [run_layers(): jnp.concatenate([history[:, :, :features], jnp.where(in_history, history[...]
    all_to_all x1, blocking collectives: 21.3 us -> 19.5 us  [local(): lax.all_to_all(delta, 'user', split_axis=0, concat_axis=0, tiled=True)]
  transfers between devices with their start and end apart: 1 -> 1, of which waited for: 1 -> 1; matrix products, arithmetic and copies ran while one was open for 21% -> 18% of each run, Pallas kernels for 0% -> 0%
where the time goes in v9:
time: 66.8 us; the launch traced here: 66.6 us
  Pallas kernels  19.7 us (29%)
  blocking collectives  19.5 us (29%)
  other arithmetic  12 us (18%)
  starting transfers between devices  7.96 us (12%)
  waiting for transfers between devices  4.92 us (7%)
  matrix products  1.73 us (3%)
  between operations  0.71 us (1%)
    all_to_all x1, blocking collectives, local(): lax.all_to_all(delta, 'user', split_axis=0, concat_axis=0, tiled=True)  19.5 us
    pallas_call x1, Pallas kernels, run_layers(): pl.pallas_call(layers_kernel, grid_spec=grid_spec, out_shape=jax.ShapeDty...  16.8 us
    concatenate x1, other arithmetic, run_layers(): jnp.concatenate([history[:, :, :features], jnp.where(in_history, history[...  9.3 us
    all_to_all x1, starting transfers between devices, local(): lax.all_to_all(outgoing, 'user', split_axis=0, concat_axis=0, tiled=True)  7.96 us
    all_to_all x1, waiting for transfers between devices, local(): lax.all_to_all(outgoing, 'user', split_axis=0, concat_axis=0, tiled=True)  4.92 us
    pallas_call x1, Pallas kernels, pack_rows(): pl.pallas_call(functools.partial(pack_kernel, group_size=group_size, user...  2.92 us
    slice x1, other arithmetic, run_layers(): history[:, :, :features]  2.71 us
    dot_general x1, matrix products, local(): lax.dot_general(placing, returned.reshape(-1, features), (((0,), (0,)), (...  1.73 us
  transfers between devices with their start and end apart: 1, of which 1 were waited for; matrix products, arithmetic and copies ran while one was open for 18% of the time, Pallas kernels for 0%

profile of v9, /device:TPU:0, one launch (start us, length us, event | category | flops | bytes accessed | tf_op | source)
XLA Modules:
  0.0 66.6 jit_solution(11386256151086364896)
XLA Ops:
  0.0 2.9 %shard_map.64 = (bf16[1024,512]{1,0:T(8,128)(2,1)}, s32[1,512]{1,0:T(1,128)}) custom-call(s32[1,512]{1,0:T(1,128)} %bitcast.11, bf16[512,512]{1,0:T(8,128)(2,1)} %emb_ref.1), custom_call_target="tpu_custom_call" | custom-call | flops 545259520 | bytes 1572864 | tf_op jit(solution)/shard_map/pallas_call | solution.py:168
  2.9 8.0 %all-to-all-start = ((bf16[16,64,512]{2,1,0:T(8,128)(2,1)}), bf16[16,64,512]{2,1,0:T(8,128)(2,1)S(1)}, u32[]{:S(2)}, u32[]{:S(2)}) async-start(bf16[16,64,512]{2,1,0:T(8,128)(2,1)} %bitcast.9), calls=%async_computation | async-start | bytes 2097152 | tf_op jit(solution)/shard_map/all_to_all | solution.py:195
  11.6 0.0 copy-start.1
  11.6 2.7 %fusion.3 = (bf16[2,1024,512]{2,1,0:T(8,128)(2,1)S(1)}, bf16[2,1024,512]{2,1,0:T(8,128)(2,1)S(1)}) fusion(bf16[2,1024,1024]{2,1,0:T(8,128)(2,1)} %bitcast.8, pred[1024]{0:T(1024)(128)(4,1)S(1)} %iota_compare_fusion.4), kind=kLoop, calls=%fused_computation.7 | loop fusion | flops 1048576 | bytes 8389632 | tf_op jit(solution)/shard_map/slice | solution.py:102
  14.3 0.0 copy-done.1
  14.3 0.0 copy-start
  14.3 9.3 %pad_maximum_fusion.tables_hbm = bf16[2,2560,512]{2,1,0:T(8,128)(2,1)} fusion(bf16[2,512,512]{2,1,0:T(8,128)(2,1)S(1)} %copy-done.1, bf16[2,1024,512]{2,1,0:T(8,128)(2,1)S(1)} %get-tuple-element.10, bf16[2,1024,512]{2,1,0:T(8,128)(2,1)S(1)} %get-tuple-element.9), kind=kLoop, calls=%fused_computation | loop fusion | flops 15728640 | bytes 10485760 | tf_op jit(solution)/shard_map/concatenate | solution.py:100
  23.6 0.0 copy-start.3
  23.6 4.9 %all-to-all-done.rows_ref = bf16[16,64,512]{2,1,0:T(8,128)(2,1)S(1)} async-done(((bf16[16,64,512]{2,1,0:T(8,128)(2,1)}), bf16[16,64,512]{2,1,0:T(8,128)(2,1)S(1)}, u32[]{:S(2)}, u32[]{:S(2)}) %all-to-all-start) | async-done | bytes 1048608 | tf_op jit(solution)/shard_map/all_to_all | solution.py:195
  28.5 0.0 copy-done
  28.5 0.0 copy-start.2
  28.5 16.8 %shard_map.65 = bf16[16,64,512]{2,1,0:T(8,128)(2,1)S(1)} custom-call(bf16[16,64,512]{2,1,0:T(8,128)(2,1)S(1)} %all-to-all-done.rows_ref, bf16[2,512,1024]{2,1,0:T(8,128)(2,1)S(1)} %copy-done, bf16[2,2560,512]{2,1,0:T(8,128)(2,1)} %pad_maximum_fusion.tables_hbm), custom_call_target="tpu_custom_call" | custom-call | flops 7516192768 | bytes 9437184 | tf_op jit(solution)/shard_map/pallas_call | solution.py:127
  45.3 19.5 %all_to_all.10 = bf16[16,64,512]{2,1,0:T(8,128)(2,1)S(1)} all-to-all(bf16[16,64,512]{2,1,0:T(8,128)(2,1)S(1)} %shard_map.65), channel_id=1, replica_groups=mesh['user'=16,'cand'=8] {'user'}, dimensions={0} | all-to-all | bytes 2097152 | tf_op jit(solution)/shard_map/all_to_all | solution.py:198
  64.8 0.0 copy-done.3
  64.8 0.0 copy-done.2
  64.8 1.7 %fusion.1 = f32[512,512]{1,0:T(8,128)} fusion(bf16[1024,512]{1,0:T(8,128)(2,1)S(1)} %bitcast.10, s32[512]{0:T(512)S(1)} %bitcast.12, bf16[512,512]{1,0:T(8,128)(2,1)S(1)} %copy-done.2), kind=kOutput, calls=%fused_computation.4 | convolution fusion | flops 537919488 | bytes 2623488 | tf_op jit(solution)/shard_map/dot_general | solution.py:199
  (1 shorter events, 0.0 us)
Async XLA Ops:
  2.9 25.6 %all-to-all-start = ((bf16[16,64,512]{2,1,0:T(8,128)(2,1)}), bf16[16,64,512]{2,1,0:T(8,128)(2,1)S(1)}, u32[]{:S(2)}, u32[]{:S(2)}) async-start(bf16[16,64,512]{2,1,0:T(8,128)(2,1)} %bitcast.9), calls=%async_computation | async-start | bytes 2097152 | tf_op jit(solution)/shard_map/all_to_all | solution.py:195
  11.6 2.7 %copy-start.1 = (bf16[2,512,512]{2,1,0:T(8,128)(2,1)S(1)}, bf16[2,512,512]{2,1,0:T(8,128)(2,1)}, u32[]{:S(2)}) copy-start(bf16[2,512,512]{2,1,0:T(8,128)(2,1)} %param.11) | copy-start | bytes 3145732
  14.3 14.2 %copy-start = (bf16[2,512,1024]{2,1,0:T(8,128)(2,1)S(1)}, bf16[2,512,1024]{2,1,0:T(8,128)(2,1)}, u32[]{:S(2)}) copy-start(bf16[2,512,1024]{2,1,0:T(8,128)(2,1)} %w_in_ref.1) | copy-start | bytes 6291460
  23.6 41.2 %copy-start.3 = (s32[1,512]{1,0:T(1,128)S(1)}, s32[1,512]{1,0:T(1,128)}, u32[]{:S(2)}) copy-start(s32[1,512]{1,0:T(1,128)} %get-tuple-element.7) | copy-start | bytes 6148
  28.5 36.3 %copy-start.2 = (bf16[512,512]{1,0:T(8,128)(2,1)S(1)}, bf16[512,512]{1,0:T(8,128)(2,1)}, u32[]{:S(2)}) copy-start(bf16[512,512]{1,0:T(8,128)(2,1)} %emb_ref.1) | copy-start | bytes 1572868

commit v10 on v9

--- a/solution.py
+++ b/solution.py
@@ -141,7 +141,8 @@
 
 def pack_kernel(route_ref, emb_ref, packed_ref, position_ref, *, group_size, user_count):
     cand_rows = emb_ref.shape[0]
-    capacity = packed_ref.shape[0] // user_count
+    block_slots = packed_ref.shape[0]
+    capacity = 2 * cand_rows // user_count
     owner = route_ref[...] // group_size
     member = (lax.broadcasted_iota(jnp.int32, (user_count, cand_rows), 0) == owner).astype(
         jnp.float32
@@ -154,8 +155,9 @@
     ranking = jnp.sum(member * before, axis=0, keepdims=True).astype(jnp.int32)
     position = owner * capacity + ranking
     position_ref[...] = position
+    first = pl.program_id(0) * block_slots
     placing = (
-        lax.broadcasted_iota(jnp.int32, (packed_ref.shape[0], cand_rows), 0) == position
+        lax.broadcasted_iota(jnp.int32, (block_slots, cand_rows), 0) + first == position
     ).astype(jnp.bfloat16)
     packed_ref[...] = jnp.dot(
         placing, emb_ref[...], preferred_element_type=jnp.float32
@@ -165,16 +167,25 @@
 def pack_rows(cand_emb, cand_route, user_count, group_size):
     cand_rows, features = cand_emb.shape
     slots = 2 * cand_rows
+    block_slots = slots // 4
     return pl.pallas_call(
         functools.partial(pack_kernel, group_size=group_size, user_count=user_count),
+        grid=(slots // block_slots,),
         out_shape=(
             jax.ShapeDtypeStruct((slots, features), jnp.bfloat16),
             jax.ShapeDtypeStruct((1, cand_rows), jnp.int32),
         ),
-        in_specs=[pl.BlockSpec(memory_space=pltpu.VMEM)] * 2,
-        out_specs=(pl.BlockSpec(memory_space=pltpu.VMEM),) * 2,
+        in_specs=[
+            pl.BlockSpec((1, cand_rows), lambda i: (0, 0)),
+            pl.BlockSpec((cand_rows, features), lambda i: (0, 0)),
+        ],
+        out_specs=(
+            pl.BlockSpec((block_slots, features), lambda i: (i, 0)),
+            pl.BlockSpec((1, cand_rows), lambda i: (0, 0)),
+        ),
+        compiler_params=pltpu.CompilerParams(dimension_semantics=("arbitrary",)),
         cost_estimate=pl.CostEstimate(
-            flops=2 * slots * cand_rows * features + 2 * user_count * cand_rows * cand_rows,
+            flops=2 * slots * cand_rows * features + 8 * user_count * cand_rows * cand_rows,
             transcendentals=0,
             bytes_accessed=2 * (cand_emb.size + slots * features),
         ),

time: 66.8 us -> 67.8 us (1.015)
  Pallas kernels: 19.7 us -> 20.7 us
    pallas_call x1, Pallas kernels: 2.92 us -> 3.93 us  [pack_rows(): pl.pallas_call(functools.partial(pack_kernel, group_size=group_size, user...]
where the time goes in v10:
time: 67.8 us; the launch traced here: 67.6 us
  Pallas kernels  20.7 us (31%)
  blocking collectives  19.5 us (29%)
  other arithmetic  12 us (18%)
  starting transfers between devices  7.96 us (12%)
  waiting for transfers between devices  4.93 us (7%)
  matrix products  1.73 us (3%)
  between operations  0.71 us (1%)
    all_to_all x1, blocking collectives, local(): lax.all_to_all(delta, 'user', split_axis=0, concat_axis=0, tiled=True)  19.5 us
    pallas_call x1, Pallas kernels, run_layers(): pl.pallas_call(layers_kernel, grid_spec=grid_spec, out_shape=jax.ShapeDty...  16.8 us
    concatenate x1, other arithmetic, run_layers(): jnp.concatenate([history[:, :, :features], jnp.where(in_history, history[...  9.3 us
    all_to_all x1, starting transfers between devices, local(): lax.all_to_all(outgoing, 'user', split_axis=0, concat_axis=0, tiled=True)  7.96 us
    all_to_all x1, waiting for transfers between devices, local(): lax.all_to_all(outgoing, 'user', split_axis=0, concat_axis=0, tiled=True)  4.93 us
    pallas_call x1, Pallas kernels, pack_rows(): pl.pallas_call(functools.partial(pack_kernel, group_size=group_size, user...  3.93 us
    slice x1, other arithmetic, run_layers(): history[:, :, :features]  2.71 us
    dot_general x1, matrix products, local(): lax.dot_general(placing, returned.reshape(-1, features), (((0,), (0,)), (...  1.73 us
  transfers between devices with their start and end apart: 1, of which 1 were waited for; matrix products, arithmetic and copies ran while one was open for 18% of the time, Pallas kernels for 0%

profile of v10, /device:TPU:0, one launch (start us, length us, event | category | flops | bytes accessed | tf_op | source)
XLA Modules:
  0.0 67.6 jit_solution(6160744701376179768)
XLA Ops:
  0.0 3.9 %shard_map.64 = (bf16[1024,512]{1,0:T(8,128)(2,1)}, s32[1,512]{1,0:T(1,128)}) custom-call(s32[1,512]{1,0:T(1,128)} %bitcast.11, bf16[512,512]{1,0:T(8,128)(2,1)} %emb_ref.1), custom_call_target="tpu_custom_call" | custom-call | flops 570425344 | bytes 1572864 | tf_op jit(solution)/shard_map/pallas_call | solution.py:171
  3.9 8.0 %all-to-all-start = ((bf16[16,64,512]{2,1,0:T(8,128)(2,1)}), bf16[16,64,512]{2,1,0:T(8,128)(2,1)S(1)}, u32[]{:S(2)}, u32[]{:S(2)}) async-start(bf16[16,64,512]{2,1,0:T(8,128)(2,1)} %bitcast.9), calls=%async_computation | async-start | bytes 2097152 | tf_op jit(solution)/shard_map/all_to_all | solution.py:206
  12.6 0.0 copy-start.1
  12.6 2.7 %fusion.3 = (bf16[2,1024,512]{2,1,0:T(8,128)(2,1)S(1)}, bf16[2,1024,512]{2,1,0:T(8,128)(2,1)S(1)}) fusion(bf16[2,1024,1024]{2,1,0:T(8,128)(2,1)} %bitcast.8, pred[1024]{0:T(1024)(128)(4,1)S(1)} %iota_compare_fusion.4), kind=kLoop, calls=%fused_computation.7 | loop fusion | flops 1048576 | bytes 8389632 | tf_op jit(solution)/shard_map/slice | solution.py:102
  15.3 0.0 copy-done.1
  15.3 0.0 copy-start
  15.3 9.3 %pad_maximum_fusion.tables_hbm = bf16[2,2560,512]{2,1,0:T(8,128)(2,1)} fusion(bf16[2,512,512]{2,1,0:T(8,128)(2,1)S(1)} %copy-done.1, bf16[2,1024,512]{2,1,0:T(8,128)(2,1)S(1)} %get-tuple-element.10, bf16[2,1024,512]{2,1,0:T(8,128)(2,1)S(1)} %get-tuple-element.9), kind=kLoop, calls=%fused_computation | loop fusion | flops 15728640 | bytes 10485760 | tf_op jit(solution)/shard_map/concatenate | solution.py:100
  24.6 0.0 copy-start.3
  24.6 4.9 %all-to-all-done.rows_ref = bf16[16,64,512]{2,1,0:T(8,128)(2,1)S(1)} async-done(((bf16[16,64,512]{2,1,0:T(8,128)(2,1)}), bf16[16,64,512]{2,1,0:T(8,128)(2,1)S(1)}, u32[]{:S(2)}, u32[]{:S(2)}) %all-to-all-start) | async-done | bytes 1048608 | tf_op jit(solution)/shard_map/all_to_all | solution.py:206
  29.5 0.0 copy-done
  29.5 0.0 copy-start.2
  29.5 16.8 %shard_map.65 = bf16[16,64,512]{2,1,0:T(8,128)(2,1)S(1)} custom-call(bf16[16,64,512]{2,1,0:T(8,128)(2,1)S(1)} %all-to-all-done.rows_ref, bf16[2,512,1024]{2,1,0:T(8,128)(2,1)S(1)} %copy-done, bf16[2,2560,512]{2,1,0:T(8,128)(2,1)} %pad_maximum_fusion.tables_hbm), custom_call_target="tpu_custom_call" | custom-call | flops 7516192768 | bytes 9437184 | tf_op jit(solution)/shard_map/pallas_call | solution.py:127
  46.4 19.5 %all_to_all.10 = bf16[16,64,512]{2,1,0:T(8,128)(2,1)S(1)} all-to-all(bf16[16,64,512]{2,1,0:T(8,128)(2,1)S(1)} %shard_map.65), channel_id=1, replica_groups=mesh['user'=16,'cand'=8] {'user'}, dimensions={0} | all-to-all | bytes 2097152 | tf_op jit(solution)/shard_map/all_to_all | solution.py:209
  65.8 0.0 copy-done.3
  65.8 0.0 copy-done.2
  65.8 1.7 %fusion.1 = f32[512,512]{1,0:T(8,128)} fusion(bf16[1024,512]{1,0:T(8,128)(2,1)S(1)} %bitcast.10, s32[512]{0:T(512)S(1)} %bitcast.12, bf16[512,512]{1,0:T(8,128)(2,1)S(1)} %copy-done.2), kind=kOutput, calls=%fused_computation.4 | convolution fusion | flops 537919488 | bytes 2623488 | tf_op jit(solution)/shard_map/dot_general | solution.py:210
  (1 shorter events, 0.0 us)
Async XLA Ops:
  3.9 25.6 %all-to-all-start = ((bf16[16,64,512]{2,1,0:T(8,128)(2,1)}), bf16[16,64,512]{2,1,0:T(8,128)(2,1)S(1)}, u32[]{:S(2)}, u32[]{:S(2)}) async-start(bf16[16,64,512]{2,1,0:T(8,128)(2,1)} %bitcast.9), calls=%async_computation | async-start | bytes 2097152 | tf_op jit(solution)/shard_map/all_to_all | solution.py:206
  12.6 2.7 %copy-start.1 = (bf16[2,512,512]{2,1,0:T(8,128)(2,1)S(1)}, bf16[2,512,512]{2,1,0:T(8,128)(2,1)}, u32[]{:S(2)}) copy-start(bf16[2,512,512]{2,1,0:T(8,128)(2,1)} %param.11) | copy-start | bytes 3145732
  15.3 14.2 %copy-start = (bf16[2,512,1024]{2,1,0:T(8,128)(2,1)S(1)}, bf16[2,512,1024]{2,1,0:T(8,128)(2,1)}, u32[]{:S(2)}) copy-start(bf16[2,512,1024]{2,1,0:T(8,128)(2,1)} %w_in_ref.1) | copy-start | bytes 6291460
  24.6 41.2 %copy-start.3 = (s32[1,512]{1,0:T(1,128)S(1)}, s32[1,512]{1,0:T(1,128)}, u32[]{:S(2)}) copy-start(s32[1,512]{1,0:T(1,128)} %get-tuple-element.7) | copy-start | bytes 6148
  29.5 36.3 %copy-start.2 = (bf16[512,512]{1,0:T(8,128)(2,1)S(1)}, bf16[512,512]{1,0:T(8,128)(2,1)}, u32[]{:S(2)}) copy-start(bf16[512,512]{1,0:T(8,128)(2,1)} %emb_ref.1) | copy-start | bytes 1572868

commit v11 on v9

--- a/solution.py
+++ b/solution.py
@@ -23,28 +23,39 @@
     return center * lax.rsqrt(spread + epsilon)
 
 
-def layers_kernel(rows_ref, w_in_ref, tables_hbm, out_ref, tables_ref, copy_sems):
+def layers_kernel(
+    rows_ref, w_in_ref, hist_hbm, tables_hbm, out_ref, keys_ref, tables_ref, copy_sems
+):
     sources, slots, features = rows_ref.shape
     block_rows = sources * slots
     layer_count = w_in_ref.shape[0]
-    history_span = (tables_ref.shape[1] - features) // 2
+    history_span = keys_ref.shape[1]
     head_dim = features // HEADS
     factor = head_dim ** (-0.5)
     step = pl.program_id(0)
     copies = [
-        pltpu.make_async_copy(tables_hbm.at[layer], tables_ref.at[layer], copy_sems.at[layer])
+        (
+            pltpu.make_async_copy(
+                hist_hbm.at[layer, :, :features], keys_ref.at[layer], copy_sems.at[0, layer]
+            ),
+            pltpu.make_async_copy(
+                tables_hbm.at[layer], tables_ref.at[layer], copy_sems.at[1, layer]
+            ),
+        )
         for layer in range(layer_count)
     ]
 
     @pl.when(step == 0)
     def _():
-        for copy in copies:
-            copy.start()
+        for pair in copies:
+            for copy in pair:
+                copy.start()
 
     def arrive(index):
         @pl.when(step == 0)
         def _():
-            copies[index].wait()
+            for copy in copies[index]:
+                copy.wait()
 
     busy = jnp.max(jnp.abs(rows_ref[...].astype(jnp.float32))) > 0
 
@@ -68,10 +79,8 @@
             for head in range(HEADS):
                 low = head * head_dim
                 query = projected[:, features + low:features + low + head_dim]
-                keys = tables_ref[layer_index, :history_span, low:low + head_dim]
-                values = tables_ref[
-                    layer_index, history_span:2 * history_span, low:low + head_dim
-                ]
+                keys = keys_ref[layer_index, :, low:low + head_dim]
+                values = tables_ref[layer_index, :history_span, low:low + head_dim]
                 scores = lax.dot_general(
                     query, keys, (((1,), (1,)), ((), ())), preferred_element_type=jnp.float32
                 )
@@ -87,7 +96,7 @@
             branch = (layer_normed(attended) * gate).astype(jnp.bfloat16)
             residual = residual + jnp.dot(
                 branch,
-                tables_ref[layer_index, 2 * history_span:, :],
+                tables_ref[layer_index, history_span:, :],
                 preferred_element_type=jnp.float32,
             )
         out_ref[...] = (residual - start).reshape(sources, slots, features).astype(out_ref.dtype)
@@ -99,7 +108,6 @@
     in_history = lax.broadcasted_iota(jnp.int32, (1, history_span, 1), 1) < length[0]
     tables = jnp.concatenate(
         [
-            history[:, :, :features],
             jnp.where(in_history, history[:, :, features:], jnp.zeros((), history.dtype)),
             w_out,
         ],
@@ -113,11 +121,13 @@
             pl.BlockSpec((sources, SLOT_BLOCK, features), lambda i: (0, i, 0)),
             pl.BlockSpec(w_in.shape, lambda i: (0, 0, 0)),
             pl.BlockSpec(memory_space=pltpu.MemorySpace.HBM),
+            pl.BlockSpec(memory_space=pltpu.MemorySpace.HBM),
         ],
         out_specs=pl.BlockSpec((sources, SLOT_BLOCK, features), lambda i: (0, i, 0)),
         scratch_shapes=[
+            pltpu.VMEM((layer_count, history_span, features), history.dtype),
             pltpu.VMEM(tables.shape, tables.dtype),
-            pltpu.SemaphoreType.DMA((layer_count,)),
+            pltpu.SemaphoreType.DMA((2, layer_count)),
         ],
     )
     row_count = sources * capacity
@@ -136,7 +146,7 @@
             transcendentals=row_count * layer_count * (HEADS * history_span + 2 * features),
             bytes_accessed=2 * (history.size + w_in.size + w_out.size + 2 * buckets.size),
         ),
-    )(buckets, w_in, tables)
+    )(buckets, w_in, history, tables)
 
 
 def pack_kernel(route_ref, emb_ref, packed_ref, position_ref, *, group_size, user_count):

time: 66.8 us -> 66.9 us (level)
  other arithmetic: 12 us -> 3.67 us
  waiting for transfers between devices: 4.92 us -> 13.2 us
    all_to_all x1, waiting for transfers between devices: 4.92 us -> 13.2 us  [local(): lax.all_to_all(outgoing, 'user', split_axis=0, concat_axis=0, tiled=True)]
    concatenate x1, other arithmetic: 9.3 us -> 1.85 us  [run_layers(): jnp.concatenate([jnp.where(in_history, history[:, :, features:], jnp.zero...]
    slice x1 -> x0, other arithmetic: 2.71 us -> none  [run_layers(): history[:, :, :features]]
    select_n x0 -> x1, other arithmetic: none -> 1.81 us  [run_layers(): jnp.where(in_history, history[:, :, features:], jnp.zeros((), history.dty...]
  transfers between devices with their start and end apart: 1 -> 1, of which waited for: 1 -> 1; matrix products, arithmetic and copies ran while one was open for 18% -> 6% of each run, Pallas kernels for 0% -> 0%
where the time goes in v11:
time: 66.9 us; the launch traced here: 66.6 us
  Pallas kernels  19.7 us (29%)
  blocking collectives  19.5 us (29%)
  waiting for transfers between devices  13.2 us (20%)
  starting transfers between devices  7.96 us (12%)
  other arithmetic  3.67 us (5%)
  matrix products  1.73 us (3%)
  between operations  0.8 us (1%)
    all_to_all x1, blocking collectives, local(): lax.all_to_all(delta, 'user', split_axis=0, concat_axis=0, tiled=True)  19.5 us
    pallas_call x1, Pallas kernels, run_layers(): pl.pallas_call(layers_kernel, grid_spec=grid_spec, out_shape=jax.ShapeDty...  16.8 us
    all_to_all x1, waiting for transfers between devices, local(): lax.all_to_all(outgoing, 'user', split_axis=0, concat_axis=0, tiled=True)  13.2 us
    all_to_all x1, starting transfers between devices, local(): lax.all_to_all(outgoing, 'user', split_axis=0, concat_axis=0, tiled=True)  7.96 us
    pallas_call x1, Pallas kernels, pack_rows(): pl.pallas_call(functools.partial(pack_kernel, group_size=group_size, user...  2.92 us
    concatenate x1, other arithmetic, run_layers(): jnp.concatenate([jnp.where(in_history, history[:, :, features:], jnp.zero...  1.85 us
    select_n x1, other arithmetic, run_layers(): jnp.where(in_history, history[:, :, features:], jnp.zeros((), history.dty...  1.81 us
    dot_general x1, matrix products, local(): lax.dot_general(placing, returned.reshape(-1, features), (((0,), (0,)), (...  1.73 us
  transfers between devices with their start and end apart: 1, of which 1 were waited for; matrix products, arithmetic and copies ran while one was open for 6% of the time, Pallas kernels for 0%

profile of v11, /device:TPU:0, one launch (start us, length us, event | category | flops | bytes accessed | tf_op | source)
XLA Modules:
  0.0 66.6 jit_solution(741236556674416218)
XLA Ops:
  0.0 2.9 %shard_map.64 = (bf16[1024,512]{1,0:T(8,128)(2,1)}, s32[1,512]{1,0:T(1,128)}) custom-call(s32[1,512]{1,0:T(1,128)} %bitcast.12, bf16[512,512]{1,0:T(8,128)(2,1)} %emb_ref.1), custom_call_target="tpu_custom_call" | custom-call | flops 545259520 | bytes 1572864 | tf_op jit(solution)/shard_map/pallas_call | solution.py:178
  2.9 8.0 %all-to-all-start = ((bf16[16,64,512]{2,1,0:T(8,128)(2,1)}), bf16[16,64,512]{2,1,0:T(8,128)(2,1)S(1)}, u32[]{:S(2)}, u32[]{:S(2)}) async-start(bf16[16,64,512]{2,1,0:T(8,128)(2,1)} %bitcast.10), calls=%async_computation | async-start | bytes 2097152 | tf_op jit(solution)/shard_map/all_to_all | solution.py:205
  10.9 0.0 copy-start.1
  11.7 1.8 %slice_select_fusion = bf16[2,1024,512]{2,1,0:T(8,128)(2,1)S(1)} fusion(bf16[2,1024,1024]{2,1,0:T(8,128)(2,1)} %bitcast.8, pred[1024]{0:T(1024)(128)(4,1)S(1)} %iota_compare_fusion.4), kind=kLoop, calls=%fused_computation.1 | loop fusion | flops 1048576 | bytes 4195328 | tf_op jit(solution)/shard_map/jit(_where)/select_n | solution.py:111
  13.5 0.0 copy-done.1
  13.5 0.0 copy-start
  13.5 1.9 %pad_maximum_fusion.tables_hbm = bf16[2,1536,512]{2,1,0:T(8,128)(2,1)} fusion(bf16[2,512,512]{2,1,0:T(8,128)(2,1)S(1)} %copy-done.1, bf16[2,1024,512]{2,1,0:T(8,128)(2,1)S(1)} %slice_select_fusion), kind=kLoop, calls=%fused_computation | loop fusion | flops 6291456 | bytes 6291456 | tf_op jit(solution)/shard_map/concatenate | solution.py:109
  15.3 0.0 copy-start.3
  15.4 13.2 %all-to-all-done.rows_ref = bf16[16,64,512]{2,1,0:T(8,128)(2,1)S(1)} async-done(((bf16[16,64,512]{2,1,0:T(8,128)(2,1)}), bf16[16,64,512]{2,1,0:T(8,128)(2,1)S(1)}, u32[]{:S(2)}, u32[]{:S(2)}) %all-to-all-start) | async-done | bytes 1048608 | tf_op jit(solution)/shard_map/all_to_all | solution.py:205
  28.5 0.0 copy-done
  28.5 0.0 copy-start.2
  28.5 16.8 %shard_map.65 = bf16[16,64,512]{2,1,0:T(8,128)(2,1)S(1)} custom-call(bf16[16,64,512]{2,1,0:T(8,128)(2,1)S(1)} %all-to-all-done.rows_ref, bf16[2,512,1024]{2,1,0:T(8,128)(2,1)S(1)} %copy-done, bf16[2,1024,1024]{2,1,0:T(8,128)(2,1)} %bitcast.9, bf16[2,1536,512]{2,1,0:T(8,128)(2,1)} %pad_maximum_fusion.tables_hbm), custom_call_target="tpu_custom_call" | custom-call | flops 7516192768 | bytes 9437184 | tf_op jit(solution)/shard_map/pallas_call | solution.py:137
  45.4 19.5 %all_to_all.10 = bf16[16,64,512]{2,1,0:T(8,128)(2,1)S(1)} all-to-all(bf16[16,64,512]{2,1,0:T(8,128)(2,1)S(1)} %shard_map.65), channel_id=1, replica_groups=mesh['user'=16,'cand'=8] {'user'}, dimensions={0} | all-to-all | bytes 2097152 | tf_op jit(solution)/shard_map/all_to_all | solution.py:208
  64.8 0.0 copy-done.3
  64.8 0.0 copy-done.2
  64.8 1.7 %fusion.1 = f32[512,512]{1,0:T(8,128)} fusion(bf16[1024,512]{1,0:T(8,128)(2,1)S(1)} %bitcast.11, s32[512]{0:T(512)S(1)} %bitcast.13, bf16[512,512]{1,0:T(8,128)(2,1)S(1)} %copy-done.2), kind=kOutput, calls=%fused_computation.4 | convolution fusion | flops 537919488 | bytes 2623488 | tf_op jit(solution)/shard_map/dot_general | solution.py:209
  (1 shorter events, 0.0 us)
Async XLA Ops:
  2.9 25.6 %all-to-all-start = ((bf16[16,64,512]{2,1,0:T(8,128)(2,1)}), bf16[16,64,512]{2,1,0:T(8,128)(2,1)S(1)}, u32[]{:S(2)}, u32[]{:S(2)}) async-start(bf16[16,64,512]{2,1,0:T(8,128)(2,1)} %bitcast.10), calls=%async_computation | async-start | bytes 2097152 | tf_op jit(solution)/shard_map/all_to_all | solution.py:205
  10.9 2.6 %copy-start.1 = (bf16[2,512,512]{2,1,0:T(8,128)(2,1)S(1)}, bf16[2,512,512]{2,1,0:T(8,128)(2,1)}, u32[]{:S(2)}) copy-start(bf16[2,512,512]{2,1,0:T(8,128)(2,1)} %param.11) | copy-start | bytes 3145732
  13.5 15.1 %copy-start = (bf16[2,512,1024]{2,1,0:T(8,128)(2,1)S(1)}, bf16[2,512,1024]{2,1,0:T(8,128)(2,1)}, u32[]{:S(2)}) copy-start(bf16[2,512,1024]{2,1,0:T(8,128)(2,1)} %w_in_ref.1) | copy-start | bytes 6291460
  15.3 49.5 %copy-start.3 = (s32[1,512]{1,0:T(1,128)S(1)}, s32[1,512]{1,0:T(1,128)}, u32[]{:S(2)}) copy-start(s32[1,512]{1,0:T(1,128)} %get-tuple-element.7) | copy-start | bytes 6148
  28.5 36.3 %copy-start.2 = (bf16[512,512]{1,0:T(8,128)(2,1)S(1)}, bf16[512,512]{1,0:T(8,128)(2,1)}, u32[]{:S(2)}) copy-start(bf16[512,512]{1,0:T(8,128)(2,1)} %emb_ref.1) | copy-start | bytes 1572868

commit v12 on v10

--- a/solution.py
+++ b/solution.py
@@ -139,21 +139,30 @@
     )(buckets, w_in, tables)
 
 
-def pack_kernel(route_ref, emb_ref, packed_ref, position_ref, *, group_size, user_count):
+def pack_kernel(
+    route_ref, emb_ref, packed_ref, position_ref, placed_ref, *, group_size, user_count
+):
     cand_rows = emb_ref.shape[0]
     block_slots = packed_ref.shape[0]
     capacity = 2 * cand_rows // user_count
-    owner = route_ref[...] // group_size
-    member = (lax.broadcasted_iota(jnp.int32, (user_count, cand_rows), 0) == owner).astype(
-        jnp.float32
-    )
-    earlier = (
-        lax.broadcasted_iota(jnp.int32, (cand_rows, cand_rows), 0)
-        < lax.broadcasted_iota(jnp.int32, (cand_rows, cand_rows), 1)
-    ).astype(jnp.bfloat16)
-    before = jnp.dot(member.astype(jnp.bfloat16), earlier, preferred_element_type=jnp.float32)
-    ranking = jnp.sum(member * before, axis=0, keepdims=True).astype(jnp.int32)
-    position = owner * capacity + ranking
+
+    @pl.when(pl.program_id(0) == 0)
+    def _():
+        owner = route_ref[...] // group_size
+        member = (
+            lax.broadcasted_iota(jnp.int32, (user_count, cand_rows), 0) == owner
+        ).astype(jnp.float32)
+        earlier = (
+            lax.broadcasted_iota(jnp.int32, (cand_rows, cand_rows), 0)
+            < lax.broadcasted_iota(jnp.int32, (cand_rows, cand_rows), 1)
+        ).astype(jnp.bfloat16)
+        before = jnp.dot(
+            member.astype(jnp.bfloat16), earlier, preferred_element_type=jnp.float32
+        )
+        ranking = jnp.sum(member * before, axis=0, keepdims=True).astype(jnp.int32)
+        placed_ref[...] = owner * capacity + ranking
+
+    position = placed_ref[...]
     position_ref[...] = position
     first = pl.program_id(0) * block_slots
     placing = (
@@ -167,7 +176,7 @@
 def pack_rows(cand_emb, cand_route, user_count, group_size):
     cand_rows, features = cand_emb.shape
     slots = 2 * cand_rows
-    block_slots = slots // 4
+    block_slots = slots // 2
     return pl.pallas_call(
         functools.partial(pack_kernel, group_size=group_size, user_count=user_count),
         grid=(slots // block_slots,),
@@ -183,9 +192,10 @@
             pl.BlockSpec((block_slots, features), lambda i: (i, 0)),
             pl.BlockSpec((1, cand_rows), lambda i: (0, 0)),
         ),
+        scratch_shapes=[pltpu.VMEM((1, cand_rows), jnp.int32)],
         compiler_params=pltpu.CompilerParams(dimension_semantics=("arbitrary",)),
         cost_estimate=pl.CostEstimate(
-            flops=2 * slots * cand_rows * features + 8 * user_count * cand_rows * cand_rows,
+            flops=2 * slots * cand_rows * features + 2 * user_count * cand_rows * cand_rows,
             transcendentals=0,
             bytes_accessed=2 * (cand_emb.size + slots * features),
         ),

time: 67.8 us -> 66.8 us (0.985)
  Pallas kernels: 20.7 us -> 19.7 us
    pallas_call x1, Pallas kernels: 3.93 us -> 2.95 us  [pack_rows(): pl.pallas_call(functools.partial(pack_kernel, group_size=group_size, user...]
where the time goes in v12:
time: 66.8 us; the launch traced here: 66.6 us
  Pallas kernels  19.7 us (29%)
  blocking collectives  19.5 us (29%)
  other arithmetic  12 us (18%)
  starting transfers between devices  7.95 us (12%)
  waiting for transfers between devices  4.93 us (7%)
  matrix products  1.73 us (3%)
  between operations  0.71 us (1%)
    all_to_all x1, blocking collectives, local(): lax.all_to_all(delta, 'user', split_axis=0, concat_axis=0, tiled=True)  19.5 us
    pallas_call x1, Pallas kernels, run_layers(): pl.pallas_call(layers_kernel, grid_spec=grid_spec, out_shape=jax.ShapeDty...  16.8 us
    concatenate x1, other arithmetic, run_layers(): jnp.concatenate([history[:, :, :features], jnp.where(in_history, history[...  9.3 us
    all_to_all x1, starting transfers between devices, local(): lax.all_to_all(outgoing, 'user', split_axis=0, concat_axis=0, tiled=True)  7.95 us
    all_to_all x1, waiting for transfers between devices, local(): lax.all_to_all(outgoing, 'user', split_axis=0, concat_axis=0, tiled=True)  4.93 us
    pallas_call x1, Pallas kernels, pack_rows(): pl.pallas_call(functools.partial(pack_kernel, group_size=group_size, user...  2.95 us
    slice x1, other arithmetic, run_layers(): history[:, :, :features]  2.71 us
    dot_general x1, matrix products, local(): lax.dot_general(placing, returned.reshape(-1, features), (((0,), (0,)), (...  1.73 us
  transfers between devices with their start and end apart: 1, of which 1 were waited for; matrix products, arithmetic and copies ran while one was open for 18% of the time, Pallas kernels for 0%

profile of v12, /device:TPU:0, one launch (start us, length us, event | category | flops | bytes accessed | tf_op | source)
XLA Modules:
  0.0 66.6 jit_solution(14206633561424883950)
XLA Ops:
  0.0 3.0 %shard_map.64 = (bf16[1024,512]{1,0:T(8,128)(2,1)}, s32[1,512]{1,0:T(1,128)}) custom-call(s32[1,512]{1,0:T(1,128)} %bitcast.11, bf16[512,512]{1,0:T(8,128)(2,1)} %emb_ref.1), custom_call_target="tpu_custom_call" | custom-call | flops 545259520 | bytes 1572864 | tf_op jit(solution)/shard_map/pallas_call | solution.py:180
  3.0 8.0 %all-to-all-start = ((bf16[16,64,512]{2,1,0:T(8,128)(2,1)}), bf16[16,64,512]{2,1,0:T(8,128)(2,1)S(1)}, u32[]{:S(2)}, u32[]{:S(2)}) async-start(bf16[16,64,512]{2,1,0:T(8,128)(2,1)} %bitcast.9), calls=%async_computation | async-start | bytes 2097152 | tf_op jit(solution)/shard_map/all_to_all | solution.py:216
  11.6 0.0 copy-start.1
  11.6 2.7 %fusion.3 = (bf16[2,1024,512]{2,1,0:T(8,128)(2,1)S(1)}, bf16[2,1024,512]{2,1,0:T(8,128)(2,1)S(1)}) fusion(bf16[2,1024,1024]{2,1,0:T(8,128)(2,1)} %bitcast.8, pred[1024]{0:T(1024)(128)(4,1)S(1)} %iota_compare_fusion.4), kind=kLoop, calls=%fused_computation.7 | loop fusion | flops 1048576 | bytes 8389632 | tf_op jit(solution)/shard_map/slice | solution.py:102
  14.3 0.0 copy-done.1
  14.3 0.0 copy-start
  14.3 9.3 %pad_maximum_fusion.tables_hbm = bf16[2,2560,512]{2,1,0:T(8,128)(2,1)} fusion(bf16[2,512,512]{2,1,0:T(8,128)(2,1)S(1)} %copy-done.1, bf16[2,1024,512]{2,1,0:T(8,128)(2,1)S(1)} %get-tuple-element.10, bf16[2,1024,512]{2,1,0:T(8,128)(2,1)S(1)} %get-tuple-element.9), kind=kLoop, calls=%fused_computation | loop fusion | flops 15728640 | bytes 10485760 | tf_op jit(solution)/shard_map/concatenate | solution.py:100
  23.6 0.0 copy-start.3
  23.6 4.9 %all-to-all-done.rows_ref = bf16[16,64,512]{2,1,0:T(8,128)(2,1)S(1)} async-done(((bf16[16,64,512]{2,1,0:T(8,128)(2,1)}), bf16[16,64,512]{2,1,0:T(8,128)(2,1)S(1)}, u32[]{:S(2)}, u32[]{:S(2)}) %all-to-all-start) | async-done | bytes 1048608 | tf_op jit(solution)/shard_map/all_to_all | solution.py:216
  28.6 0.0 copy-done
  28.6 0.0 copy-start.2
  28.6 16.8 %shard_map.65 = bf16[16,64,512]{2,1,0:T(8,128)(2,1)S(1)} custom-call(bf16[16,64,512]{2,1,0:T(8,128)(2,1)S(1)} %all-to-all-done.rows_ref, bf16[2,512,1024]{2,1,0:T(8,128)(2,1)S(1)} %copy-done, bf16[2,2560,512]{2,1,0:T(8,128)(2,1)} %pad_maximum_fusion.tables_hbm), custom_call_target="tpu_custom_call" | custom-call | flops 7516192768 | bytes 9437184 | tf_op jit(solution)/shard_map/pallas_call | solution.py:127
  45.4 19.5 %all_to_all.10 = bf16[16,64,512]{2,1,0:T(8,128)(2,1)S(1)} all-to-all(bf16[16,64,512]{2,1,0:T(8,128)(2,1)S(1)} %shard_map.65), channel_id=1, replica_groups=mesh['user'=16,'cand'=8] {'user'}, dimensions={0} | all-to-all | bytes 2097152 | tf_op jit(solution)/shard_map/all_to_all | solution.py:219
  64.9 0.0 copy-done.3
  64.9 0.0 copy-done.2
  64.9 1.7 %fusion.1 = f32[512,512]{1,0:T(8,128)} fusion(bf16[1024,512]{1,0:T(8,128)(2,1)S(1)} %bitcast.10, s32[512]{0:T(512)S(1)} %bitcast.12, bf16[512,512]{1,0:T(8,128)(2,1)S(1)} %copy-done.2), kind=kOutput, calls=%fused_computation.4 | convolution fusion | flops 537919488 | bytes 2623488 | tf_op jit(solution)/shard_map/dot_general | solution.py:220
  (1 shorter events, 0.0 us)
Async XLA Ops:
  3.0 25.6 %all-to-all-start = ((bf16[16,64,512]{2,1,0:T(8,128)(2,1)}), bf16[16,64,512]{2,1,0:T(8,128)(2,1)S(1)}, u32[]{:S(2)}, u32[]{:S(2)}) async-start(bf16[16,64,512]{2,1,0:T(8,128)(2,1)} %bitcast.9), calls=%async_computation | async-start | bytes 2097152 | tf_op jit(solution)/shard_map/all_to_all | solution.py:216
  11.6 2.7 %copy-start.1 = (bf16[2,512,512]{2,1,0:T(8,128)(2,1)S(1)}, bf16[2,512,512]{2,1,0:T(8,128)(2,1)}, u32[]{:S(2)}) copy-start(bf16[2,512,512]{2,1,0:T(8,128)(2,1)} %param.11) | copy-start | bytes 3145732
  14.3 14.2 %copy-start = (bf16[2,512,1024]{2,1,0:T(8,128)(2,1)S(1)}, bf16[2,512,1024]{2,1,0:T(8,128)(2,1)}, u32[]{:S(2)}) copy-start(bf16[2,512,1024]{2,1,0:T(8,128)(2,1)} %w_in_ref.1) | copy-start | bytes 6291460
  23.6 41.2 %copy-start.3 = (s32[1,512]{1,0:T(1,128)S(1)}, s32[1,512]{1,0:T(1,128)}, u32[]{:S(2)}) copy-start(s32[1,512]{1,0:T(1,128)} %get-tuple-element.7) | copy-start | bytes 6148
  28.6 36.3 %copy-start.2 = (bf16[512,512]{1,0:T(8,128)(2,1)S(1)}, bf16[512,512]{1,0:T(8,128)(2,1)}, u32[]{:S(2)}) copy-start(bf16[512,512]{1,0:T(8,128)(2,1)} %emb_ref.1) | copy-start | bytes 1572868

commit v13 on v9

--- a/solution.py
+++ b/solution.py
@@ -139,7 +139,7 @@
     )(buckets, w_in, tables)
 
 
-def pack_kernel(route_ref, emb_ref, packed_ref, position_ref, *, group_size, user_count):
+def pack_kernel(route_ref, column_ref, emb_ref, packed_ref, position_ref, *, group_size, user_count):
     cand_rows = emb_ref.shape[0]
     capacity = packed_ref.shape[0] // user_count
     owner = route_ref[...] // group_size
@@ -153,7 +153,19 @@
     before = jnp.dot(member.astype(jnp.bfloat16), earlier, preferred_element_type=jnp.float32)
     ranking = jnp.sum(member * before, axis=0, keepdims=True).astype(jnp.int32)
     position = owner * capacity + ranking
-    position_ref[...] = position
+    owner_column = column_ref[...] // group_size
+    member_column = (
+        lax.broadcasted_iota(jnp.int32, (cand_rows, user_count), 1) == owner_column
+    ).astype(jnp.float32)
+    later = (
+        lax.broadcasted_iota(jnp.int32, (cand_rows, cand_rows), 1)
+        < lax.broadcasted_iota(jnp.int32, (cand_rows, cand_rows), 0)
+    ).astype(jnp.bfloat16)
+    before_column = jnp.dot(
+        later, member_column.astype(jnp.bfloat16), preferred_element_type=jnp.float32
+    )
+    ranking_column = jnp.sum(member_column * before_column, axis=1, keepdims=True)
+    position_ref[...] = owner_column * capacity + ranking_column.astype(jnp.int32)
     placing = (
         lax.broadcasted_iota(jnp.int32, (packed_ref.shape[0], cand_rows), 0) == position
     ).astype(jnp.bfloat16)
@@ -169,16 +181,41 @@
         functools.partial(pack_kernel, group_size=group_size, user_count=user_count),
         out_shape=(
             jax.ShapeDtypeStruct((slots, features), jnp.bfloat16),
-            jax.ShapeDtypeStruct((1, cand_rows), jnp.int32),
-        ),
-        in_specs=[pl.BlockSpec(memory_space=pltpu.VMEM)] * 2,
+            jax.ShapeDtypeStruct((cand_rows, 1), jnp.int32),
+        ),
+        in_specs=[pl.BlockSpec(memory_space=pltpu.VMEM)] * 3,
         out_specs=(pl.BlockSpec(memory_space=pltpu.VMEM),) * 2,
         cost_estimate=pl.CostEstimate(
-            flops=2 * slots * cand_rows * features + 2 * user_count * cand_rows * cand_rows,
+            flops=2 * slots * cand_rows * features + 4 * user_count * cand_rows * cand_rows,
             transcendentals=0,
             bytes_accessed=2 * (cand_emb.size + slots * features),
         ),
-    )(cand_route.reshape(1, cand_rows), cand_emb)
+    )(cand_route.reshape(1, cand_rows), cand_route.reshape(cand_rows, 1), cand_emb)
+
+
+def unpack_kernel(returned_ref, position_ref, emb_ref, out_ref):
+    cand_rows, slots = position_ref.shape[0], returned_ref.shape[0]
+    picking = (
+        lax.broadcasted_iota(jnp.int32, (cand_rows, slots), 1) == position_ref[...]
+    ).astype(jnp.bfloat16)
+    out_ref[...] = emb_ref[...].astype(jnp.float32) + jnp.dot(
+        picking, returned_ref[...], preferred_element_type=jnp.float32
+    )
+
+
+def unpack_rows(returned, position, cand_emb):
+    cand_rows, features = cand_emb.shape
+    return pl.pallas_call(
+        unpack_kernel,
+        out_shape=jax.ShapeDtypeStruct((cand_rows, features), jnp.float32),
+        in_specs=[pl.BlockSpec(memory_space=pltpu.VMEM)] * 3,
+        out_specs=pl.BlockSpec(memory_space=pltpu.VMEM),
+        cost_estimate=pl.CostEstimate(
+            flops=2 * cand_rows * returned.shape[0] * features,
+            transcendentals=0,
+            bytes_accessed=2 * returned.size + 6 * cand_emb.size,
+        ),
+    )(returned, position, cand_emb)
 
 
 def local(cand_emb, cand_route, hist_kv, hist_len, w_in, w_out):
@@ -188,21 +225,12 @@
     packed, position = pack_rows(cand_emb, cand_route, user_count, group_size)
     slots = packed.shape[0]
     capacity = slots // user_count
-    placing = (lax.broadcasted_iota(jnp.int32, (slots, cand_rows), 0) == position).astype(
-        jnp.bfloat16
-    )
     outgoing = packed.reshape(user_count, capacity, features)
     items = lax.all_to_all(outgoing, "user", split_axis=0, concat_axis=0, tiled=True)
     history = hist_kv.reshape(hist_kv.shape[0], hist_kv.shape[2], hist_kv.shape[3])
     delta = run_layers(items, history, hist_len, w_in, w_out)
     returned = lax.all_to_all(delta, "user", split_axis=0, concat_axis=0, tiled=True)
-    gathered = lax.dot_general(
-        placing,
-        returned.reshape(-1, features),
-        (((0,), (0,)), ((), ())),
-        preferred_element_type=jnp.float32,
-    )
-    return cand_emb.astype(jnp.float32) + gathered
+    return unpack_rows(returned.reshape(-1, features), position, cand_emb)
 
 
 def solution(mesh):

time: 66.8 us -> 70.3 us (1.052)
  Pallas kernels: 19.7 us -> 23.1 us
  matrix products: 1.73 us -> 0 us
  local copies, waits for them, and re-layouts: 0.02 us -> 1.54 us
    pallas_call x0 -> x1, Pallas kernels: none -> 3.16 us  [unpack_rows(): pl.pallas_call(unpack_kernel, out_shape=jax.ShapeDtypeStruct((cand_rows,...]
    dot_general x1 -> x0, matrix products: 1.73 us -> none  [local(): lax.dot_general(placing, returned.reshape(-1, features), (((0,), (0,)), (...]
    reshape x0 -> x1, local copies, waits for them, and re-layouts: none -> 1.53 us  [pack_rows(): cand_route.reshape(cand_rows, 1)]
  transfers between devices with their start and end apart: 1 -> 1, of which waited for: 1 -> 1; matrix products, arithmetic and copies ran while one was open for 18% -> 17% of each run, Pallas kernels for 0% -> 0%
where the time goes in v13:
time: 70.3 us; the launch traced here: 70 us
  Pallas kernels  23.1 us (33%)
  blocking collectives  19.7 us (28%)
  other arithmetic  12 us (17%)
  starting transfers between devices  7.96 us (11%)
  waiting for transfers between devices  4.92 us (7%)
  local copies, waits for them, and re-layouts  1.54 us (2%)
  between operations  0.71 us (1%)
    all_to_all x1, blocking collectives, local(): lax.all_to_all(delta, 'user', split_axis=0, concat_axis=0, tiled=True)  19.7 us
    pallas_call x1, Pallas kernels, run_layers(): pl.pallas_call(layers_kernel, grid_spec=grid_spec, out_shape=jax.ShapeDty...  16.7 us
    concatenate x1, other arithmetic, run_layers(): jnp.concatenate([history[:, :, :features], jnp.where(in_history, history[...  9.31 us
    all_to_all x1, starting transfers between devices, local(): lax.all_to_all(outgoing, 'user', split_axis=0, concat_axis=0, tiled=True)  7.96 us
    all_to_all x1, waiting for transfers between devices, local(): lax.all_to_all(outgoing, 'user', split_axis=0, concat_axis=0, tiled=True)  4.92 us
    pallas_call x1, Pallas kernels, pack_rows(): pl.pallas_call(functools.partial(pack_kernel, group_size=group_size, user...  3.22 us
    pallas_call x1, Pallas kernels, unpack_rows(): pl.pallas_call(unpack_kernel, out_shape=jax.ShapeDtypeStruct((cand_rows,...  3.16 us
    slice x1, other arithmetic, run_layers(): history[:, :, :features]  2.71 us
  transfers between devices with their start and end apart: 1, of which 1 were waited for; matrix products, arithmetic and copies ran while one was open for 17% of the time, Pallas kernels for 0%

profile of v13, /device:TPU:0, one launch (start us, length us, event | category | flops | bytes accessed | tf_op | source)
XLA Modules:
  0.0 70.0 jit_solution(5238020951986791939)
XLA Ops:
  0.0 1.5 %copy.7.column_ref = s32[512,1]{1,0:T(8,128)} copy(s32[512,1]{0,1:T(1,128)} %bitcast.10) | data formatting | bytes 4096 | tf_op jit(solution)/shard_map/reshape | solution.py:193
  1.5 3.2 %shard_map.64 = (bf16[1024,512]{1,0:T(8,128)(2,1)}, s32[512,1]{1,0:T(8,128)}) custom-call(s32[1,512]{1,0:T(1,128)} %bitcast.11, s32[512,1]{1,0:T(8,128)} %copy.7.column_ref, bf16[512,512]{1,0:T(8,128)(2,1)} %emb_ref.3), custom_call_target="tpu_custom_call" | custom-call | flops 553648128 | bytes 1572864 | tf_op jit(solution)/shard_map/pallas_call | solution.py:180
  4.7 8.0 %all-to-all-start = ((bf16[16,64,512]{2,1,0:T(8,128)(2,1)}), bf16[16,64,512]{2,1,0:T(8,128)(2,1)S(1)}, u32[]{:S(2)}, u32[]{:S(2)}) async-start(bf16[16,64,512]{2,1,0:T(8,128)(2,1)} %bitcast.9), calls=%async_computation | async-start | bytes 2097152 | tf_op jit(solution)/shard_map/all_to_all | solution.py:229
  13.4 0.0 copy-start.1
  13.4 2.7 %fusion = (bf16[2,1024,512]{2,1,0:T(8,128)(2,1)S(1)}, bf16[2,1024,512]{2,1,0:T(8,128)(2,1)S(1)}) fusion(bf16[2,1024,1024]{2,1,0:T(8,128)(2,1)} %bitcast.7, pred[1024]{0:T(1024)(128)(4,1)S(1)} %iota_compare_fusion), kind=kLoop, calls=%fused_computation.3 | loop fusion | flops 1048576 | bytes 8389632 | tf_op jit(solution)/shard_map/slice | solution.py:102
  16.1 0.0 copy-done.1
  16.1 0.0 copy-start
  16.1 9.3 %pad_maximum_fusion.tables_hbm = bf16[2,2560,512]{2,1,0:T(8,128)(2,1)} fusion(bf16[2,512,512]{2,1,0:T(8,128)(2,1)S(1)} %copy-done.1, bf16[2,1024,512]{2,1,0:T(8,128)(2,1)S(1)} %get-tuple-element.10, bf16[2,1024,512]{2,1,0:T(8,128)(2,1)S(1)} %get-tuple-element.9), kind=kLoop, calls=%fused_computation | loop fusion | flops 15728640 | bytes 10485760 | tf_op jit(solution)/shard_map/concatenate | solution.py:100
  25.4 4.9 %all-to-all-done.rows_ref = bf16[16,64,512]{2,1,0:T(8,128)(2,1)S(1)} async-done(((bf16[16,64,512]{2,1,0:T(8,128)(2,1)}), bf16[16,64,512]{2,1,0:T(8,128)(2,1)S(1)}, u32[]{:S(2)}, u32[]{:S(2)}) %all-to-all-start) | async-done | bytes 1048608 | tf_op jit(solution)/shard_map/all_to_all | solution.py:229
  30.4 0.0 copy-done
  30.4 16.7 %shard_map.65 = bf16[16,64,512]{2,1,0:T(8,128)(2,1)S(1)} custom-call(bf16[16,64,512]{2,1,0:T(8,128)(2,1)S(1)} %all-to-all-done.rows_ref, bf16[2,512,1024]{2,1,0:T(8,128)(2,1)S(1)} %copy-done, bf16[2,2560,512]{2,1,0:T(8,128)(2,1)} %pad_maximum_fusion.tables_hbm), custom_call_target="tpu_custom_call" | custom-call | flops 7516192768 | bytes 9437184 | tf_op jit(solution)/shard_map/pallas_call | solution.py:127
  47.1 19.7 %all_to_all.10 = bf16[16,64,512]{2,1,0:T(8,128)(2,1)} all-to-all(bf16[16,64,512]{2,1,0:T(8,128)(2,1)S(1)} %shard_map.65), channel_id=1, replica_groups=mesh['user'=16,'cand'=8] {'user'}, dimensions={0} | all-to-all | bytes 2097152 | tf_op jit(solution)/shard_map/all_to_all | solution.py:232
  66.8 3.2 %shard_map.66 = f32[512,512]{1,0:T(8,128)} custom-call(bf16[1024,512]{1,0:T(8,128)(2,1)} %bitcast.8, s32[512,1]{1,0:T(8,128)} %get-tuple-element.8.position_ref, bf16[512,512]{1,0:T(8,128)(2,1)} %emb_ref.3), custom_call_target="tpu_custom_call" | custom-call | flops 536870912 | bytes 2621440 | tf_op jit(solution)/shard_map/pallas_call | solution.py:208
  (1 shorter events, 0.0 us)
Async XLA Ops:
  4.7 25.6 %all-to-all-start = ((bf16[16,64,512]{2,1,0:T(8,128)(2,1)}), bf16[16,64,512]{2,1,0:T(8,128)(2,1)S(1)}, u32[]{:S(2)}, u32[]{:S(2)}) async-start(bf16[16,64,512]{2,1,0:T(8,128)(2,1)} %bitcast.9), calls=%async_computation | async-start | bytes 2097152 | tf_op jit(solution)/shard_map/all_to_all | solution.py:229
  13.4 2.7 %copy-start.1 = (bf16[2,512,512]{2,1,0:T(8,128)(2,1)S(1)}, bf16[2,512,512]{2,1,0:T(8,128)(2,1)}, u32[]{:S(2)}) copy-start(bf16[2,512,512]{2,1,0:T(8,128)(2,1)} %param.11) | copy-start | bytes 3145732
  16.1 14.2 %copy-start = (bf16[2,512,1024]{2,1,0:T(8,128)(2,1)S(1)}, bf16[2,512,1024]{2,1,0:T(8,128)(2,1)}, u32[]{:S(2)}) copy-start(bf16[2,512,1024]{2,1,0:T(8,128)(2,1)} %w_in_ref.1) | copy-start | bytes 6291460

commit v14 on v9

--- a/solution.py
+++ b/solution.py
@@ -111,7 +111,7 @@
         grid=(steps,),
         in_specs=[
             pl.BlockSpec((sources, SLOT_BLOCK, features), lambda i: (0, i, 0)),
-            pl.BlockSpec(w_in.shape, lambda i: (0, 0, 0)),
+            pl.BlockSpec(memory_space=pltpu.VMEM),
             pl.BlockSpec(memory_space=pltpu.MemorySpace.HBM),
         ],
         out_specs=pl.BlockSpec((sources, SLOT_BLOCK, features), lambda i: (0, i, 0)),

time: 66.8 us -> 66.8 us (level)
  no operation moved by 1% of the time
where the time goes in v14:
time: 66.8 us; the launch traced here: 66.6 us
  Pallas kernels  19.7 us (29%)
  blocking collectives  19.5 us (29%)
  other arithmetic  12 us (18%)
  starting transfers between devices  7.96 us (12%)
  waiting for transfers between devices  4.92 us (7%)
  matrix products  1.73 us (3%)
  between operations  0.71 us (1%)
    all_to_all x1, blocking collectives, local(): lax.all_to_all(delta, 'user', split_axis=0, concat_axis=0, tiled=True)  19.5 us
    pallas_call x1, Pallas kernels, run_layers(): pl.pallas_call(layers_kernel, grid_spec=grid_spec, out_shape=jax.ShapeDty...  16.8 us
    concatenate x1, other arithmetic, run_layers(): jnp.concatenate([history[:, :, :features], jnp.where(in_history, history[...  9.3 us
    all_to_all x1, starting transfers between devices, local(): lax.all_to_all(outgoing, 'user', split_axis=0, concat_axis=0, tiled=True)  7.96 us
    all_to_all x1, waiting for transfers between devices, local(): lax.all_to_all(outgoing, 'user', split_axis=0, concat_axis=0, tiled=True)  4.92 us
    pallas_call x1, Pallas kernels, pack_rows(): pl.pallas_call(functools.partial(pack_kernel, group_size=group_size, user...  2.92 us
    slice x1, other arithmetic, run_layers(): history[:, :, :features]  2.71 us
    dot_general x1, matrix products, local(): lax.dot_general(placing, returned.reshape(-1, features), (((0,), (0,)), (...  1.73 us
  transfers between devices with their start and end apart: 1, of which 1 were waited for; matrix products, arithmetic and copies ran while one was open for 18% of the time, Pallas kernels for 0%

profile of v14, /device:TPU:0, one launch (start us, length us, event | category | flops | bytes accessed | tf_op | source)
XLA Modules:
  0.0 66.6 jit_solution(11386256151086364896)
XLA Ops:
  0.0 2.9 %shard_map.64 = (bf16[1024,512]{1,0:T(8,128)(2,1)}, s32[1,512]{1,0:T(1,128)}) custom-call(s32[1,512]{1,0:T(1,128)} %bitcast.11, bf16[512,512]{1,0:T(8,128)(2,1)} %emb_ref.1), custom_call_target="tpu_custom_call" | custom-call | flops 545259520 | bytes 1572864 | tf_op jit(solution)/shard_map/pallas_call | solution.py:168
  2.9 8.0 %all-to-all-start = ((bf16[16,64,512]{2,1,0:T(8,128)(2,1)}), bf16[16,64,512]{2,1,0:T(8,128)(2,1)S(1)}, u32[]{:S(2)}, u32[]{:S(2)}) async-start(bf16[16,64,512]{2,1,0:T(8,128)(2,1)} %bitcast.9), calls=%async_computation | async-start | bytes 2097152 | tf_op jit(solution)/shard_map/all_to_all | solution.py:195
  11.6 0.0 copy-start.1
  11.6 2.7 %fusion.3 = (bf16[2,1024,512]{2,1,0:T(8,128)(2,1)S(1)}, bf16[2,1024,512]{2,1,0:T(8,128)(2,1)S(1)}) fusion(bf16[2,1024,1024]{2,1,0:T(8,128)(2,1)} %bitcast.8, pred[1024]{0:T(1024)(128)(4,1)S(1)} %iota_compare_fusion.4), kind=kLoop, calls=%fused_computation.7 | loop fusion | flops 1048576 | bytes 8389632 | tf_op jit(solution)/shard_map/slice | solution.py:102
  14.3 0.0 copy-done.1
  14.3 0.0 copy-start
  14.3 9.3 %pad_maximum_fusion.tables_hbm = bf16[2,2560,512]{2,1,0:T(8,128)(2,1)} fusion(bf16[2,512,512]{2,1,0:T(8,128)(2,1)S(1)} %copy-done.1, bf16[2,1024,512]{2,1,0:T(8,128)(2,1)S(1)} %get-tuple-element.10, bf16[2,1024,512]{2,1,0:T(8,128)(2,1)S(1)} %get-tuple-element.9), kind=kLoop, calls=%fused_computation | loop fusion | flops 15728640 | bytes 10485760 | tf_op jit(solution)/shard_map/concatenate | solution.py:100
  23.6 0.0 copy-start.3
  23.6 4.9 %all-to-all-done.rows_ref = bf16[16,64,512]{2,1,0:T(8,128)(2,1)S(1)} async-done(((bf16[16,64,512]{2,1,0:T(8,128)(2,1)}), bf16[16,64,512]{2,1,0:T(8,128)(2,1)S(1)}, u32[]{:S(2)}, u32[]{:S(2)}) %all-to-all-start) | async-done | bytes 1048608 | tf_op jit(solution)/shard_map/all_to_all | solution.py:195
  28.5 0.0 copy-done
  28.5 0.0 copy-start.2
  28.5 16.8 %shard_map.65 = bf16[16,64,512]{2,1,0:T(8,128)(2,1)S(1)} custom-call(bf16[16,64,512]{2,1,0:T(8,128)(2,1)S(1)} %all-to-all-done.rows_ref, bf16[2,512,1024]{2,1,0:T(8,128)(2,1)S(1)} %copy-done, bf16[2,2560,512]{2,1,0:T(8,128)(2,1)} %pad_maximum_fusion.tables_hbm), custom_call_target="tpu_custom_call" | custom-call | flops 7516192768 | bytes 9437184 | tf_op jit(solution)/shard_map/pallas_call | solution.py:127
  45.3 19.5 %all_to_all.10 = bf16[16,64,512]{2,1,0:T(8,128)(2,1)S(1)} all-to-all(bf16[16,64,512]{2,1,0:T(8,128)(2,1)S(1)} %shard_map.65), channel_id=1, replica_groups=mesh['user'=16,'cand'=8] {'user'}, dimensions={0} | all-to-all | bytes 2097152 | tf_op jit(solution)/shard_map/all_to_all | solution.py:198
  64.8 0.0 copy-done.3
  64.8 0.0 copy-done.2
  64.8 1.7 %fusion.1 = f32[512,512]{1,0:T(8,128)} fusion(bf16[1024,512]{1,0:T(8,128)(2,1)S(1)} %bitcast.10, s32[512]{0:T(512)S(1)} %bitcast.12, bf16[512,512]{1,0:T(8,128)(2,1)S(1)} %copy-done.2), kind=kOutput, calls=%fused_computation.4 | convolution fusion | flops 537919488 | bytes 2623488 | tf_op jit(solution)/shard_map/dot_general | solution.py:199
  (1 shorter events, 0.0 us)
Async XLA Ops:
  2.9 25.6 %all-to-all-start = ((bf16[16,64,512]{2,1,0:T(8,128)(2,1)}), bf16[16,64,512]{2,1,0:T(8,128)(2,1)S(1)}, u32[]{:S(2)}, u32[]{:S(2)}) async-start(bf16[16,64,512]{2,1,0:T(8,128)(2,1)} %bitcast.9), calls=%async_computation | async-start | bytes 2097152 | tf_op jit(solution)/shard_map/all_to_all | solution.py:195
  11.6 2.7 %copy-start.1 = (bf16[2,512,512]{2,1,0:T(8,128)(2,1)S(1)}, bf16[2,512,512]{2,1,0:T(8,128)(2,1)}, u32[]{:S(2)}) copy-start(bf16[2,512,512]{2,1,0:T(8,128)(2,1)} %param.11) | copy-start | bytes 3145732
  14.3 14.2 %copy-start = (bf16[2,512,1024]{2,1,0:T(8,128)(2,1)S(1)}, bf16[2,512,1024]{2,1,0:T(8,128)(2,1)}, u32[]{:S(2)}) copy-start(bf16[2,512,1024]{2,1,0:T(8,128)(2,1)} %w_in_ref.1) | copy-start | bytes 6291460
  23.6 41.2 %copy-start.3 = (s32[1,512]{1,0:T(1,128)S(1)}, s32[1,512]{1,0:T(1,128)}, u32[]{:S(2)}) copy-start(s32[1,512]{1,0:T(1,128)} %get-tuple-element.7) | copy-start | bytes 6148
  28.5 36.3 %copy-start.2 = (bf16[512,512]{1,0:T(8,128)(2,1)S(1)}, bf16[512,512]{1,0:T(8,128)(2,1)}, u32[]{:S(2)}) copy-start(bf16[512,512]{1,0:T(8,128)(2,1)} %emb_ref.1) | copy-start | bytes 1572868

commit v15 on v14

--- a/solution.py
+++ b/solution.py
@@ -23,7 +23,9 @@
     return center * lax.rsqrt(spread + epsilon)
 
 
-def layers_kernel(rows_ref, w_in_ref, tables_hbm, out_ref, tables_ref, copy_sems):
+def layers_kernel(
+    length_ref, rows_ref, w_in_ref, tables_hbm, out_ref, tables_ref, attended_ref, copy_sems
+):
     sources, slots, features = rows_ref.shape
     block_rows = sources * slots
     layer_count = w_in_ref.shape[0]
@@ -64,26 +66,33 @@
             projected = silu(mixed).astype(jnp.bfloat16)
             gate = projected[:, :features].astype(jnp.float32)
             arrive(layer_index)
-            heads = []
-            for head in range(HEADS):
-                low = head * head_dim
-                query = projected[:, features + low:features + low + head_dim]
-                keys = tables_ref[layer_index, :history_span, low:low + head_dim]
-                values = tables_ref[
-                    layer_index, history_span:2 * history_span, low:low + head_dim
-                ]
-                scores = lax.dot_general(
-                    query, keys, (((1,), (1,)), ((), ())), preferred_element_type=jnp.float32
-                )
-                weight = silu(scores * factor).astype(jnp.bfloat16)
-                heads.append(
-                    jnp.dot(
-                        weight,
-                        values,
-                        preferred_element_type=jnp.float32,
+            def attend(span, layer_index=layer_index, projected=projected):
+                heads = []
+                for head in range(HEADS):
+                    low = head * head_dim
+                    query = projected[:, features + low:features + low + head_dim]
+                    keys = tables_ref[layer_index, :span, low:low + head_dim]
+                    values = tables_ref[
+                        layer_index, history_span:history_span + span, low:low + head_dim
+                    ]
+                    scores = lax.dot_general(
+                        query, keys, (((1,), (1,)), ((), ())), preferred_element_type=jnp.float32
                     )
-                )
-            attended = jnp.concatenate(heads, axis=1)
+                    weight = silu(scores * factor).astype(jnp.bfloat16)
+                    heads.append(jnp.dot(weight, values, preferred_element_type=jnp.float32))
+                attended_ref[...] = jnp.concatenate(heads, axis=1)
+
+            short = length_ref[0] <= history_span // 2
+
+            @pl.when(short)
+            def _():
+                attend(history_span // 2)
+
+            @pl.when(jnp.logical_not(short))
+            def _():
+                attend(history_span)
+
+            attended = attended_ref[...]
             branch = (layer_normed(attended) * gate).astype(jnp.bfloat16)
             residual = residual + jnp.dot(
                 branch,
@@ -107,16 +116,17 @@
     )
     steps = capacity // SLOT_BLOCK
     grid_spec = pltpu.PrefetchScalarGridSpec(
-        num_scalar_prefetch=0,
+        num_scalar_prefetch=1,
         grid=(steps,),
         in_specs=[
-            pl.BlockSpec((sources, SLOT_BLOCK, features), lambda i: (0, i, 0)),
-            pl.BlockSpec(memory_space=pltpu.VMEM),
+            pl.BlockSpec((sources, SLOT_BLOCK, features), lambda i, n: (0, i, 0)),
+            pl.BlockSpec(w_in.shape, lambda i, n: (0, 0, 0)),
             pl.BlockSpec(memory_space=pltpu.MemorySpace.HBM),
         ],
-        out_specs=pl.BlockSpec((sources, SLOT_BLOCK, features), lambda i: (0, i, 0)),
+        out_specs=pl.BlockSpec((sources, SLOT_BLOCK, features), lambda i, n: (0, i, 0)),
         scratch_shapes=[
             pltpu.VMEM(tables.shape, tables.dtype),
+            pltpu.VMEM((sources * SLOT_BLOCK, features), jnp.float32),
             pltpu.SemaphoreType.DMA((layer_count,)),
         ],
     )
@@ -136,7 +146,7 @@
             transcendentals=row_count * layer_count * (HEADS * history_span + 2 * features),
             bytes_accessed=2 * (history.size + w_in.size + w_out.size + 2 * buckets.size),
         ),
-    )(buckets, w_in, tables)
+    )(length, buckets, w_in, tables)
 
 
 def pack_kernel(route_ref, emb_ref, packed_ref, position_ref, *, group_size, user_count):

time: 66.8 us -> 66.9 us (level)
  Pallas kernels: 19.7 us -> 17.8 us
  blocking collectives: 19.5 us -> 21.2 us
    pallas_call x1, Pallas kernels: 16.8 us -> 14.9 us  [run_layers(): pl.pallas_call(layers_kernel, grid_spec=grid_spec, out_shape=jax.ShapeDty...]
    all_to_all x1, blocking collectives: 19.5 us -> 21.2 us  [local(): lax.all_to_all(delta, 'user', split_axis=0, concat_axis=0, tiled=True)]
where the time goes in v15:
time: 66.9 us; the launch traced here: 66.3 us
  blocking collectives  21.2 us (32%)
  Pallas kernels  17.8 us (27%)
  other arithmetic  12 us (18%)
  starting transfers between devices  7.96 us (12%)
  waiting for transfers between devices  4.92 us (7%)
  matrix products  1.73 us (3%)
  between operations  0.71 us (1%)
    all_to_all x1, blocking collectives, local(): lax.all_to_all(delta, 'user', split_axis=0, concat_axis=0, tiled=True)  21.2 us
    pallas_call x1, Pallas kernels, run_layers(): pl.pallas_call(layers_kernel, grid_spec=grid_spec, out_shape=jax.ShapeDty...  14.9 us
    concatenate x1, other arithmetic, run_layers(): jnp.concatenate([history[:, :, :features], jnp.where(in_history, history[...  9.3 us
    all_to_all x1, starting transfers between devices, local(): lax.all_to_all(outgoing, 'user', split_axis=0, concat_axis=0, tiled=True)  7.96 us
    all_to_all x1, waiting for transfers between devices, local(): lax.all_to_all(outgoing, 'user', split_axis=0, concat_axis=0, tiled=True)  4.92 us
    pallas_call x1, Pallas kernels, pack_rows(): pl.pallas_call(functools.partial(pack_kernel, group_size=group_size, user...  2.92 us
    slice x1, other arithmetic, run_layers(): history[:, :, :features]  2.71 us
    dot_general x1, matrix products, local(): lax.dot_general(placing, returned.reshape(-1, features), (((0,), (0,)), (...  1.73 us
  transfers between devices with their start and end apart: 1, of which 1 were waited for; matrix products, arithmetic and copies ran while one was open for 18% of the time, Pallas kernels for 0%

profile of v15, /device:TPU:0, one launch (start us, length us, event | category | flops | bytes accessed | tf_op | source)
XLA Modules:
  0.0 66.3 jit_solution(9602032777368362300)
XLA Ops:
  0.0 2.9 %shard_map.64 = (bf16[1024,512]{1,0:T(8,128)(2,1)}, s32[1,512]{1,0:T(1,128)}) custom-call(s32[1,512]{1,0:T(1,128)} %bitcast.11, bf16[512,512]{1,0:T(8,128)(2,1)} %emb_ref.1), custom_call_target="tpu_custom_call" | custom-call | flops 545259520 | bytes 1572864 | tf_op jit(solution)/shard_map/pallas_call | solution.py:178
  2.9 8.0 %all-to-all-start = ((bf16[16,64,512]{2,1,0:T(8,128)(2,1)}), bf16[16,64,512]{2,1,0:T(8,128)(2,1)S(1)}, u32[]{:S(2)}, u32[]{:S(2)}) async-start(bf16[16,64,512]{2,1,0:T(8,128)(2,1)} %bitcast.9), calls=%async_computation | async-start | bytes 2097152 | tf_op jit(solution)/shard_map/all_to_all | solution.py:205
  11.6 0.0 copy-start.1
  11.6 2.7 %fusion.3 = (bf16[2,1024,512]{2,1,0:T(8,128)(2,1)S(1)}, bf16[2,1024,512]{2,1,0:T(8,128)(2,1)S(1)}) fusion(bf16[2,1024,1024]{2,1,0:T(8,128)(2,1)} %bitcast.8, pred[1024]{0:T(1024)(128)(4,1)S(1)} %iota_compare_fusion.4), kind=kLoop, calls=%fused_computation.7 | loop fusion | flops 1048576 | bytes 8389632 | tf_op jit(solution)/shard_map/slice | solution.py:111
  14.3 0.0 copy-done.1
  14.3 0.0 copy-start
  14.3 9.3 %pad_maximum_fusion.tables_hbm = bf16[2,2560,512]{2,1,0:T(8,128)(2,1)} fusion(bf16[2,512,512]{2,1,0:T(8,128)(2,1)S(1)} %copy-done.1, bf16[2,1024,512]{2,1,0:T(8,128)(2,1)S(1)} %get-tuple-element.10, bf16[2,1024,512]{2,1,0:T(8,128)(2,1)S(1)} %get-tuple-element.9), kind=kLoop, calls=%fused_computation | loop fusion | flops 15728640 | bytes 10485760 | tf_op jit(solution)/shard_map/concatenate | solution.py:109
  23.6 0.0 copy-start.3
  23.6 4.9 %all-to-all-done.rows_ref = bf16[16,64,512]{2,1,0:T(8,128)(2,1)S(1)} async-done(((bf16[16,64,512]{2,1,0:T(8,128)(2,1)}), bf16[16,64,512]{2,1,0:T(8,128)(2,1)S(1)}, u32[]{:S(2)}, u32[]{:S(2)}) %all-to-all-start) | async-done | bytes 1048608 | tf_op jit(solution)/shard_map/all_to_all | solution.py:205
  28.5 0.0 copy-done
  28.5 0.0 copy-start.2
  28.5 14.9 %shard_map.65 = bf16[16,64,512]{2,1,0:T(8,128)(2,1)S(1)} custom-call(s32[1]{0:T(128)} %copy.7.length_ref, bf16[16,64,512]{2,1,0:T(8,128)(2,1)S(1)} %all-to-all-done.rows_ref, bf16[2,512,1024]{2,1,0:T(8,128)(2,1)S(1)} %copy-done, bf16[2,2560,512]{2,1,0:T(8,128)(2,1)} %pad_maximum_fusion.tables_hbm), custom_call_target="tpu_custom_call" | custom-call | flops 7516192768 | bytes 9437184 | tf_op jit(solution)/shard_map/pallas_call | solution.py:137
  43.4 21.2 %all_to_all.10 = bf16[16,64,512]{2,1,0:T(8,128)(2,1)S(1)} all-to-all(bf16[16,64,512]{2,1,0:T(8,128)(2,1)S(1)} %shard_map.65), channel_id=1, replica_groups=mesh['user'=16,'cand'=8] {'user'}, dimensions={0} | all-to-all | bytes 2097152 | tf_op jit(solution)/shard_map/all_to_all | solution.py:208
  64.6 0.0 copy-done.3
  64.6 0.0 copy-done.2
  64.6 1.7 %fusion.1 = f32[512,512]{1,0:T(8,128)} fusion(bf16[1024,512]{1,0:T(8,128)(2,1)S(1)} %bitcast.10, s32[512]{0:T(512)S(1)} %bitcast.12, bf16[512,512]{1,0:T(8,128)(2,1)S(1)} %copy-done.2), kind=kOutput, calls=%fused_computation.4 | convolution fusion | flops 537919488 | bytes 2623488 | tf_op jit(solution)/shard_map/dot_general | solution.py:209
  (1 shorter events, 0.0 us)
Async XLA Ops:
  2.9 25.6 %all-to-all-start = ((bf16[16,64,512]{2,1,0:T(8,128)(2,1)}), bf16[16,64,512]{2,1,0:T(8,128)(2,1)S(1)}, u32[]{:S(2)}, u32[]{:S(2)}) async-start(bf16[16,64,512]{2,1,0:T(8,128)(2,1)} %bitcast.9), calls=%async_computation | async-start | bytes 2097152 | tf_op jit(solution)/shard_map/all_to_all | solution.py:205
  11.6 2.7 %copy-start.1 = (bf16[2,512,512]{2,1,0:T(8,128)(2,1)S(1)}, bf16[2,512,512]{2,1,0:T(8,128)(2,1)}, u32[]{:S(2)}) copy-start(bf16[2,512,512]{2,1,0:T(8,128)(2,1)} %param.11) | copy-start | bytes 3145732
  14.3 14.2 %copy-start = (bf16[2,512,1024]{2,1,0:T(8,128)(2,1)S(1)}, bf16[2,512,1024]{2,1,0:T(8,128)(2,1)}, u32[]{:S(2)}) copy-start(bf16[2,512,1024]{2,1,0:T(8,128)(2,1)} %w_in_ref.1) | copy-start | bytes 6291460
  23.6 41.0 %copy-start.3 = (s32[1,512]{1,0:T(1,128)S(1)}, s32[1,512]{1,0:T(1,128)}, u32[]{:S(2)}) copy-start(s32[1,512]{1,0:T(1,128)} %get-tuple-element.7) | copy-start | bytes 6148
  28.5 36.1 %copy-start.2 = (bf16[512,512]{1,0:T(8,128)(2,1)S(1)}, bf16[512,512]{1,0:T(8,128)(2,1)}, u32[]{:S(2)}) copy-start(bf16[512,512]{1,0:T(8,128)(2,1)} %emb_ref.1) | copy-start | bytes 1572868

commit v16 on v9

--- a/solution.py
+++ b/solution.py
@@ -38,13 +38,14 @@
 
     @pl.when(step == 0)
     def _():
-        for copy in copies:
-            copy.start()
+        copies[0].start()
 
     def arrive(index):
         @pl.when(step == 0)
         def _():
             copies[index].wait()
+            if index + 1 < len(copies):
+                copies[index + 1].start()
 
     busy = jnp.max(jnp.abs(rows_ref[...].astype(jnp.float32))) > 0
 

time: 66.8 us -> 66.8 us (level)
  no operation moved by 1% of the time
where the time goes in v16:
time: 66.8 us; the launch traced here: 66.6 us
  Pallas kernels  19.7 us (29%)
  blocking collectives  19.5 us (29%)
  other arithmetic  12 us (18%)
  starting transfers between devices  7.96 us (12%)
  waiting for transfers between devices  4.92 us (7%)
  matrix products  1.73 us (3%)
  between operations  0.71 us (1%)
    all_to_all x1, blocking collectives, local(): lax.all_to_all(delta, 'user', split_axis=0, concat_axis=0, tiled=True)  19.5 us
    pallas_call x1, Pallas kernels, run_layers(): pl.pallas_call(layers_kernel, grid_spec=grid_spec, out_shape=jax.ShapeDty...  16.8 us
    concatenate x1, other arithmetic, run_layers(): jnp.concatenate([history[:, :, :features], jnp.where(in_history, history[...  9.3 us
    all_to_all x1, starting transfers between devices, local(): lax.all_to_all(outgoing, 'user', split_axis=0, concat_axis=0, tiled=True)  7.96 us
    all_to_all x1, waiting for transfers between devices, local(): lax.all_to_all(outgoing, 'user', split_axis=0, concat_axis=0, tiled=True)  4.92 us
    pallas_call x1, Pallas kernels, pack_rows(): pl.pallas_call(functools.partial(pack_kernel, group_size=group_size, user...  2.92 us
    slice x1, other arithmetic, run_layers(): history[:, :, :features]  2.71 us
    dot_general x1, matrix products, local(): lax.dot_general(placing, returned.reshape(-1, features), (((0,), (0,)), (...  1.73 us
  transfers between devices with their start and end apart: 1, of which 1 were waited for; matrix products, arithmetic and copies ran while one was open for 18% of the time, Pallas kernels for 0%

profile of v16, /device:TPU:0, one launch (start us, length us, event | category | flops | bytes accessed | tf_op | source)
XLA Modules:
  0.0 66.6 jit_solution(4829559036722759743)
XLA Ops:
  0.0 2.9 %shard_map.64 = (bf16[1024,512]{1,0:T(8,128)(2,1)}, s32[1,512]{1,0:T(1,128)}) custom-call(s32[1,512]{1,0:T(1,128)} %bitcast.11, bf16[512,512]{1,0:T(8,128)(2,1)} %emb_ref.1), custom_call_target="tpu_custom_call" | custom-call | flops 545259520 | bytes 1572864 | tf_op jit(solution)/shard_map/pallas_call | solution.py:169
  2.9 8.0 %all-to-all-start = ((bf16[16,64,512]{2,1,0:T(8,128)(2,1)}), bf16[16,64,512]{2,1,0:T(8,128)(2,1)S(1)}, u32[]{:S(2)}, u32[]{:S(2)}) async-start(bf16[16,64,512]{2,1,0:T(8,128)(2,1)} %bitcast.9), calls=%async_computation | async-start | bytes 2097152 | tf_op jit(solution)/shard_map/all_to_all | solution.py:196
  11.6 0.0 copy-start.1
  11.6 2.7 %fusion.3 = (bf16[2,1024,512]{2,1,0:T(8,128)(2,1)S(1)}, bf16[2,1024,512]{2,1,0:T(8,128)(2,1)S(1)}) fusion(bf16[2,1024,1024]{2,1,0:T(8,128)(2,1)} %bitcast.8, pred[1024]{0:T(1024)(128)(4,1)S(1)} %iota_compare_fusion.4), kind=kLoop, calls=%fused_computation.7 | loop fusion | flops 1048576 | bytes 8389632 | tf_op jit(solution)/shard_map/slice | solution.py:103
  14.3 0.0 copy-done.1
  14.3 0.0 copy-start
  14.3 9.3 %pad_maximum_fusion.tables_hbm = bf16[2,2560,512]{2,1,0:T(8,128)(2,1)} fusion(bf16[2,512,512]{2,1,0:T(8,128)(2,1)S(1)} %copy-done.1, bf16[2,1024,512]{2,1,0:T(8,128)(2,1)S(1)} %get-tuple-element.10, bf16[2,1024,512]{2,1,0:T(8,128)(2,1)S(1)} %get-tuple-element.9), kind=kLoop, calls=%fused_computation | loop fusion | flops 15728640 | bytes 10485760 | tf_op jit(solution)/shard_map/concatenate | solution.py:101
  23.6 0.0 copy-start.3
  23.6 4.9 %all-to-all-done.rows_ref = bf16[16,64,512]{2,1,0:T(8,128)(2,1)S(1)} async-done(((bf16[16,64,512]{2,1,0:T(8,128)(2,1)}), bf16[16,64,512]{2,1,0:T(8,128)(2,1)S(1)}, u32[]{:S(2)}, u32[]{:S(2)}) %all-to-all-start) | async-done | bytes 1048608 | tf_op jit(solution)/shard_map/all_to_all | solution.py:196
  28.5 0.0 copy-done
  28.5 0.0 copy-start.2
  28.5 16.8 %shard_map.65 = bf16[16,64,512]{2,1,0:T(8,128)(2,1)S(1)} custom-call(bf16[16,64,512]{2,1,0:T(8,128)(2,1)S(1)} %all-to-all-done.rows_ref, bf16[2,512,1024]{2,1,0:T(8,128)(2,1)S(1)} %copy-done, bf16[2,2560,512]{2,1,0:T(8,128)(2,1)} %pad_maximum_fusion.tables_hbm), custom_call_target="tpu_custom_call" | custom-call | flops 7516192768 | bytes 9437184 | tf_op jit(solution)/shard_map/pallas_call | solution.py:128
  45.3 19.5 %all_to_all.10 = bf16[16,64,512]{2,1,0:T(8,128)(2,1)S(1)} all-to-all(bf16[16,64,512]{2,1,0:T(8,128)(2,1)S(1)} %shard_map.65), channel_id=1, replica_groups=mesh['user'=16,'cand'=8] {'user'}, dimensions={0} | all-to-all | bytes 2097152 | tf_op jit(solution)/shard_map/all_to_all | solution.py:199
  64.8 0.0 copy-done.3
  64.8 0.0 copy-done.2
  64.8 1.7 %fusion.1 = f32[512,512]{1,0:T(8,128)} fusion(bf16[1024,512]{1,0:T(8,128)(2,1)S(1)} %bitcast.10, s32[512]{0:T(512)S(1)} %bitcast.12, bf16[512,512]{1,0:T(8,128)(2,1)S(1)} %copy-done.2), kind=kOutput, calls=%fused_computation.4 | convolution fusion | flops 537919488 | bytes 2623488 | tf_op jit(solution)/shard_map/dot_general | solution.py:200
  (1 shorter events, 0.0 us)
Async XLA Ops:
  2.9 25.6 %all-to-all-start = ((bf16[16,64,512]{2,1,0:T(8,128)(2,1)}), bf16[16,64,512]{2,1,0:T(8,128)(2,1)S(1)}, u32[]{:S(2)}, u32[]{:S(2)}) async-start(bf16[16,64,512]{2,1,0:T(8,128)(2,1)} %bitcast.9), calls=%async_computation | async-start | bytes 2097152 | tf_op jit(solution)/shard_map/all_to_all | solution.py:196
  11.6 2.7 %copy-start.1 = (bf16[2,512,512]{2,1,0:T(8,128)(2,1)S(1)}, bf16[2,512,512]{2,1,0:T(8,128)(2,1)}, u32[]{:S(2)}) copy-start(bf16[2,512,512]{2,1,0:T(8,128)(2,1)} %param.11) | copy-start | bytes 3145732
  14.3 14.2 %copy-start = (bf16[2,512,1024]{2,1,0:T(8,128)(2,1)S(1)}, bf16[2,512,1024]{2,1,0:T(8,128)(2,1)}, u32[]{:S(2)}) copy-start(bf16[2,512,1024]{2,1,0:T(8,128)(2,1)} %w_in_ref.1) | copy-start | bytes 6291460
  23.6 41.2 %copy-start.3 = (s32[1,512]{1,0:T(1,128)S(1)}, s32[1,512]{1,0:T(1,128)}, u32[]{:S(2)}) copy-start(s32[1,512]{1,0:T(1,128)} %get-tuple-element.7) | copy-start | bytes 6148
  28.5 36.3 %copy-start.2 = (bf16[512,512]{1,0:T(8,128)(2,1)S(1)}, bf16[512,512]{1,0:T(8,128)(2,1)}, u32[]{:S(2)}) copy-start(bf16[512,512]{1,0:T(8,128)(2,1)} %emb_ref.1) | copy-start | bytes 1572868

commit v17 on v9

--- a/solution.py
+++ b/solution.py
@@ -139,9 +139,12 @@
     )(buckets, w_in, tables)
 
 
-def pack_kernel(route_ref, emb_ref, packed_ref, position_ref, *, group_size, user_count):
+def pack_kernel(
+    route_ref, emb_ref, packed_hbm, position_ref, staged_ref, copy_sems, *, group_size, user_count
+):
     cand_rows = emb_ref.shape[0]
-    capacity = packed_ref.shape[0] // user_count
+    parts, part_slots = staged_ref.shape[0], staged_ref.shape[1]
+    capacity = parts * part_slots // user_count
     owner = route_ref[...] // group_size
     member = (lax.broadcasted_iota(jnp.int32, (user_count, cand_rows), 0) == owner).astype(
         jnp.float32
@@ -154,17 +157,30 @@
     ranking = jnp.sum(member * before, axis=0, keepdims=True).astype(jnp.int32)
     position = owner * capacity + ranking
     position_ref[...] = position
-    placing = (
-        lax.broadcasted_iota(jnp.int32, (packed_ref.shape[0], cand_rows), 0) == position
-    ).astype(jnp.bfloat16)
-    packed_ref[...] = jnp.dot(
-        placing, emb_ref[...], preferred_element_type=jnp.float32
-    ).astype(packed_ref.dtype)
+    copies = []
+    for part in range(parts):
+        placing = (
+            lax.broadcasted_iota(jnp.int32, (part_slots, cand_rows), 0) + part * part_slots
+            == position
+        ).astype(jnp.bfloat16)
+        staged_ref[part] = jnp.dot(
+            placing, emb_ref[...], preferred_element_type=jnp.float32
+        ).astype(staged_ref.dtype)
+        copy = pltpu.make_async_copy(
+            staged_ref.at[part],
+            packed_hbm.at[pl.ds(part * part_slots, part_slots)],
+            copy_sems.at[part],
+        )
+        copy.start()
+        copies.append(copy)
+    for copy in copies:
+        copy.wait()
 
 
 def pack_rows(cand_emb, cand_route, user_count, group_size):
     cand_rows, features = cand_emb.shape
     slots = 2 * cand_rows
+    parts = 2
     return pl.pallas_call(
         functools.partial(pack_kernel, group_size=group_size, user_count=user_count),
         out_shape=(
@@ -172,7 +188,11 @@
             jax.ShapeDtypeStruct((1, cand_rows), jnp.int32),
         ),
         in_specs=[pl.BlockSpec(memory_space=pltpu.VMEM)] * 2,
-        out_specs=(pl.BlockSpec(memory_space=pltpu.VMEM),) * 2,
+        out_specs=(pl.BlockSpec(memory_space=pl.ANY), pl.BlockSpec(memory_space=pltpu.VMEM)),
+        scratch_shapes=[
+            pltpu.VMEM((parts, slots // parts, features), jnp.bfloat16),
+            pltpu.SemaphoreType.DMA((parts,)),
+        ],
         cost_estimate=pl.CostEstimate(
             flops=2 * slots * cand_rows * features + 2 * user_count * cand_rows * cand_rows,
             transcendentals=0,

time: 66.8 us -> 67.3 us (level)
  no operation moved by 1% of the time
where the time goes in v17:
time: 67.3 us; the launch traced here: 67 us
  Pallas kernels  20.2 us (30%)
  blocking collectives  19.5 us (29%)
  other arithmetic  12 us (18%)
  starting transfers between devices  7.98 us (12%)
  waiting for transfers between devices  4.93 us (7%)
  matrix products  1.73 us (3%)
  between operations  0.71 us (1%)
    all_to_all x1, blocking collectives, local(): lax.all_to_all(delta, 'user', split_axis=0, concat_axis=0, tiled=True)  19.5 us
    pallas_call x1, Pallas kernels, run_layers(): pl.pallas_call(layers_kernel, grid_spec=grid_spec, out_shape=jax.ShapeDty...  16.8 us
    concatenate x1, other arithmetic, run_layers(): jnp.concatenate([history[:, :, :features], jnp.where(in_history, history[...  9.3 us
    all_to_all x1, starting transfers between devices, local(): lax.all_to_all(outgoing, 'user', split_axis=0, concat_axis=0, tiled=True)  7.98 us
    all_to_all x1, waiting for transfers between devices, local(): lax.all_to_all(outgoing, 'user', split_axis=0, concat_axis=0, tiled=True)  4.93 us
    pallas_call x1, Pallas kernels, pack_rows(): pl.pallas_call(functools.partial(pack_kernel, group_size=group_size, user...  3.37 us
    slice x1, other arithmetic, run_layers(): history[:, :, :features]  2.71 us
    dot_general x1, matrix products, local(): lax.dot_general(placing, returned.reshape(-1, features), (((0,), (0,)), (...  1.73 us
  transfers between devices with their start and end apart: 1, of which 1 were waited for; matrix products, arithmetic and copies ran while one was open for 18% of the time, Pallas kernels for 0%

profile of v17, /device:TPU:0, one launch (start us, length us, event | category | flops | bytes accessed | tf_op | source)
XLA Modules:
  0.0 67.0 jit_solution(3012944666768059526)
XLA Ops:
  0.0 3.4 %shard_map.64 = (bf16[1024,512]{1,0:T(8,128)(2,1)}, s32[1,512]{1,0:T(1,128)}) custom-call(s32[1,512]{1,0:T(1,128)} %bitcast.11, bf16[512,512]{1,0:T(8,128)(2,1)} %emb_ref.1), custom_call_target="tpu_custom_call" | custom-call | flops 545259520 | bytes 1572864 | tf_op jit(solution)/shard_map/pallas_call | solution.py:184
  3.4 8.0 %all-to-all-start = ((bf16[16,64,512]{2,1,0:T(8,128)(2,1)}), bf16[16,64,512]{2,1,0:T(8,128)(2,1)S(1)}, u32[]{:S(2)}, u32[]{:S(2)}) async-start(bf16[16,64,512]{2,1,0:T(8,128)(2,1)} %bitcast.9), calls=%async_computation | async-start | bytes 2097152 | tf_op jit(solution)/shard_map/all_to_all | solution.py:215
  12.0 0.0 copy-start.1
  12.0 2.7 %fusion.3 = (bf16[2,1024,512]{2,1,0:T(8,128)(2,1)S(1)}, bf16[2,1024,512]{2,1,0:T(8,128)(2,1)S(1)}) fusion(bf16[2,1024,1024]{2,1,0:T(8,128)(2,1)} %bitcast.8, pred[1024]{0:T(1024)(128)(4,1)S(1)} %iota_compare_fusion.4), kind=kLoop, calls=%fused_computation.7 | loop fusion | flops 1048576 | bytes 8389632 | tf_op jit(solution)/shard_map/slice | solution.py:102
  14.8 0.0 copy-done.1
  14.8 0.0 copy-start
  14.8 9.3 %pad_maximum_fusion.tables_hbm = bf16[2,2560,512]{2,1,0:T(8,128)(2,1)} fusion(bf16[2,512,512]{2,1,0:T(8,128)(2,1)S(1)} %copy-done.1, bf16[2,1024,512]{2,1,0:T(8,128)(2,1)S(1)} %get-tuple-element.10, bf16[2,1024,512]{2,1,0:T(8,128)(2,1)S(1)} %get-tuple-element.9), kind=kLoop, calls=%fused_computation | loop fusion | flops 15728640 | bytes 10485760 | tf_op jit(solution)/shard_map/concatenate | solution.py:100
  24.1 0.0 copy-start.3
  24.1 4.9 %all-to-all-done.rows_ref = bf16[16,64,512]{2,1,0:T(8,128)(2,1)S(1)} async-done(((bf16[16,64,512]{2,1,0:T(8,128)(2,1)}), bf16[16,64,512]{2,1,0:T(8,128)(2,1)S(1)}, u32[]{:S(2)}, u32[]{:S(2)}) %all-to-all-start) | async-done | bytes 1048608 | tf_op jit(solution)/shard_map/all_to_all | solution.py:215
  29.0 0.0 copy-done
  29.0 0.0 copy-start.2
  29.0 16.8 %shard_map.65 = bf16[16,64,512]{2,1,0:T(8,128)(2,1)S(1)} custom-call(bf16[16,64,512]{2,1,0:T(8,128)(2,1)S(1)} %all-to-all-done.rows_ref, bf16[2,512,1024]{2,1,0:T(8,128)(2,1)S(1)} %copy-done, bf16[2,2560,512]{2,1,0:T(8,128)(2,1)} %pad_maximum_fusion.tables_hbm), custom_call_target="tpu_custom_call" | custom-call | flops 7516192768 | bytes 9437184 | tf_op jit(solution)/shard_map/pallas_call | solution.py:127
  45.8 19.5 %all_to_all.10 = bf16[16,64,512]{2,1,0:T(8,128)(2,1)S(1)} all-to-all(bf16[16,64,512]{2,1,0:T(8,128)(2,1)S(1)} %shard_map.65), channel_id=1, replica_groups=mesh['user'=16,'cand'=8] {'user'}, dimensions={0} | all-to-all | bytes 2097152 | tf_op jit(solution)/shard_map/all_to_all | solution.py:218
  65.3 0.0 copy-done.3
  65.3 0.0 copy-done.2
  65.3 1.7 %fusion.1 = f32[512,512]{1,0:T(8,128)} fusion(bf16[1024,512]{1,0:T(8,128)(2,1)S(1)} %bitcast.10, s32[512]{0:T(512)S(1)} %bitcast.12, bf16[512,512]{1,0:T(8,128)(2,1)S(1)} %copy-done.2), kind=kOutput, calls=%fused_computation.4 | convolution fusion | flops 537919488 | bytes 2623488 | tf_op jit(solution)/shard_map/dot_general | solution.py:219
  (1 shorter events, 0.0 us)
Async XLA Ops:
  3.4 25.6 %all-to-all-start = ((bf16[16,64,512]{2,1,0:T(8,128)(2,1)}), bf16[16,64,512]{2,1,0:T(8,128)(2,1)S(1)}, u32[]{:S(2)}, u32[]{:S(2)}) async-start(bf16[16,64,512]{2,1,0:T(8,128)(2,1)} %bitcast.9), calls=%async_computation | async-start | bytes 2097152 | tf_op jit(solution)/shard_map/all_to_all | solution.py:215
  12.0 2.7 %copy-start.1 = (bf16[2,512,512]{2,1,0:T(8,128)(2,1)S(1)}, bf16[2,512,512]{2,1,0:T(8,128)(2,1)}, u32[]{:S(2)}) copy-start(bf16[2,512,512]{2,1,0:T(8,128)(2,1)} %param.11) | copy-start | bytes 3145732
  14.8 14.2 %copy-start = (bf16[2,512,1024]{2,1,0:T(8,128)(2,1)S(1)}, bf16[2,512,1024]{2,1,0:T(8,128)(2,1)}, u32[]{:S(2)}) copy-start(bf16[2,512,1024]{2,1,0:T(8,128)(2,1)} %w_in_ref.1) | copy-start | bytes 6291460
  24.1 41.2 %copy-start.3 = (s32[1,512]{1,0:T(1,128)S(1)}, s32[1,512]{1,0:T(1,128)}, u32[]{:S(2)}) copy-start(s32[1,512]{1,0:T(1,128)} %get-tuple-element.7) | copy-start | bytes 6148
  29.0 36.3 %copy-start.2 = (bf16[512,512]{1,0:T(8,128)(2,1)S(1)}, bf16[512,512]{1,0:T(8,128)(2,1)}, u32[]{:S(2)}) copy-start(bf16[512,512]{1,0:T(8,128)(2,1)} %emb_ref.1) | copy-start | bytes 1572868
